TPU v7x, 1024 devices: a whole 8x8x8 slice. The times are simulated.
1024 devices in a mesh: gx: 16 (over y, core), gy: 64 (over z, x).
Axes of the slice: x: 8, y: 8, z: 8, core: 2. Of those that a mesh axis runs over, the one named last changes fastest.
Arguments:
- positions: float32 [16, 64, 5, 3, 128], P('gx', 'gy'), may hold values from 0 to 80
- polarity: float32 [16, 64, 5, 128], P('gx', 'gy'), may hold values from 0.25 to 1.25
- direct_field: float32 [16, 64, 5, 6, 128], P('gx', 'gy'), may hold values from -30 to 30
- atom_count: int32 [16, 64, 5], P('gx', 'gy'), may hold values from 64 to 128, as said below
- pair_list: int32 [16, 64, 3, 61], P('gx', 'gy'), may hold values from 0 to 4, as said below
- pair_count: int32 [16, 64], P('gx', 'gy'), may hold values from 9 to 61, as said below
Outputs:
- dipoles: float32 [16, 64, 5, 6, 128], P('gx', 'gy')
- residual: float32 [16, 64, 5, 6, 128], P('gx', 'gy')
Inputs may be any that keep to these rules, and one draw needn't show every extreme that they name: `atom_count`: every device has one block with all 128 atoms. `pair_list`: for e < pair_count the entry (b, s, c) has s in 0..4; with s = 0, c is b or b + 1, otherwise c is b - 1, b or b + 1, all blocks within 0..4; no entry appears twice; every device lists all its s = 0 entries; entries from pair_count on are zeros. `pair_count`: some device lists all 61 possible entries.
All inputs are finite; a program needn't handle non-finite values.
Results may differ from a plain program's by a relative error of at most 0.003.
Values sent between devices are 32-bit elements; how exact they have to be, the bound alone decides.
No kernel may reach another device: no remote copies, remote signals or barrier semaphores. Data moves between devices by JAX's collectives and lax.ppermute only.
A program may use at most 32 MiB of HBM per device.

v0:
```python
import jax
import jax.numpy as jnp
from jax import lax
from jax.sharding import PartitionSpec as P

ITERS = 2


thole_factor = 0.39
column_width = 8.0
pair_batch = 8
slot_shift_x = (0.0, 0.0, 1.0, 1.0, 1.0)
slot_shift_y = (0.0, 1.0, -1.0, 0.0, 1.0)


def padded_2(cells, sides, width):
    for axis, dim in sides:
        count = lax.axis_size(axis)
        head = lax.slice_in_dim(cells, 0, width, axis=dim)
        tail = lax.slice_in_dim(cells, cells.shape[dim] - width, cells.shape[dim], axis=dim)
        cells = jnp.concatenate(
            [
                lax.ppermute(tail, axis, [(i, (i + 1) % count) for i in range(count)]),
                cells,
                lax.ppermute(head, axis, [((i + 1) % count, i) for i in range(count)]),
            ],
            axis=dim,
        )
    return cells


def from_behind(value, axis, steps):
    count = lax.axis_size(axis)
    pairs = [(source, (source + steps) % count) for source in range(count)]
    return lax.ppermute(value, axis, pairs)


def tensor_apply(coef_three, coef_five, deltas, moment, axis_sum):
    if axis_sum == 2:
        moments = [moment[:, member, None, :] for member in range(3)]
    else:
        moments = [moment[:, member, :, None] for member in range(3)]
    project = deltas[0] * moments[0] + deltas[1] * moments[1] + deltas[2] * moments[2]
    scaled = coef_five * project
    return jnp.stack(
        [
            jnp.sum(scaled * deltas[member] - coef_three * moments[member], axis=axis_sum)
            for member in range(3)
        ],
        axis=1,
    )


def pair_fields(geom_i, geom_j, dip_i, dip_j, slot_ids, same_block):
    chosen = (slot_ids[:, None] == jnp.arange(5, dtype=jnp.int32)[None, :]).astype(jnp.float32)
    offset_x = column_width * jnp.sum(
        chosen * jnp.array(slot_shift_x, jnp.float32)[None, :], axis=1
    )
    offset_y = column_width * jnp.sum(
        chosen * jnp.array(slot_shift_y, jnp.float32)[None, :], axis=1
    )
    delta_x = geom_j[:, 0, None, :] + offset_x[:, None, None] - geom_i[:, 0, :, None]
    delta_y = geom_j[:, 1, None, :] + offset_y[:, None, None] - geom_i[:, 1, :, None]
    delta_z = geom_j[:, 2, None, :] - geom_i[:, 2, :, None]
    dist_sq = delta_x * delta_x + delta_y * delta_y + delta_z * delta_z
    atom_width = geom_i.shape[2]
    same_atom = jnp.arange(atom_width)[:, None] == jnp.arange(atom_width)[None, :]
    diagonal = same_atom[None, :, :] & same_block[:, None, None]
    dist_sq = jnp.where(diagonal, 1.0, dist_sq)
    inv_dist = lax.rsqrt(dist_sq)
    inv_cube = inv_dist * inv_dist * inv_dist
    root_pol = jnp.sqrt(geom_i[:, 3, :, None] * geom_j[:, 3, None, :])
    damping = thole_factor * dist_sq * jnp.sqrt(dist_sq) / root_pol
    lambda_three = -jnp.expm1(-damping)
    lambda_five = lambda_three - damping * jnp.exp(-damping)
    keep_pair = jnp.where(diagonal, 0.0, 1.0)
    coef_three = keep_pair * lambda_three * inv_cube
    coef_five = keep_pair * 3.0 * lambda_five * inv_cube * inv_dist * inv_dist
    deltas = (delta_x, delta_y, delta_z)
    forward = jnp.concatenate(
        [
            tensor_apply(coef_three, coef_five, deltas, dip_j[:, 0:3], 2),
            tensor_apply(coef_three, coef_five, deltas, dip_j[:, 3:6], 2),
        ],
        axis=1,
    )
    backward = jnp.concatenate(
        [
            tensor_apply(coef_three, coef_five, deltas, dip_i[:, 0:3], 1),
            tensor_apply(coef_three, coef_five, deltas, dip_i[:, 3:6], 1),
        ],
        axis=1,
    )
    return (forward, backward)


def accumulate(geom_stack, dip_stack, entries, pair_total, live_turns, capacity_turns):
    blocks = geom_stack.shape[0] // 5
    atom_width = geom_stack.shape[2]
    targets = jnp.arange(5 * blocks, dtype=jnp.int32)
    padded = jnp.pad(entries, ((0, 0), (0, capacity_turns * pair_batch - entries.shape[1])))

    def one_turn(turn_index, accumulated):
        first_row = (turn_index * pair_batch).astype(jnp.int32)
        group_rows = lax.dynamic_slice_in_dim(padded, first_row, pair_batch, 1)
        own_block = group_rows[0]
        slot_ids = group_rows[1]
        other_block = group_rows[2]
        source = slot_ids * blocks + other_block
        live_rows = (first_row + jnp.arange(pair_batch, dtype=jnp.int32) < pair_total).astype(
            jnp.float32
        )
        same_block = (slot_ids == 0) & (own_block == other_block)
        forward, backward = pair_fields(
            jnp.take(geom_stack, own_block, axis=0),
            jnp.take(geom_stack, source, axis=0),
            jnp.take(dip_stack, own_block, axis=0),
            jnp.take(dip_stack, source, axis=0),
            slot_ids,
            same_block,
        )
        to_own = (own_block[:, None] == targets[None, :]).astype(jnp.float32) * live_rows[:, None]
        twoway = live_rows * (1.0 - same_block.astype(jnp.float32))
        to_other = (source[:, None] == targets[None, :]).astype(jnp.float32) * twoway[:, None]
        accumulated = accumulated + jnp.einsum(
            "gt,gca->tca", to_own, forward, precision=lax.Precision.HIGHEST
        )
        return accumulated + jnp.einsum(
            "gt,gca->tca", to_other, backward, precision=lax.Precision.HIGHEST
        )

    return lax.fori_loop(
        0, live_turns, one_turn, jnp.zeros((5 * blocks, 6, atom_width), jnp.float32)
    )


def neighbours(block_data):
    column = padded_2(block_data[None, None], (("gy", 1),), 1)
    across = from_behind(column, "gx", -1)
    return jnp.concatenate([block_data[None], column[0, 2:3], across[0]], axis=0)


def send_back(partials):
    received = from_behind(partials[None, 1:4], "gx", 1)
    paired = jnp.stack([received[0, 0], received[0, 2] + partials[0]], axis=0)[None]
    column = padded_2(paired, (("gy", 1),), 1)
    return column[0, 0] + column[0, 3] + received[0, 1]


def set_sums(first_vec, second_vec):
    product = (first_vec * second_vec).reshape(first_vec.shape[0], 2, 3, first_vec.shape[2])
    return jnp.sum(product, axis=(0, 2, 3))


def spread_sets(values):
    return jnp.repeat(values, 3)[None, :, None]


def global_sums(local_values):
    return lax.psum(local_values, ("gx", "gy"))


def per_device(positions, polarity, direct_field, atom_count, pair_list, pair_count):
    blocks = positions.shape[2]
    atom_width = positions.shape[4]
    atom_mask = (
        jnp.arange(atom_width, dtype=jnp.int32)[None, :] < atom_count[0, 0][:, None]
    ).astype(jnp.float32)
    pol_wide = polarity[0, 0][:, None, :]
    geometry = jnp.concatenate([positions[0, 0], pol_wide], axis=1)
    entries = pair_list[0, 0]
    pair_total = pair_count[0, 0]
    capacity_turns = -(-entries.shape[1] // pair_batch)
    live_turns = (pair_total + pair_batch - 1) // pair_batch
    residual = direct_field[0, 0] * atom_mask[:, None, :]
    dipoles = jnp.zeros_like(residual)
    geom_stack = None
    search = pol_wide * residual
    rho_now = global_sums(set_sums(residual, search))
    for iteration in range(ITERS):
        operate_geom_stack = geom_stack
        if operate_geom_stack is None:
            stacked = neighbours(jnp.concatenate([geometry, search], axis=1))
            operate_geom_stack = stacked[:, :, 0:4].reshape(5 * blocks, 4, atom_width)
            dip_stack = stacked[:, :, 4:10].reshape(5 * blocks, 6, atom_width)
        else:
            dip_stack = neighbours(search).reshape(5 * blocks, 6, atom_width)
        accumulated = accumulate(
            operate_geom_stack, dip_stack, entries, pair_total, live_turns, capacity_turns
        )
        accumulated = accumulated.reshape(5, blocks, 6, atom_width)
        mutual = (accumulated[0] + send_back(accumulated[1:5])) * atom_mask[:, None, :]
        image_vec = search / pol_wide - mutual
        geom_stack = operate_geom_stack
        step_size = spread_sets(rho_now / global_sums(set_sums(search, image_vec)))
        dipoles = dipoles + step_size * search
        residual = residual - step_size * image_vec
        if iteration + 1 < ITERS:
            precond = pol_wide * residual
            rho_next = global_sums(set_sums(residual, precond))
            search = precond + spread_sets(rho_next / rho_now) * search
            rho_now = rho_next
    return (dipoles[None, None], residual[None, None])


def solution(mesh):
    in_specs = (
        P("gx", "gy", None, None, None),
        P("gx", "gy", None, None),
        P("gx", "gy", None, None, None),
        P("gx", "gy", None),
        P("gx", "gy", None, None),
        P("gx", "gy"),
    )
    out_specs = (P("gx", "gy", None, None, None), P("gx", "gy", None, None, None))
    return jax.shard_map(
        per_device, mesh=mesh, in_specs=in_specs, out_specs=out_specs, check_vma=False
    )
```

profile of v0, /device:TPU:1, one launch (start us, length us, event | category | flops | bytes accessed | tf_op | source)
XLA Modules:
  0.0 571.1 jit_solution(9359612414683311918)
XLA Ops:
  0.6 0.7 copy.81
  1.3 0.7 fusion.132
  2.1 0.7 copy-done.3
  2.8 20.2 %collective-permute-start = (f32[1,1,5,10,128]{4,3,2,1,0:T(8,128)S(1)}, f32[1,1,5,10,128]{4,3,2,1,0:T(8,128)S(1)}, u32[]{:S(2)}, u32[]{:S(2)}) collective-permute-start(f32[1,1,5,10,128]{4,3,2,1,0:T(8,128)S(1)} %get-tuple-element.422), channel_id=1, source_target_pairs={{1,0},{2,1},{3,2},{4,3},{5,4},{6,5},{7,6},{8,7},{9,8},{10,9},{11,1... | collective-permute-start | bytes 76808 | tf_op jit(solution)/shard_map/ppermute | solution.py:25
  23.0 1.9 collective-permute-start.1
  24.9 6.1 %collective-permute-done.1 = f32[1,1,5,10,128]{4,3,2,1,0:T(8,128)S(1)} collective-permute-done((f32[1,1,5,10,128]{4,3,2,1,0:T(8,128)S(1)}, f32[1,1,5,10,128]{4,3,2,1,0:T(8,128)S(1)}, u32[]{:S(2)}, u32[]{:S(2)}) %collective-permute-start.1) | collective-permute-done | bytes 25632 | tf_op jit(solution)/shard_map/ppermute | solution.py:23
  31.1 2.1 collective-permute-start.2
  33.9 0.7 copy-done.5
  34.5 2.5 collective-permute-done.2
  37.8 58.2 %while.26 = (s32[]{:T(128)}, f32[25,6,128]{2,0,1:T(8,128)S(1)}, s32[]{:T(128)}, s32[3,64]{1,0:T(4,128)S(1)}, s32[]{:T(128)}, /*index=5*/f32[25,4,128]{2,1,0:T(4,...) while((s32[]{:T(128)}, f32[25,6,128]{2,0,1:T(8,128)S(1)}, ...), condition=%wide.region_18.21_spmd.clone.clone.clone, body=%wide.region_3.20_spmd.sunk.clone.clone.clone.sunk | while | flops 20531916 | bytes 1168975 | solution.py:132
  40.7 0.7 compare_select_fusion.13
  41.4 2.7 fusion.173
  44.2 1.8 fusion.171
  50.4 0.7 compare_select_fusion.13
  51.1 2.7 fusion.173
  53.9 1.8 fusion.171
  55.8 0.7 compare_convert_fusion.4
  60.1 0.7 compare_select_fusion.13
  60.8 2.7 fusion.173
  63.6 1.8 fusion.171
  69.8 0.7 compare_select_fusion.13
  70.5 2.7 fusion.173
  73.3 1.8 fusion.171
  79.5 0.7 compare_select_fusion.13
  80.2 2.7 fusion.173
  83.0 1.8 fusion.171
  89.2 0.7 compare_select_fusion.13
  89.9 2.7 fusion.173
  92.8 1.8 fusion.171
  96.1 1.3 collective-permute-done.3
  97.4 1.9 collective-permute-start.4
  99.3 6.7 %collective-permute-start.5 = (f32[1,1,5,6,128]{4,3,2,1,0:T(8,128)S(1)}, f32[1,1,5,6,128]{4,3,2,1,0:T(8,128)S(1)}, u32[]{:S(2)}, u32[]{:S(2)}) collective-permute-start(f32[1,1,5,6,128]{4,3,2,1,0:T(8,128)S(1)} %get-tuple-element.419), channel_id=1, source_target_pairs={{1,0},{2,1},{3,2},{4,3},{5,4},{6,5},{7,6},{8,7},{9,8},{10,9},{11,1... | collective-permute-start | bytes 46088 | tf_op jit(solution)/shard_map/ppermute | solution.py:25
  106.0 6.9 %collective-permute-done.5 = f32[1,1,5,6,128]{4,3,2,1,0:T(8,128)S(1)} collective-permute-done((f32[1,1,5,6,128]{4,3,2,1,0:T(8,128)S(1)}, f32[1,1,5,6,128]{4,3,2,1,0:T(8,128)S(1)}, u32[]{:S(2)}, u32[]{:S(2)}) %collective-permute-start.5) | collective-permute-done | bytes 15392 | tf_op jit(solution)/shard_map/ppermute | solution.py:25
  113.5 127.3 %all-reduce.1 = (f32[2]{0:T(128)S(1)}, f32[2]{0:T(128)S(1)}) all-reduce(f32[2]{0:T(128)S(1)} %reduce_sum.318, f32[2]{0:T(128)S(1)} %reduce_sum.321), channel_id=1, replica_groups=mesh['gx'=16,'gy'=64] {'gx','gy'}, use_global_device_ids=true, to_apply=%region_2.3 | all-reduce | flops 4 | bytes 32 | tf_op jit(solution)/shard_map/psum | solution.py:160
  241.4 109.5 %psum.30 = f32[2]{0:T(128)S(1)} all-reduce(f32[2]{0:T(128)S(1)} %reduce_sum.324), channel_id=1, replica_groups=mesh['gx'=16,'gy'=64] {'gx','gy'}, use_global_device_ids=true, to_apply=%region_24.27 | all-reduce | flops 2 | bytes 16 | tf_op jit(solution)/shard_map/psum | solution.py:160
  351.2 4.2 collective-permute-start.6
  355.4 1.9 collective-permute-start.7
  357.3 5.9 %collective-permute-done.7 = f32[1,1,5,6,128]{4,3,2,1,0:T(8,128)S(1)} collective-permute-done((f32[1,1,5,6,128]{4,3,2,1,0:T(8,128)S(1)}, f32[1,1,5,6,128]{4,3,2,1,0:T(8,128)S(1)}, u32[]{:S(2)}, u32[]{:S(2)}) %collective-permute-start.7) | collective-permute-done | bytes 15392 | tf_op jit(solution)/shard_map/ppermute | solution.py:23
  363.2 2.1 collective-permute-start.8
  365.4 3.1 collective-permute-done.8
  368.6 58.4 %while.27 = (s32[]{:T(128)}, f32[25,6,128]{2,0,1:T(8,128)S(1)}, s32[]{:T(128)}, s32[3,64]{1,0:T(4,128)S(1)}, s32[]{:T(128)}, /*index=5*/f32[25,4,128]{2,1,0:T(4,...) while((s32[]{:T(128)}, f32[25,6,128]{2,0,1:T(8,128)S(1)}, ...), condition=%wide.region_40.43_spmd.clone.clone.clone, body=%wide.region_25.42_spmd.sunk.clone.clone.clone.sunk | while | flops 20531916 | bytes 1168975 | solution.py:132
  371.6 0.7 compare_select_fusion.15
  372.3 2.8 fusion.182
  375.1 1.8 fusion.180
  381.3 0.7 compare_select_fusion.15
  382.0 2.8 fusion.182
  384.8 1.8 fusion.180
  391.0 0.7 compare_select_fusion.15
  391.7 2.8 fusion.182
  394.5 1.8 fusion.180
  400.8 0.7 compare_select_fusion.15
  401.4 2.8 fusion.182
  404.3 1.8 fusion.180
  410.5 0.7 compare_select_fusion.15
  411.2 2.8 fusion.182
  414.0 1.8 fusion.180
  420.2 0.7 compare_select_fusion.15
  420.9 2.8 fusion.182
  423.7 1.8 fusion.180
  427.1 1.3 collective-permute-done.9
  428.4 1.9 collective-permute-start.10
  430.3 6.7 %collective-permute-start.11 = (f32[1,1,5,6,128]{4,3,2,1,0:T(8,128)S(1)}, f32[1,1,5,6,128]{4,3,2,1,0:T(8,128)S(1)}, u32[]{:S(2)}, u32[]{:S(2)}) collective-permute-start(f32[1,1,5,6,128]{4,3,2,1,0:T(8,128)S(1)} %get-tuple-element.417), channel_id=1, source_target_pairs={{1,0},{2,1},{3,2},{4,3},{5,4},{6,5},{7,6},{8,7},{9,8},{10,9},{11,1... | collective-permute-start | bytes 46088 | tf_op jit(solution)/shard_map/ppermute | solution.py:25
  437.0 11.6 %collective-permute-done.11 = f32[1,1,5,6,128]{4,3,2,1,0:T(8,128)S(1)} collective-permute-done((f32[1,1,5,6,128]{4,3,2,1,0:T(8,128)S(1)}, f32[1,1,5,6,128]{4,3,2,1,0:T(8,128)S(1)}, u32[]{:S(2)}, u32[]{:S(2)}) %collective-permute-start.11) | collective-permute-done | bytes 15392 | tf_op jit(solution)/shard_map/ppermute | solution.py:25
  448.9 120.7 %psum.31 = f32[2]{0:T(128)S(1)} all-reduce(f32[2]{0:T(128)S(1)} %reduce_sum.327), channel_id=1, replica_groups=mesh['gx'=16,'gy'=64] {'gx','gy'}, use_global_device_ids=true, to_apply=%region_43.46 | all-reduce | flops 2 | bytes 16 | tf_op jit(solution)/shard_map/psum | solution.py:160
  (472 shorter events, 55.0 us)
Async XLA Ops:
  0.6 1.4 copy-start.4
  0.6 1.4 copy-start
  2.1 0.7 copy-start.3
  2.8 22.1 %collective-permute-start = (f32[1,1,5,10,128]{4,3,2,1,0:T(8,128)S(1)}, f32[1,1,5,10,128]{4,3,2,1,0:T(8,128)S(1)}, u32[]{:S(2)}, u32[]{:S(2)}) collective-permute-start(f32[1,1,5,10,128]{4,3,2,1,0:T(8,128)S(1)} %get-tuple-element.422), channel_id=1, source_target_pairs={{1,0},{2,1},{3,2},{4,3},{5,4},{6,5},{7,6},{8,7},{9,8},{10,9},{11,1... | collective-permute-start | bytes 76808 | tf_op jit(solution)/shard_map/ppermute | solution.py:25
  23.0 8.1 %collective-permute-start.1 = (f32[1,1,5,10,128]{4,3,2,1,0:T(8,128)S(1)}, f32[1,1,5,10,128]{4,3,2,1,0:T(8,128)S(1)}, u32[]{:S(2)}, u32[]{:S(2)}) collective-permute-start(f32[1,1,5,10,128]{4,3,2,1,0:T(8,128)S(1)} %get-tuple-element.422), channel_id=1, source_target_pairs={{0,1},{1,2},{2,3},{3,4},{4,5},{5,6},{6,7},{7,8},{8,9},{9,10},{10,1... | collective-permute-start | bytes 76808 | tf_op jit(solution)/shard_map/ppermute | solution.py:23
  31.1 6.0 %collective-permute-start.2 = (f32[1,3,5,10,128]{4,3,2,1,0:T(8,128)S(1)}, f32[1,3,5,10,128]{4,3,2,1,0:T(8,128)S(1)}, u32[]{:S(2)}, u32[]{:S(2)}) collective-permute-start(f32[1,3,5,10,128]{4,3,2,1,0:T(8,128)S(1)} %pad_maximum_fusion), channel_id=1, source_target_pairs={{0,960},{64,0},{128,64},{192,128},{256,192},{320,256},{384,320},{4... | collective-permute-start | bytes 230408 | tf_op jit(solution)/shard_map/ppermute | solution.py:35
  33.8 0.7 copy-start.5
  37.1 0.7 copy-start.1
  37.1 0.7 copy-start.2
  96.1 1.3 collective-permute-start.3
  97.4 8.6 %collective-permute-start.4 = (f32[1,1,5,6,128]{4,3,2,1,0:T(8,128)S(1)}, f32[1,1,5,6,128]{4,3,2,1,0:T(8,128)S(1)}, u32[]{:S(2)}, u32[]{:S(2)}) collective-permute-start(f32[1,1,5,6,128]{4,3,2,1,0:T(8,128)S(1)} %get-tuple-element.420), channel_id=1, source_target_pairs={{0,1},{1,2},{2,3},{3,4},{4,5},{5,6},{6,7},{7,8},{8,9},{9,10},{10,1... | collective-permute-start | bytes 46088 | tf_op jit(solution)/shard_map/ppermute | solution.py:23
  99.3 13.6 %collective-permute-start.5 = (f32[1,1,5,6,128]{4,3,2,1,0:T(8,128)S(1)}, f32[1,1,5,6,128]{4,3,2,1,0:T(8,128)S(1)}, u32[]{:S(2)}, u32[]{:S(2)}) collective-permute-start(f32[1,1,5,6,128]{4,3,2,1,0:T(8,128)S(1)} %get-tuple-element.419), channel_id=1, source_target_pairs={{1,0},{2,1},{3,2},{4,3},{5,4},{6,5},{7,6},{8,7},{9,8},{10,9},{11,1... | collective-permute-start | bytes 46088 | tf_op jit(solution)/shard_map/ppermute | solution.py:25
  351.2 6.2 %collective-permute-start.6 = (f32[1,1,5,6,128]{4,3,2,1,0:T(8,128)S(1)}, f32[1,1,5,6,128]{4,3,2,1,0:T(8,128)S(1)}, u32[]{:S(2)}, u32[]{:S(2)}) collective-permute-start(f32[1,1,5,6,128]{4,3,2,1,0:T(8,128)S(1)} %multiply_add_fusion), channel_id=1, source_target_pairs={{1,0},{2,1},{3,2},{4,3},{5,4},{6,5},{7,6},{8,7},{9,8},{10,9},{11,1... | collective-permute-start | bytes 46088 | tf_op jit(solution)/shard_map/ppermute | solution.py:25
  355.4 7.8 %collective-permute-start.7 = (f32[1,1,5,6,128]{4,3,2,1,0:T(8,128)S(1)}, f32[1,1,5,6,128]{4,3,2,1,0:T(8,128)S(1)}, u32[]{:S(2)}, u32[]{:S(2)}) collective-permute-start(f32[1,1,5,6,128]{4,3,2,1,0:T(8,128)S(1)} %multiply_add_fusion), channel_id=1, source_target_pairs={{0,1},{1,2},{2,3},{3,4},{4,5},{5,6},{6,7},{7,8},{8,9},{9,10},{10,1... | collective-permute-start | bytes 46088 | tf_op jit(solution)/shard_map/ppermute | solution.py:23
  363.2 5.3 collective-permute-start.8
  427.0 1.3 collective-permute-start.9
  428.4 8.6 %collective-permute-start.10 = (f32[1,1,5,6,128]{4,3,2,1,0:T(8,128)S(1)}, f32[1,1,5,6,128]{4,3,2,1,0:T(8,128)S(1)}, u32[]{:S(2)}, u32[]{:S(2)}) collective-permute-start(f32[1,1,5,6,128]{4,3,2,1,0:T(8,128)S(1)} %get-tuple-element.418), channel_id=1, source_target_pairs={{0,1},{1,2},{2,3},{3,4},{4,5},{5,6},{6,7},{7,8},{8,9},{9,10},{10,1... | collective-permute-start | bytes 46088 | tf_op jit(solution)/shard_map/ppermute | solution.py:23
  430.3 18.3 %collective-permute-start.11 = (f32[1,1,5,6,128]{4,3,2,1,0:T(8,128)S(1)}, f32[1,1,5,6,128]{4,3,2,1,0:T(8,128)S(1)}, u32[]{:S(2)}, u32[]{:S(2)}) collective-permute-start(f32[1,1,5,6,128]{4,3,2,1,0:T(8,128)S(1)} %get-tuple-element.417), channel_id=1, source_target_pairs={{1,0},{2,1},{3,2},{4,3},{5,4},{6,5},{7,6},{8,7},{9,8},{10,9},{11,1... | collective-permute-start | bytes 46088 | tf_op jit(solution)/shard_map/ppermute | solution.py:25
where the time goes:
time: 572 us; the launch traced here: 571 us
  blocking collectives  358 us (63%)
  other arithmetic  77.7 us (14%)
  starting transfers between devices  49.7 us (9%)
  waiting for transfers between devices  38.8 us (7%)
  local copies, waits for them, and re-layouts  34.1 us (6%)
  matrix products  8.56 us (1%)
    psum x3, blocking collectives, global_sums(): return lax.psum(local_values, ('gx', 'gy'))  358 us
    reduce_sum x24, other arithmetic, tensor_apply(): jnp.sum(scaled * deltas[member] - coef_three * moments[member], axis=axis...  54.2 us
    ppermute x4, starting transfers between devices, padded_2(): lax.ppermute(head, axis, [((i + 1) % count, i) for i in range(count)])  37.8 us
    ppermute x4, waiting for transfers between devices, padded_2(): lax.ppermute(head, axis, [((i + 1) % count, i) for i in range(count)])  18.5 us
    ppermute x4, waiting for transfers between devices, padded_2(): lax.ppermute(tail, axis, [(i, (i + 1) % count) for i in range(count)])  12 us
  transfers between devices with their start and end apart: 12, of which 8 were waited for; matrix products, arithmetic and copies ran while one was open for 0% of the time, Pallas kernels for 0%

commit v1 on v0

--- a/solution.py
+++ b/solution.py
@@ -157,7 +157,8 @@
 
 
 def global_sums(local_values):
-    return lax.psum(local_values, ("gx", "gy"))
+    column = jnp.sum(lax.all_gather(local_values, "gy"), axis=0)
+    return jnp.sum(lax.all_gather(column, "gx"), axis=0)
 
 
 def per_device(positions, polarity, direct_field, atom_count, pair_list, pair_count):
@@ -172,34 +173,51 @@
     pair_total = pair_count[0, 0]
     capacity_turns = -(-entries.shape[1] // pair_batch)
     live_turns = (pair_total + pair_batch - 1) // pair_batch
+
+    def mutual_field(geom_stack, dip_stack):
+        accumulated = accumulate(
+            geom_stack, dip_stack, entries, pair_total, live_turns, capacity_turns
+        )
+        accumulated = accumulated.reshape(5, blocks, 6, atom_width)
+        return (accumulated[0] + send_back(accumulated[1:5])) * atom_mask[:, None, :]
+
     residual = direct_field[0, 0] * atom_mask[:, None, :]
-    dipoles = jnp.zeros_like(residual)
-    geom_stack = None
     search = pol_wide * residual
-    rho_now = global_sums(set_sums(residual, search))
-    for iteration in range(ITERS):
-        operate_geom_stack = geom_stack
-        if operate_geom_stack is None:
-            stacked = neighbours(jnp.concatenate([geometry, search], axis=1))
-            operate_geom_stack = stacked[:, :, 0:4].reshape(5 * blocks, 4, atom_width)
-            dip_stack = stacked[:, :, 4:10].reshape(5 * blocks, 6, atom_width)
-        else:
-            dip_stack = neighbours(search).reshape(5 * blocks, 6, atom_width)
-        accumulated = accumulate(
-            operate_geom_stack, dip_stack, entries, pair_total, live_turns, capacity_turns
-        )
-        accumulated = accumulated.reshape(5, blocks, 6, atom_width)
-        mutual = (accumulated[0] + send_back(accumulated[1:5])) * atom_mask[:, None, :]
-        image_vec = search / pol_wide - mutual
-        geom_stack = operate_geom_stack
-        step_size = spread_sets(rho_now / global_sums(set_sums(search, image_vec)))
-        dipoles = dipoles + step_size * search
-        residual = residual - step_size * image_vec
-        if iteration + 1 < ITERS:
-            precond = pol_wide * residual
-            rho_next = global_sums(set_sums(residual, precond))
-            search = precond + spread_sets(rho_next / rho_now) * search
-            rho_now = rho_next
+    stacked = neighbours(jnp.concatenate([geometry, search], axis=1))
+    geom_stack = stacked[:, :, 0:4].reshape(5 * blocks, 4, atom_width)
+    dip_stack = stacked[:, :, 4:10].reshape(5 * blocks, 6, atom_width)
+    image = search / pol_wide - mutual_field(geom_stack, dip_stack)
+    scaled = pol_wide * image
+    scaled_dip = neighbours(scaled).reshape(5 * blocks, 6, atom_width)
+    image_scaled = scaled / pol_wide - mutual_field(geom_stack, scaled_dip)
+    first = global_sums(
+        jnp.concatenate([set_sums(residual, search), set_sums(search, image)])
+    )
+    rho_now = first[0:2]
+    curv_now = first[2:4]
+    step_size = spread_sets(rho_now / curv_now)
+    dipoles = step_size * search
+    residual = residual - step_size * image
+    precond = pol_wide * residual
+    precond_image = image - step_size * image_scaled
+    second = global_sums(
+        jnp.concatenate(
+            [
+                set_sums(residual, precond),
+                set_sums(precond, precond_image),
+                set_sums(precond, image) + set_sums(search, precond_image),
+            ]
+        )
+    )
+    rho_next = second[0:2]
+    ratio = rho_next / rho_now
+    curv_next = second[2:4] + ratio * second[4:6] + ratio * ratio * curv_now
+    ratio_wide = spread_sets(ratio)
+    search = precond + ratio_wide * search
+    image = precond_image + ratio_wide * image
+    step_size = spread_sets(rho_next / curv_next)
+    dipoles = dipoles + step_size * search
+    residual = residual - step_size * image
     return (dipoles[None, None], residual[None, None])
 
 

time: 572 us -> 567 us (level)
  starting transfers between devices: 49.7 us -> 115 us
  other arithmetic: 77.7 us -> 40.5 us
  waiting for transfers between devices: 38.8 us -> 16.8 us
  local copies, waits for them, and re-layouts: 34.1 us -> 23.1 us
    unnamed x0 -> x4, blocking collectives: none -> 361 us
    psum x3 -> x0, blocking collectives: 358 us -> none  [global_sums(): return lax.psum(local_values, ('gx', 'gy'))]
    ppermute x4, starting transfers between devices: 4.24 us -> 45.6 us  [from_behind(): return lax.ppermute(value, axis, pairs)]
    reduce_sum x24 -> x12, other arithmetic: 54.2 us -> 27.1 us  [tensor_apply(): jnp.sum(scaled * deltas[member] - coef_three * moments[member], axis=axis...]
    ppermute x4, waiting for transfers between devices: 18.5 us -> 0.66 us  [padded_2(): lax.ppermute(head, axis, [((i + 1) % count, i) for i in range(count)])]
    ppermute x4, starting transfers between devices: 7.68 us -> 24.9 us  [padded_2(): lax.ppermute(tail, axis, [(i, (i + 1) % count) for i in range(count)])]
    ppermute x4, starting transfers between devices: 37.8 us -> 44.2 us  [padded_2(): lax.ppermute(head, axis, [((i + 1) % count, i) for i in range(count)])]
  transfers between devices with their start and end apart: 12 -> 12, of which waited for: 8 -> 6; matrix products, arithmetic and copies ran while one was open for 0% -> 1% of each run, Pallas kernels for 0% -> 0%
where the time goes in v1:
time: 567 us; the launch traced here: 566 us
  blocking collectives  361 us (64%)
  starting transfers between devices  115 us (20%)
  other arithmetic  40.5 us (7%)
  local copies, waits for them, and re-layouts  23.1 us (4%)
  waiting for transfers between devices  16.8 us (3%)
    unnamed x4, blocking collectives  361 us
    ppermute x4, starting transfers between devices, from_behind(): return lax.ppermute(value, axis, pairs)  45.6 us
    ppermute x4, starting transfers between devices, padded_2(): lax.ppermute(head, axis, [((i + 1) % count, i) for i in range(count)])  44.2 us
    reduce_sum x12, other arithmetic, tensor_apply(): jnp.sum(scaled * deltas[member] - coef_three * moments[member], axis=axis...  27.1 us
    ppermute x4, starting transfers between devices, padded_2(): lax.ppermute(tail, axis, [(i, (i + 1) % count) for i in range(count)])  24.9 us
    ppermute x4, waiting for transfers between devices, padded_2(): lax.ppermute(tail, axis, [(i, (i + 1) % count) for i in range(count)])  12 us
  transfers between devices with their start and end apart: 12, of which 6 were waited for; matrix products, arithmetic and copies ran while one was open for 1% of the time, Pallas kernels for 0%

profile of v1, /device:TPU:1, one launch (start us, length us, event | category | flops | bytes accessed | tf_op | source)
XLA Modules:
  0.0 566.1 jit_solution(5256454796550048569)
XLA Ops:
  0.6 0.7 copy.77
  1.3 0.7 fusion.135
  2.1 0.7 copy-done.3
  2.8 20.2 %collective-permute-start = (f32[1,1,5,10,128]{4,3,2,1,0:T(8,128)S(1)}, f32[1,1,5,10,128]{4,3,2,1,0:T(8,128)S(1)}, u32[]{:S(2)}, u32[]{:S(2)}) collective-permute-start(f32[1,1,5,10,128]{4,3,2,1,0:T(8,128)S(1)} %get-tuple-element.426), channel_id=1, source_target_pairs={{1,0},{2,1},{3,2},{4,3},{5,4},{6,5},{7,6},{8,7},{9,8},{10,9},{11,1... | collective-permute-start | bytes 76808 | tf_op jit(solution)/shard_map/ppermute | solution.py:25
  23.0 1.9 collective-permute-start.1
  24.9 6.1 %collective-permute-done.1 = f32[1,1,5,10,128]{4,3,2,1,0:T(8,128)S(1)} collective-permute-done((f32[1,1,5,10,128]{4,3,2,1,0:T(8,128)S(1)}, f32[1,1,5,10,128]{4,3,2,1,0:T(8,128)S(1)}, u32[]{:S(2)}, u32[]{:S(2)}) %collective-permute-start.1) | collective-permute-done | bytes 25632 | tf_op jit(solution)/shard_map/ppermute | solution.py:23
  31.1 2.1 collective-permute-start.2
  33.9 0.7 copy-done.5
  34.5 2.5 collective-permute-done.2
  37.1 0.6 copy-done.1
  37.8 29.1 %while.26 = (s32[]{:T(128)}, f32[25,6,128]{2,0,1:T(8,128)S(1)}, s32[]{:T(128)}, s32[3,64]{1,0:T(4,128)S(1)}, s32[]{:T(128)}, /*index=5*/f32[25,4,128]{2,1,0:T(4,...) while((s32[]{:T(128)}, f32[25,6,128]{2,0,1:T(8,128)S(1)}, ...), condition=%wide.region_17.20_spmd.clone.clone.clone, body=%wide.region_2.19_spmd.sunk.clone.clone.clone.sunk | while | flops 20531916 | bytes 1168975 | solution.py:132
  37.9 0.6 gather_fusion.3
  38.5 0.6 gather_fusion.2
  40.7 0.7 compare_select_fusion.13
  41.4 2.7 fusion.176
  44.2 1.8 fusion.174
  46.0 0.7 compare_convert_fusion.4
  47.6 0.6 gather_fusion.3
  48.2 0.6 gather_fusion.2
  50.4 0.7 compare_select_fusion.13
  51.1 2.7 fusion.176
  53.9 1.8 fusion.174
  55.8 0.7 compare_convert_fusion.4
  57.3 0.6 gather_fusion.3
  57.9 0.6 gather_fusion.2
  60.1 0.7 compare_select_fusion.13
  60.8 2.7 fusion.176
  63.6 1.8 fusion.174
  65.5 0.7 compare_convert_fusion.4
  66.9 19.3 %collective-permute-start.3 = (f32[1,3,5,6,128]{4,3,2,1,0:T(8,128)S(1)}, f32[1,3,5,6,128]{4,3,2,1,0:T(8,128)S(1)}, u32[]{:S(2)}, u32[]{:S(2)}) collective-permute-start(f32[1,3,5,6,128]{4,3,2,1,0:T(8,128)S(1)} %bitcast.446), channel_id=1, source_target_pairs={{0,64},{64,128},{128,192},{192,256},{256,320},{320,384},{384,448},... | collective-permute-start | bytes 138248 | tf_op jit(solution)/shard_map/ppermute | solution.py:35
  86.2 1.3 collective-permute-done.3
  87.6 18.5 %collective-permute-start.4 = (f32[1,1,5,6,128]{4,3,2,1,0:T(8,128)S(1)}, f32[1,1,5,6,128]{4,3,2,1,0:T(8,128)S(1)}, u32[]{:S(2)}, u32[]{:S(2)}) collective-permute-start(f32[1,1,5,6,128]{4,3,2,1,0:T(8,128)S(1)} %get-tuple-element.424), channel_id=1, source_target_pairs={{0,1},{1,2},{2,3},{3,4},{4,5},{5,6},{6,7},{7,8},{8,9},{9,10},{10,1... | collective-permute-start | bytes 46088 | tf_op jit(solution)/shard_map/ppermute | solution.py:23
  106.0 14.7 %collective-permute-start.5 = (f32[1,1,5,6,128]{4,3,2,1,0:T(8,128)S(1)}, f32[1,1,5,6,128]{4,3,2,1,0:T(8,128)S(1)}, u32[]{:S(2)}, u32[]{:S(2)}) collective-permute-start(f32[1,1,5,6,128]{4,3,2,1,0:T(8,128)S(1)} %get-tuple-element.423), channel_id=1, source_target_pairs={{1,0},{2,1},{3,2},{4,3},{5,4},{6,5},{7,6},{8,7},{9,8},{10,9},{11,1... | collective-permute-start | bytes 46088 | tf_op jit(solution)/shard_map/ppermute | solution.py:25
  120.7 1.3 dynamic-slice
  122.0 1.3 dynamic-slice.1
  125.8 3.4 collective-permute-start.6
  129.2 1.9 collective-permute-start.7
  131.2 5.9 %collective-permute-done.7 = f32[1,1,5,6,128]{4,3,2,1,0:T(8,128)S(1)} collective-permute-done((f32[1,1,5,6,128]{4,3,2,1,0:T(8,128)S(1)}, f32[1,1,5,6,128]{4,3,2,1,0:T(8,128)S(1)}, u32[]{:S(2)}, u32[]{:S(2)}) %collective-permute-start.7) | collective-permute-done | bytes 15392 | tf_op jit(solution)/shard_map/ppermute | solution.py:23
  137.1 6.1 %collective-permute-start.8 = (f32[1,3,5,6,128]{4,3,2,1,0:T(8,128)S(1)}, f32[1,3,5,6,128]{4,3,2,1,0:T(8,128)S(1)}, u32[]{:S(2)}, u32[]{:S(2)}) collective-permute-start(f32[1,3,5,6,128]{4,3,2,1,0:T(8,128)S(1)} %pad_maximum_fusion.4), channel_id=1, source_target_pairs={{0,960},{64,0},{128,64},{192,128},{256,192},{320,256},{384,320},{4... | collective-permute-start | bytes 138248 | tf_op jit(solution)/shard_map/ppermute | solution.py:35
  144.1 29.2 %while.27 = (s32[]{:T(128)}, f32[25,6,128]{2,0,1:T(8,128)S(1)}, s32[]{:T(128)}, s32[3,64]{1,0:T(4,128)S(1)}, s32[]{:T(128)}, /*index=5*/f32[25,4,128]{2,1,0:T(4,...) while((s32[]{:T(128)}, f32[25,6,128]{2,0,1:T(8,128)S(1)}, ...), condition=%wide.region_39.42_spmd.clone.clone.clone, body=%wide.region_24.41_spmd.sunk.clone.clone.clone.sunk | while | flops 20531916 | bytes 1168975 | solution.py:132
  144.8 0.6 gather_fusion.6
  147.1 0.7 compare_select_fusion.15
  147.8 2.8 fusion.185
  150.6 1.8 fusion.183
  152.4 0.7 compare_convert_fusion.5
  154.0 0.6 gather_fusion.7
  156.8 0.7 compare_select_fusion.15
  157.5 2.8 fusion.185
  160.3 1.8 fusion.183
  162.2 0.7 compare_convert_fusion.5
  166.5 0.7 compare_select_fusion.15
  167.2 2.8 fusion.185
  170.0 1.8 fusion.183
  171.9 0.7 compare_convert_fusion.5
  173.4 18.1 %collective-permute-start.9 = (f32[1,3,5,6,128]{4,3,2,1,0:T(8,128)S(1)}, f32[1,3,5,6,128]{4,3,2,1,0:T(8,128)S(1)}, u32[]{:S(2)}, u32[]{:S(2)}) collective-permute-start(f32[1,3,5,6,128]{4,3,2,1,0:T(8,128)S(1)} %bitcast.444), channel_id=1, source_target_pairs={{0,64},{64,128},{128,192},{192,256},{256,320},{320,384},{384,448},... | collective-permute-start | bytes 138248 | tf_op jit(solution)/shard_map/ppermute | solution.py:35
  191.6 140.7 %all-reduce.1 = f32[256]{0:T(256)S(1)} all-reduce(f32[256]{0:T(256)S(1)} %maximum_dynamic-update-slice_fusion), channel_id=2, replica_groups=mesh['gx'=16,'gy'=64] {'gy'}, use_global_device_ids=true, to_apply=%add.1 | all-reduce | flops 256 | bytes 2048
  332.7 52.5 %all-reduce.2 = f32[64]{0:T(128)S(1)} all-reduce(f32[64]{0:T(128)S(1)} %dynamic-update-slice.1), channel_id=3, replica_groups=mesh['gx'=16,'gy'=64] {'gx'}, use_global_device_ids=true, to_apply=%add.2 | all-reduce | flops 64 | bytes 512
  385.4 2.6 collective-permute-start.10
  388.0 6.0 %collective-permute-start.11 = (f32[1,1,5,6,128]{4,3,2,1,0:T(8,128)S(1)}, f32[1,1,5,6,128]{4,3,2,1,0:T(8,128)S(1)}, u32[]{:S(2)}, u32[]{:S(2)}) collective-permute-start(f32[1,1,5,6,128]{4,3,2,1,0:T(8,128)S(1)} %get-tuple-element.421), channel_id=1, source_target_pairs={{1,0},{2,1},{3,2},{4,3},{5,4},{6,5},{7,6},{8,7},{9,8},{10,9},{11,1... | collective-permute-start | bytes 46088 | tf_op jit(solution)/shard_map/ppermute | solution.py:25
  394.2 0.7 collective-permute-done.11
  396.1 115.5 %all-reduce.3 = f32[384]{0:T(512)S(1)} all-reduce(f32[384]{0:T(512)S(1)} %maximum_dynamic-update-slice_fusion.1), channel_id=4, replica_groups=mesh['gx'=16,'gy'=64] {'gy'}, use_global_device_ids=true, to_apply=%add.3 | all-reduce | flops 384 | bytes 3072
  512.0 52.3 %all-reduce.4 = f32[96]{0:T(128)S(1)} all-reduce(f32[96]{0:T(128)S(1)} %dynamic-update-slice.3), channel_id=5, replica_groups=mesh['gx'=16,'gy'=64] {'gx'}, use_global_device_ids=true, to_apply=%add.4 | all-reduce | flops 96 | bytes 768
  564.8 0.6 copy.40
  565.5 0.6 copy.41
  (272 shorter events, 21.5 us)
Async XLA Ops:
  0.6 1.4 copy-start.4
  0.6 1.4 copy-start
  2.1 0.7 copy-start.3
  2.8 22.1 %collective-permute-start = (f32[1,1,5,10,128]{4,3,2,1,0:T(8,128)S(1)}, f32[1,1,5,10,128]{4,3,2,1,0:T(8,128)S(1)}, u32[]{:S(2)}, u32[]{:S(2)}) collective-permute-start(f32[1,1,5,10,128]{4,3,2,1,0:T(8,128)S(1)} %get-tuple-element.426), channel_id=1, source_target_pairs={{1,0},{2,1},{3,2},{4,3},{5,4},{6,5},{7,6},{8,7},{9,8},{10,9},{11,1... | collective-permute-start | bytes 76808 | tf_op jit(solution)/shard_map/ppermute | solution.py:25
  23.0 8.1 %collective-permute-start.1 = (f32[1,1,5,10,128]{4,3,2,1,0:T(8,128)S(1)}, f32[1,1,5,10,128]{4,3,2,1,0:T(8,128)S(1)}, u32[]{:S(2)}, u32[]{:S(2)}) collective-permute-start(f32[1,1,5,10,128]{4,3,2,1,0:T(8,128)S(1)} %get-tuple-element.426), channel_id=1, source_target_pairs={{0,1},{1,2},{2,3},{3,4},{4,5},{5,6},{6,7},{7,8},{8,9},{9,10},{10,1... | collective-permute-start | bytes 76808 | tf_op jit(solution)/shard_map/ppermute | solution.py:23
  31.1 6.0 %collective-permute-start.2 = (f32[1,3,5,10,128]{4,3,2,1,0:T(8,128)S(1)}, f32[1,3,5,10,128]{4,3,2,1,0:T(8,128)S(1)}, u32[]{:S(2)}, u32[]{:S(2)}) collective-permute-start(f32[1,3,5,10,128]{4,3,2,1,0:T(8,128)S(1)} %pad_maximum_fusion), channel_id=1, source_target_pairs={{0,960},{64,0},{128,64},{192,128},{256,192},{320,256},{384,320},{4... | collective-permute-start | bytes 230408 | tf_op jit(solution)/shard_map/ppermute | solution.py:35
  33.8 0.7 copy-start.5
  37.1 0.7 copy-start.1
  37.1 0.7 copy-start.2
  66.9 20.6 %collective-permute-start.3 = (f32[1,3,5,6,128]{4,3,2,1,0:T(8,128)S(1)}, f32[1,3,5,6,128]{4,3,2,1,0:T(8,128)S(1)}, u32[]{:S(2)}, u32[]{:S(2)}) collective-permute-start(f32[1,3,5,6,128]{4,3,2,1,0:T(8,128)S(1)} %bitcast.446), channel_id=1, source_target_pairs={{0,64},{64,128},{128,192},{192,256},{256,320},{320,384},{384,448},... | collective-permute-start | bytes 138248 | tf_op jit(solution)/shard_map/ppermute | solution.py:35
  87.6 38.2 %collective-permute-start.4 = (f32[1,1,5,6,128]{4,3,2,1,0:T(8,128)S(1)}, f32[1,1,5,6,128]{4,3,2,1,0:T(8,128)S(1)}, u32[]{:S(2)}, u32[]{:S(2)}) collective-permute-start(f32[1,1,5,6,128]{4,3,2,1,0:T(8,128)S(1)} %get-tuple-element.424), channel_id=1, source_target_pairs={{0,1},{1,2},{2,3},{3,4},{4,5},{5,6},{6,7},{7,8},{8,9},{9,10},{10,1... | collective-permute-start | bytes 46088 | tf_op jit(solution)/shard_map/ppermute | solution.py:23
  106.0 19.8 %collective-permute-start.5 = (f32[1,1,5,6,128]{4,3,2,1,0:T(8,128)S(1)}, f32[1,1,5,6,128]{4,3,2,1,0:T(8,128)S(1)}, u32[]{:S(2)}, u32[]{:S(2)}) collective-permute-start(f32[1,1,5,6,128]{4,3,2,1,0:T(8,128)S(1)} %get-tuple-element.423), channel_id=1, source_target_pairs={{1,0},{2,1},{3,2},{4,3},{5,4},{6,5},{7,6},{8,7},{9,8},{10,9},{11,1... | collective-permute-start | bytes 46088 | tf_op jit(solution)/shard_map/ppermute | solution.py:25
  125.8 5.3 collective-permute-start.6
  129.2 7.8 %collective-permute-start.7 = (f32[1,1,5,6,128]{4,3,2,1,0:T(8,128)S(1)}, f32[1,1,5,6,128]{4,3,2,1,0:T(8,128)S(1)}, u32[]{:S(2)}, u32[]{:S(2)}) collective-permute-start(f32[1,1,5,6,128]{4,3,2,1,0:T(8,128)S(1)} %get-tuple-element.357), channel_id=1, source_target_pairs={{0,1},{1,2},{2,3},{3,4},{4,5},{5,6},{6,7},{7,8},{8,9},{9,10},{10,1... | collective-permute-start | bytes 46088 | tf_op jit(solution)/shard_map/ppermute | solution.py:23
  137.1 7.0 %collective-permute-start.8 = (f32[1,3,5,6,128]{4,3,2,1,0:T(8,128)S(1)}, f32[1,3,5,6,128]{4,3,2,1,0:T(8,128)S(1)}, u32[]{:S(2)}, u32[]{:S(2)}) collective-permute-start(f32[1,3,5,6,128]{4,3,2,1,0:T(8,128)S(1)} %pad_maximum_fusion.4), channel_id=1, source_target_pairs={{0,960},{64,0},{128,64},{192,128},{256,192},{320,256},{384,320},{4... | collective-permute-start | bytes 138248 | tf_op jit(solution)/shard_map/ppermute | solution.py:35
  173.4 211.9 %collective-permute-start.9 = (f32[1,3,5,6,128]{4,3,2,1,0:T(8,128)S(1)}, f32[1,3,5,6,128]{4,3,2,1,0:T(8,128)S(1)}, u32[]{:S(2)}, u32[]{:S(2)}) collective-permute-start(f32[1,3,5,6,128]{4,3,2,1,0:T(8,128)S(1)} %bitcast.444), channel_id=1, source_target_pairs={{0,64},{64,128},{128,192},{192,256},{256,320},{320,384},{384,448},... | collective-permute-start | bytes 138248 | tf_op jit(solution)/shard_map/ppermute | solution.py:35
  385.4 8.9 %collective-permute-start.10 = (f32[1,1,5,6,128]{4,3,2,1,0:T(8,128)S(1)}, f32[1,1,5,6,128]{4,3,2,1,0:T(8,128)S(1)}, u32[]{:S(2)}, u32[]{:S(2)}) collective-permute-start(f32[1,1,5,6,128]{4,3,2,1,0:T(8,128)S(1)} %get-tuple-element.422), channel_id=1, source_target_pairs={{0,1},{1,2},{2,3},{3,4},{4,5},{5,6},{6,7},{7,8},{8,9},{9,10},{10,1... | collective-permute-start | bytes 46088 | tf_op jit(solution)/shard_map/ppermute | solution.py:23
  388.0 6.9 %collective-permute-start.11 = (f32[1,1,5,6,128]{4,3,2,1,0:T(8,128)S(1)}, f32[1,1,5,6,128]{4,3,2,1,0:T(8,128)S(1)}, u32[]{:S(2)}, u32[]{:S(2)}) collective-permute-start(f32[1,1,5,6,128]{4,3,2,1,0:T(8,128)S(1)} %get-tuple-element.421), channel_id=1, source_target_pairs={{1,0},{2,1},{3,2},{4,3},{5,4},{6,5},{7,6},{8,7},{9,8},{10,9},{11,1... | collective-permute-start | bytes 46088 | tf_op jit(solution)/shard_map/ppermute | solution.py:25

commit v2 on v1

--- a/solution.py
+++ b/solution.py
@@ -190,28 +190,34 @@
     scaled = pol_wide * image
     scaled_dip = neighbours(scaled).reshape(5 * blocks, 6, atom_width)
     image_scaled = scaled / pol_wide - mutual_field(geom_stack, scaled_dip)
-    first = global_sums(
-        jnp.concatenate([set_sums(residual, search), set_sums(search, image)])
-    )
-    rho_now = first[0:2]
-    curv_now = first[2:4]
-    step_size = spread_sets(rho_now / curv_now)
+    sums = global_sums(
+        jnp.concatenate(
+            [
+                set_sums(residual, search),
+                set_sums(search, image),
+                set_sums(image, scaled),
+                set_sums(search, image_scaled),
+                set_sums(scaled, image_scaled),
+            ]
+        )
+    )
+    rho_now = sums[0:2]
+    curv_now = sums[2:4]
+    image_pre = sums[4:6]
+    search_cross = sums[6:8]
+    scaled_curv = sums[8:10]
+    step_now = rho_now / curv_now
+    step_size = spread_sets(step_now)
     dipoles = step_size * search
     residual = residual - step_size * image
     precond = pol_wide * residual
     precond_image = image - step_size * image_scaled
-    second = global_sums(
-        jnp.concatenate(
-            [
-                set_sums(residual, precond),
-                set_sums(precond, precond_image),
-                set_sums(precond, image) + set_sums(search, precond_image),
-            ]
-        )
-    )
-    rho_next = second[0:2]
+    rho_next = rho_now - 2.0 * step_now * curv_now + step_now * step_now * image_pre
+    mixed = image_pre + search_cross
+    precond_curv = curv_now - step_now * mixed + step_now * step_now * scaled_curv
+    cross = 2.0 * curv_now - step_now * mixed
     ratio = rho_next / rho_now
-    curv_next = second[2:4] + ratio * second[4:6] + ratio * ratio * curv_now
+    curv_next = precond_curv + ratio * cross + ratio * ratio * curv_now
     ratio_wide = spread_sets(ratio)
     search = precond + ratio_wide * search
     image = precond_image + ratio_wide * image

time: 567 us -> 412 us (0.73)
  blocking collectives: 361 us -> 166 us
  other arithmetic: 40.5 us -> 78.6 us
  starting transfers between devices: 115 us -> 91.2 us
  local copies, waits for them, and re-layouts: 23.1 us -> 36.9 us
    unnamed x4 -> x2, blocking collectives: 361 us -> 166 us
    reduce_sum x12 -> x24, other arithmetic: 27.1 us -> 54.2 us  [tensor_apply(): jnp.sum(scaled * deltas[member] - coef_three * moments[member], axis=axis...]
    ppermute x4, starting transfers between devices: 24.9 us -> 7.68 us  [padded_2(): lax.ppermute(tail, axis, [(i, (i + 1) % count) for i in range(count)])]
  transfers between devices with their start and end apart: 12 -> 12, of which waited for: 6 -> 7; matrix products, arithmetic and copies ran while one was open for 1% -> 1% of each run, Pallas kernels for 0% -> 0%
where the time goes in v2:
time: 412 us; the launch traced here: 410 us
  blocking collectives  166 us (40%)
  starting transfers between devices  91.2 us (22%)
  other arithmetic  78.6 us (19%)
  local copies, waits for them, and re-layouts  36.9 us (9%)
  waiting for transfers between devices  22.4 us (5%)
  matrix products  8.54 us (2%)
    unnamed x2, blocking collectives  166 us
    reduce_sum x24, other arithmetic, tensor_apply(): jnp.sum(scaled * deltas[member] - coef_three * moments[member], axis=axis...  54.2 us
    ppermute x4, starting transfers between devices, from_behind(): return lax.ppermute(value, axis, pairs)  42.7 us
    ppermute x4, starting transfers between devices, padded_2(): lax.ppermute(head, axis, [((i + 1) % count, i) for i in range(count)])  40.8 us
    ppermute x4, waiting for transfers between devices, padded_2(): lax.ppermute(tail, axis, [(i, (i + 1) % count) for i in range(count)])  12 us
    ppermute x4, waiting for transfers between devices, from_behind(): return lax.ppermute(value, axis, pairs)  8.62 us
  transfers between devices with their start and end apart: 12, of which 7 were waited for; matrix products, arithmetic and copies ran while one was open for 1% of the time, Pallas kernels for 0%

profile of v2, /device:TPU:1, one launch (start us, length us, event | category | flops | bytes accessed | tf_op | source)
XLA Modules:
  0.0 410.2 jit_solution(2505431337952158167)
XLA Ops:
  0.6 0.7 copy.132
  1.3 0.7 fusion.128
  2.1 0.7 copy-done.3
  2.8 20.2 %collective-permute-start = (f32[1,1,5,10,128]{4,3,2,1,0:T(8,128)S(1)}, f32[1,1,5,10,128]{4,3,2,1,0:T(8,128)S(1)}, u32[]{:S(2)}, u32[]{:S(2)}) collective-permute-start(f32[1,1,5,10,128]{4,3,2,1,0:T(8,128)S(1)} %get-tuple-element.429), channel_id=1, source_target_pairs={{1,0},{2,1},{3,2},{4,3},{5,4},{6,5},{7,6},{8,7},{9,8},{10,9},{11,1... | collective-permute-start | bytes 76808 | tf_op jit(solution)/shard_map/ppermute | solution.py:25
  23.0 1.9 collective-permute-start.1
  24.9 6.1 %collective-permute-done.1 = f32[1,1,5,10,128]{4,3,2,1,0:T(8,128)S(1)} collective-permute-done((f32[1,1,5,10,128]{4,3,2,1,0:T(8,128)S(1)}, f32[1,1,5,10,128]{4,3,2,1,0:T(8,128)S(1)}, u32[]{:S(2)}, u32[]{:S(2)}) %collective-permute-start.1) | collective-permute-done | bytes 25632 | tf_op jit(solution)/shard_map/ppermute | solution.py:23
  31.1 2.1 collective-permute-start.2
  33.9 0.7 copy-done.5
  34.5 2.5 collective-permute-done.2
  37.8 58.3 %while.26 = (s32[]{:T(128)}, f32[25,6,128]{2,0,1:T(8,128)S(1)}, s32[]{:T(128)}, s32[3,64]{1,0:T(4,128)S(1)}, s32[]{:T(128)}, /*index=5*/f32[25,4,128]{2,1,0:T(4,...) while((s32[]{:T(128)}, f32[25,6,128]{2,0,1:T(8,128)S(1)}, ...), condition=%wide.region_17.20_spmd.clone.clone.clone, body=%wide.region_2.19_spmd.sunk.clone.clone.clone.sunk | while | flops 20531916 | bytes 1168975 | solution.py:132
  40.7 0.7 compare_select_fusion.13
  41.4 2.8 fusion.168
  44.2 1.8 fusion.166
  50.4 0.7 compare_select_fusion.13
  51.1 2.8 fusion.168
  54.0 1.8 fusion.166
  60.2 0.7 compare_select_fusion.13
  60.8 2.8 fusion.168
  63.7 1.8 fusion.166
  69.9 0.7 compare_select_fusion.13
  70.6 2.8 fusion.168
  73.4 1.8 fusion.166
  79.6 0.7 compare_select_fusion.13
  80.3 2.8 fusion.168
  83.1 1.8 fusion.166
  89.3 0.7 compare_select_fusion.13
  90.0 2.8 fusion.168
  92.8 1.8 fusion.166
  96.1 19.4 %collective-permute-start.3 = (f32[1,3,5,6,128]{4,3,2,1,0:T(8,128)S(1)}, f32[1,3,5,6,128]{4,3,2,1,0:T(8,128)S(1)}, u32[]{:S(2)}, u32[]{:S(2)}) collective-permute-start(f32[1,3,5,6,128]{4,3,2,1,0:T(8,128)S(1)} %bitcast.443), channel_id=1, source_target_pairs={{0,64},{64,128},{128,192},{192,256},{256,320},{320,384},{384,448},... | collective-permute-start | bytes 138248 | tf_op jit(solution)/shard_map/ppermute | solution.py:35
  115.5 1.2 collective-permute-done.3
  116.8 1.9 collective-permute-start.4
  118.7 6.7 %collective-permute-start.5 = (f32[1,1,5,6,128]{4,3,2,1,0:T(8,128)S(1)}, f32[1,1,5,6,128]{4,3,2,1,0:T(8,128)S(1)}, u32[]{:S(2)}, u32[]{:S(2)}) collective-permute-start(f32[1,1,5,6,128]{4,3,2,1,0:T(8,128)S(1)} %get-tuple-element.424), channel_id=1, source_target_pairs={{1,0},{2,1},{3,2},{4,3},{5,4},{6,5},{7,6},{8,7},{9,8},{10,9},{11,1... | collective-permute-start | bytes 46088 | tf_op jit(solution)/shard_map/ppermute | solution.py:25
  125.4 0.9 collective-permute-done.5
  126.4 7.3 %collective-permute-start.6 = (f32[1,1,5,6,128]{4,0,3,2,1:T(1,128)S(1)}, f32[1,1,5,6,128]{4,0,3,2,1:T(1,128)S(1)}, u32[]{:S(2)}, u32[]{:S(2)}) collective-permute-start(f32[1,1,5,6,128]{4,0,3,2,1:T(1,128)S(1)} %fusion.129), channel_id=1, source_target_pairs={{1,0},{2,1},{3,2},{4,3},{5,4},{6,5},{7,6},{8,7},{9,8},{10,9},{11,1... | collective-permute-start | bytes 46088 | tf_op jit(solution)/shard_map/ppermute | solution.py:25
  133.7 1.9 collective-permute-start.7
  135.6 5.9 %collective-permute-done.7 = f32[1,1,5,6,128]{4,1,3,2,0:T(1,128)S(1)} collective-permute-done((f32[1,1,5,6,128]{4,1,3,2,0:T(1,128)S(1)}, f32[1,1,5,6,128]{4,1,3,2,0:T(1,128)S(1)}, u32[]{:S(2)}, u32[]{:S(2)}) %collective-permute-start.7) | collective-permute-done | bytes 15392 | tf_op jit(solution)/shard_map/ppermute | solution.py:23
  141.5 1.8 collective-permute-start.8
  143.4 4.9 %collective-permute-done.8 = f32[1,3,5,6,128]{4,1,3,2,0:T(4,128)S(1)} collective-permute-done((f32[1,3,5,6,128]{4,1,3,2,0:T(4,128)S(1)}, f32[1,3,5,6,128]{4,1,3,2,0:T(4,128)S(1)}, u32[]{:S(2)}, u32[]{:S(2)}) %collective-permute-start.8) | collective-permute-done | bytes 46112 | tf_op jit(solution)/shard_map/ppermute | solution.py:35
  148.4 58.3 %while.27 = (s32[]{:T(128)}, f32[25,6,128]{2,0,1:T(8,128)S(1)}, s32[]{:T(128)}, s32[3,64]{1,0:T(4,128)S(1)}, s32[]{:T(128)}, /*index=5*/f32[25,4,128]{2,1,0:T(4,...) while((s32[]{:T(128)}, f32[25,6,128]{2,0,1:T(8,128)S(1)}, ...), condition=%wide.region_37.40_spmd.clone.clone.clone, body=%wide.region_22.39_spmd.sunk.clone.clone.clone.sunk | while | flops 20531916 | bytes 1168975 | solution.py:132
  151.4 0.7 compare_select_fusion.15
  152.1 2.8 fusion.177
  154.9 1.8 fusion.175
  161.1 0.7 compare_select_fusion.15
  161.8 2.8 fusion.177
  164.6 1.8 fusion.175
  171.5 2.8 fusion.177
  174.3 1.8 fusion.175
  180.5 0.7 compare_select_fusion.15
  181.2 2.8 fusion.177
  184.0 1.8 fusion.175
  190.2 0.7 compare_select_fusion.15
  190.9 2.8 fusion.177
  193.8 1.8 fusion.175
  200.6 2.8 fusion.177
  203.5 1.8 fusion.175
  206.7 19.4 %collective-permute-start.9 = (f32[1,3,5,6,128]{4,3,2,1,0:T(8,128)S(1)}, f32[1,3,5,6,128]{4,3,2,1,0:T(8,128)S(1)}, u32[]{:S(2)}, u32[]{:S(2)}) collective-permute-start(f32[1,3,5,6,128]{4,3,2,1,0:T(8,128)S(1)} %bitcast.442), channel_id=1, source_target_pairs={{0,64},{64,128},{128,192},{192,256},{256,320},{320,384},{384,448},... | collective-permute-start | bytes 138248 | tf_op jit(solution)/shard_map/ppermute | solution.py:35
  226.2 1.3 dynamic-slice
  227.4 1.3 dynamic-slice.1
  230.1 1.9 collective-permute-start.10
  232.0 6.7 %collective-permute-start.11 = (f32[1,1,5,6,128]{4,3,2,1,0:T(8,128)S(1)}, f32[1,1,5,6,128]{4,3,2,1,0:T(8,128)S(1)}, u32[]{:S(2)}, u32[]{:S(2)}) collective-permute-start(f32[1,1,5,6,128]{4,3,2,1,0:T(8,128)S(1)} %get-tuple-element.422), channel_id=1, source_target_pairs={{1,0},{2,1},{3,2},{4,3},{5,4},{6,5},{7,6},{8,7},{9,8},{10,9},{11,1... | collective-permute-start | bytes 46088 | tf_op jit(solution)/shard_map/ppermute | solution.py:25
  238.8 0.9 collective-permute-done.11
  241.2 115.3 %all-reduce.1 = f32[640]{0:T(1024)S(1)} all-reduce(f32[640]{0:T(1024)S(1)} %dynamic-update-slice), channel_id=2, replica_groups=mesh['gx'=16,'gy'=64] {'gy'}, use_global_device_ids=true, to_apply=%add.1 | all-reduce | flops 640 | bytes 5120
  356.9 51.2 %all-reduce.2 = f32[160]{0:T(256)S(1)} all-reduce(f32[160]{0:T(256)S(1)} %dynamic-update-slice.1), channel_id=3, replica_groups=mesh['gx'=16,'gy'=64] {'gx'}, use_global_device_ids=true, to_apply=%add.2 | all-reduce | flops 160 | bytes 1280
  408.9 0.7 copy_subtract_fusion
  (491 shorter events, 57.3 us)
Async XLA Ops:
  0.6 1.4 copy-start.4
  0.6 1.4 copy-start
  2.1 0.7 copy-start.3
  2.8 22.1 %collective-permute-start = (f32[1,1,5,10,128]{4,3,2,1,0:T(8,128)S(1)}, f32[1,1,5,10,128]{4,3,2,1,0:T(8,128)S(1)}, u32[]{:S(2)}, u32[]{:S(2)}) collective-permute-start(f32[1,1,5,10,128]{4,3,2,1,0:T(8,128)S(1)} %get-tuple-element.429), channel_id=1, source_target_pairs={{1,0},{2,1},{3,2},{4,3},{5,4},{6,5},{7,6},{8,7},{9,8},{10,9},{11,1... | collective-permute-start | bytes 76808 | tf_op jit(solution)/shard_map/ppermute | solution.py:25
  23.0 8.1 %collective-permute-start.1 = (f32[1,1,5,10,128]{4,3,2,1,0:T(8,128)S(1)}, f32[1,1,5,10,128]{4,3,2,1,0:T(8,128)S(1)}, u32[]{:S(2)}, u32[]{:S(2)}) collective-permute-start(f32[1,1,5,10,128]{4,3,2,1,0:T(8,128)S(1)} %get-tuple-element.429), channel_id=1, source_target_pairs={{0,1},{1,2},{2,3},{3,4},{4,5},{5,6},{6,7},{7,8},{8,9},{9,10},{10,1... | collective-permute-start | bytes 76808 | tf_op jit(solution)/shard_map/ppermute | solution.py:23
  31.1 6.0 %collective-permute-start.2 = (f32[1,3,5,10,128]{4,3,2,1,0:T(8,128)S(1)}, f32[1,3,5,10,128]{4,3,2,1,0:T(8,128)S(1)}, u32[]{:S(2)}, u32[]{:S(2)}) collective-permute-start(f32[1,3,5,10,128]{4,3,2,1,0:T(8,128)S(1)} %pad_maximum_fusion), channel_id=1, source_target_pairs={{0,960},{64,0},{128,64},{192,128},{256,192},{320,256},{384,320},{4... | collective-permute-start | bytes 230408 | tf_op jit(solution)/shard_map/ppermute | solution.py:35
  33.8 0.7 copy-start.5
  37.1 0.7 copy-start.1
  37.1 0.7 copy-start.2
  96.1 20.6 %collective-permute-start.3 = (f32[1,3,5,6,128]{4,3,2,1,0:T(8,128)S(1)}, f32[1,3,5,6,128]{4,3,2,1,0:T(8,128)S(1)}, u32[]{:S(2)}, u32[]{:S(2)}) collective-permute-start(f32[1,3,5,6,128]{4,3,2,1,0:T(8,128)S(1)} %bitcast.443), channel_id=1, source_target_pairs={{0,64},{64,128},{128,192},{192,256},{256,320},{320,384},{384,448},... | collective-permute-start | bytes 138248 | tf_op jit(solution)/shard_map/ppermute | solution.py:35
  116.8 8.6 %collective-permute-start.4 = (f32[1,1,5,6,128]{4,3,2,1,0:T(8,128)S(1)}, f32[1,1,5,6,128]{4,3,2,1,0:T(8,128)S(1)}, u32[]{:S(2)}, u32[]{:S(2)}) collective-permute-start(f32[1,1,5,6,128]{4,3,2,1,0:T(8,128)S(1)} %get-tuple-element.425), channel_id=1, source_target_pairs={{0,1},{1,2},{2,3},{3,4},{4,5},{5,6},{6,7},{7,8},{8,9},{9,10},{10,1... | collective-permute-start | bytes 46088 | tf_op jit(solution)/shard_map/ppermute | solution.py:23
  118.7 7.6 %collective-permute-start.5 = (f32[1,1,5,6,128]{4,3,2,1,0:T(8,128)S(1)}, f32[1,1,5,6,128]{4,3,2,1,0:T(8,128)S(1)}, u32[]{:S(2)}, u32[]{:S(2)}) collective-permute-start(f32[1,1,5,6,128]{4,3,2,1,0:T(8,128)S(1)} %get-tuple-element.424), channel_id=1, source_target_pairs={{1,0},{2,1},{3,2},{4,3},{5,4},{6,5},{7,6},{8,7},{9,8},{10,9},{11,1... | collective-permute-start | bytes 46088 | tf_op jit(solution)/shard_map/ppermute | solution.py:25
  126.4 9.2 %collective-permute-start.6 = (f32[1,1,5,6,128]{4,0,3,2,1:T(1,128)S(1)}, f32[1,1,5,6,128]{4,0,3,2,1:T(1,128)S(1)}, u32[]{:S(2)}, u32[]{:S(2)}) collective-permute-start(f32[1,1,5,6,128]{4,0,3,2,1:T(1,128)S(1)} %fusion.129), channel_id=1, source_target_pairs={{1,0},{2,1},{3,2},{4,3},{5,4},{6,5},{7,6},{8,7},{9,8},{10,9},{11,1... | collective-permute-start | bytes 46088 | tf_op jit(solution)/shard_map/ppermute | solution.py:25
  133.7 7.8 %collective-permute-start.7 = (f32[1,1,5,6,128]{4,1,3,2,0:T(1,128)S(1)}, f32[1,1,5,6,128]{4,1,3,2,0:T(1,128)S(1)}, u32[]{:S(2)}, u32[]{:S(2)}) collective-permute-start(f32[1,1,5,6,128]{4,1,3,2,0:T(1,128)S(1)} %get-tuple-element.360), channel_id=1, source_target_pairs={{0,1},{1,2},{2,3},{3,4},{4,5},{5,6},{6,7},{7,8},{8,9},{9,10},{10,1... | collective-permute-start | bytes 46088 | tf_op jit(solution)/shard_map/ppermute | solution.py:23
  141.5 6.8 %collective-permute-start.8 = (f32[1,3,5,6,128]{4,1,3,2,0:T(4,128)S(1)}, f32[1,3,5,6,128]{4,1,3,2,0:T(4,128)S(1)}, u32[]{:S(2)}, u32[]{:S(2)}) collective-permute-start(f32[1,3,5,6,128]{4,1,3,2,0:T(4,128)S(1)} %pad_maximum_fusion.4), channel_id=1, source_target_pairs={{0,960},{64,0},{128,64},{192,128},{256,192},{320,256},{384,320},{4... | collective-permute-start | bytes 138248 | tf_op jit(solution)/shard_map/ppermute | solution.py:35
  206.7 23.3 %collective-permute-start.9 = (f32[1,3,5,6,128]{4,3,2,1,0:T(8,128)S(1)}, f32[1,3,5,6,128]{4,3,2,1,0:T(8,128)S(1)}, u32[]{:S(2)}, u32[]{:S(2)}) collective-permute-start(f32[1,3,5,6,128]{4,3,2,1,0:T(8,128)S(1)} %bitcast.442), channel_id=1, source_target_pairs={{0,64},{64,128},{128,192},{192,256},{256,320},{320,384},{384,448},... | collective-permute-start | bytes 138248 | tf_op jit(solution)/shard_map/ppermute | solution.py:35
  230.1 8.6 %collective-permute-start.10 = (f32[1,1,5,6,128]{4,3,2,1,0:T(8,128)S(1)}, f32[1,1,5,6,128]{4,3,2,1,0:T(8,128)S(1)}, u32[]{:S(2)}, u32[]{:S(2)}) collective-permute-start(f32[1,1,5,6,128]{4,3,2,1,0:T(8,128)S(1)} %get-tuple-element.423), channel_id=1, source_target_pairs={{0,1},{1,2},{2,3},{3,4},{4,5},{5,6},{6,7},{7,8},{8,9},{9,10},{10,1... | collective-permute-start | bytes 46088 | tf_op jit(solution)/shard_map/ppermute | solution.py:23
  232.0 7.6 %collective-permute-start.11 = (f32[1,1,5,6,128]{4,3,2,1,0:T(8,128)S(1)}, f32[1,1,5,6,128]{4,3,2,1,0:T(8,128)S(1)}, u32[]{:S(2)}, u32[]{:S(2)}) collective-permute-start(f32[1,1,5,6,128]{4,3,2,1,0:T(8,128)S(1)} %get-tuple-element.422), channel_id=1, source_target_pairs={{1,0},{2,1},{3,2},{4,3},{5,4},{6,5},{7,6},{8,7},{9,8},{10,9},{11,1... | collective-permute-start | bytes 46088 | tf_op jit(solution)/shard_map/ppermute | solution.py:25

commit v3 on v2

--- a/solution.py
+++ b/solution.py
@@ -157,8 +157,7 @@
 
 
 def global_sums(local_values):
-    column = jnp.sum(lax.all_gather(local_values, "gy"), axis=0)
-    return jnp.sum(lax.all_gather(column, "gx"), axis=0)
+    return lax.psum(local_values, ("gx", "gy"))
 
 
 def per_device(positions, polarity, direct_field, atom_count, pair_list, pair_count):

time: 412 us -> 349 us (0.85)
  starting transfers between devices: 91.2 us -> 140 us
  blocking collectives: 166 us -> 119 us
  other arithmetic: 78.6 us -> 40.7 us
  local copies, waits for them, and re-layouts: 36.9 us -> 19.1 us
  matrix products: 8.54 us -> 4.27 us
    unnamed x2 -> x0, blocking collectives: 166 us -> none
    psum x0 -> x1, blocking collectives: none -> 119 us  [global_sums(): return lax.psum(local_values, ('gx', 'gy'))]
    ppermute x4, starting transfers between devices: 42.7 us -> 82.4 us  [from_behind(): return lax.ppermute(value, axis, pairs)]
    reduce_sum x24 -> x12, other arithmetic: 54.2 us -> 27.1 us  [tensor_apply(): jnp.sum(scaled * deltas[member] - coef_three * moments[member], axis=axis...]
    ppermute x4, starting transfers between devices: 40.8 us -> 49.5 us  [padded_2(): lax.ppermute(head, axis, [((i + 1) % count, i) for i in range(count)])]
  transfers between devices with their start and end apart: 12 -> 12, of which waited for: 7 -> 8; matrix products, arithmetic and copies ran while one was open for 1% -> 0% of each run, Pallas kernels for 0% -> 0%
where the time goes in v3:
time: 349 us; the launch traced here: 348 us
  starting transfers between devices  140 us (40%)
  blocking collectives  119 us (34%)
  other arithmetic  40.7 us (12%)
  waiting for transfers between devices  22.8 us (7%)
  local copies, waits for them, and re-layouts  19.1 us (5%)
  matrix products  4.27 us (1%)
    psum x1, blocking collectives, global_sums(): return lax.psum(local_values, ('gx', 'gy'))  119 us
    ppermute x4, starting transfers between devices, from_behind(): return lax.ppermute(value, axis, pairs)  82.4 us
    ppermute x4, starting transfers between devices, padded_2(): lax.ppermute(head, axis, [((i + 1) % count, i) for i in range(count)])  49.5 us
    reduce_sum x12, other arithmetic, tensor_apply(): jnp.sum(scaled * deltas[member] - coef_three * moments[member], axis=axis...  27.1 us
    ppermute x4, waiting for transfers between devices, padded_2(): lax.ppermute(tail, axis, [(i, (i + 1) % count) for i in range(count)])  12 us
    ppermute x4, waiting for transfers between devices, from_behind(): return lax.ppermute(value, axis, pairs)  9.1 us
    ppermute x4, starting transfers between devices, padded_2(): lax.ppermute(tail, axis, [(i, (i + 1) % count) for i in range(count)])  7.68 us
  transfers between devices with their start and end apart: 12, of which 8 were waited for; matrix products, arithmetic and copies ran while one was open for 0% of the time, Pallas kernels for 0%

profile of v3, /device:TPU:1, one launch (start us, length us, event | category | flops | bytes accessed | tf_op | source)
XLA Modules:
  0.0 348.3 jit_solution(15049300558398456946)
XLA Ops:
  0.6 0.7 copy.132
  1.3 0.7 fusion.128
  2.1 0.7 copy-done.3
  2.8 20.2 %collective-permute-start = (f32[1,1,5,10,128]{4,3,2,1,0:T(8,128)S(1)}, f32[1,1,5,10,128]{4,3,2,1,0:T(8,128)S(1)}, u32[]{:S(2)}, u32[]{:S(2)}) collective-permute-start(f32[1,1,5,10,128]{4,3,2,1,0:T(8,128)S(1)} %get-tuple-element.429), channel_id=1, source_target_pairs={{1,0},{2,1},{3,2},{4,3},{5,4},{6,5},{7,6},{8,7},{9,8},{10,9},{11,1... | collective-permute-start | bytes 76808 | tf_op jit(solution)/shard_map/ppermute | solution.py:25
  23.0 1.9 collective-permute-start.1
  24.9 6.1 %collective-permute-done.1 = f32[1,1,5,10,128]{4,3,2,1,0:T(8,128)S(1)} collective-permute-done((f32[1,1,5,10,128]{4,3,2,1,0:T(8,128)S(1)}, f32[1,1,5,10,128]{4,3,2,1,0:T(8,128)S(1)}, u32[]{:S(2)}, u32[]{:S(2)}) %collective-permute-start.1) | collective-permute-done | bytes 25632 | tf_op jit(solution)/shard_map/ppermute | solution.py:23
  31.1 2.1 collective-permute-start.2
  33.9 0.7 copy-done.5
  34.5 2.5 collective-permute-done.2
  37.1 0.6 copy-done.1
  37.8 29.1 %while.26 = (s32[]{:T(128)}, f32[25,6,128]{2,0,1:T(8,128)S(1)}, s32[]{:T(128)}, s32[3,64]{1,0:T(4,128)S(1)}, s32[]{:T(128)}, /*index=5*/f32[25,4,128]{2,1,0:T(4,...) while((s32[]{:T(128)}, f32[25,6,128]{2,0,1:T(8,128)S(1)}, ...), condition=%wide.region_17.20_spmd.clone.clone.clone, body=%wide.region_2.19_spmd.sunk.clone.clone.clone.sunk | while | flops 20531916 | bytes 1168975 | solution.py:132
  37.9 0.6 gather_fusion.3
  38.5 0.6 gather_fusion.2
  40.7 0.7 compare_select_fusion.13
  41.4 2.8 fusion.168
  44.2 1.8 fusion.166
  46.1 0.7 compare_convert_fusion.4
  47.6 0.6 gather_fusion.3
  48.2 0.6 gather_fusion.2
  50.4 0.7 compare_select_fusion.13
  51.1 2.8 fusion.168
  54.0 1.8 fusion.166
  55.8 0.7 compare_convert_fusion.4
  57.3 0.6 gather_fusion.3
  57.9 0.6 gather_fusion.2
  60.2 0.7 compare_select_fusion.13
  60.8 2.8 fusion.168
  63.7 1.8 fusion.166
  65.5 0.7 compare_convert_fusion.4
  66.9 38.8 %collective-permute-start.3 = (f32[1,3,5,6,128]{4,3,2,1,0:T(8,128)S(1)}, f32[1,3,5,6,128]{4,3,2,1,0:T(8,128)S(1)}, u32[]{:S(2)}, u32[]{:S(2)}) collective-permute-start(f32[1,3,5,6,128]{4,3,2,1,0:T(8,128)S(1)} %bitcast.440), channel_id=1, source_target_pairs={{0,64},{64,128},{128,192},{192,256},{256,320},{320,384},{384,448},... | collective-permute-start | bytes 138248 | tf_op jit(solution)/shard_map/ppermute | solution.py:35
  105.8 1.2 collective-permute-done.3
  107.1 1.9 collective-permute-start.4
  109.0 11.2 %collective-permute-start.5 = (f32[1,1,5,6,128]{4,3,2,1,0:T(8,128)S(1)}, f32[1,1,5,6,128]{4,3,2,1,0:T(8,128)S(1)}, u32[]{:S(2)}, u32[]{:S(2)}) collective-permute-start(f32[1,1,5,6,128]{4,3,2,1,0:T(8,128)S(1)} %get-tuple-element.424), channel_id=1, source_target_pairs={{1,0},{2,1},{3,2},{4,3},{5,4},{6,5},{7,6},{8,7},{9,8},{10,9},{11,1... | collective-permute-start | bytes 46088 | tf_op jit(solution)/shard_map/ppermute | solution.py:25
  120.2 0.9 collective-permute-done.5
  121.2 7.0 %collective-permute-start.6 = (f32[1,1,5,6,128]{4,0,3,2,1:T(1,128)S(1)}, f32[1,1,5,6,128]{4,0,3,2,1:T(1,128)S(1)}, u32[]{:S(2)}, u32[]{:S(2)}) collective-permute-start(f32[1,1,5,6,128]{4,0,3,2,1:T(1,128)S(1)} %fusion.129), channel_id=1, source_target_pairs={{1,0},{2,1},{3,2},{4,3},{5,4},{6,5},{7,6},{8,7},{9,8},{10,9},{11,1... | collective-permute-start | bytes 46088 | tf_op jit(solution)/shard_map/ppermute | solution.py:25
  128.1 1.9 collective-permute-start.7
  130.1 5.9 %collective-permute-done.7 = f32[1,1,5,6,128]{4,1,3,2,0:T(1,128)S(1)} collective-permute-done((f32[1,1,5,6,128]{4,1,3,2,0:T(1,128)S(1)}, f32[1,1,5,6,128]{4,1,3,2,0:T(1,128)S(1)}, u32[]{:S(2)}, u32[]{:S(2)}) %collective-permute-start.7) | collective-permute-done | bytes 15392 | tf_op jit(solution)/shard_map/ppermute | solution.py:23
  136.0 2.7 collective-permute-start.8
  138.7 4.1 %collective-permute-done.8 = f32[1,3,5,6,128]{4,1,3,2,0:T(4,128)S(1)} collective-permute-done((f32[1,3,5,6,128]{4,1,3,2,0:T(4,128)S(1)}, f32[1,3,5,6,128]{4,1,3,2,0:T(4,128)S(1)}, u32[]{:S(2)}, u32[]{:S(2)}) %collective-permute-start.8) | collective-permute-done | bytes 46112 | tf_op jit(solution)/shard_map/ppermute | solution.py:35
  142.9 29.2 %while.27 = (s32[]{:T(128)}, f32[25,6,128]{2,0,1:T(8,128)S(1)}, s32[]{:T(128)}, s32[3,64]{1,0:T(4,128)S(1)}, s32[]{:T(128)}, /*index=5*/f32[25,4,128]{2,1,0:T(4,...) while((s32[]{:T(128)}, f32[25,6,128]{2,0,1:T(8,128)S(1)}, ...), condition=%wide.region_37.40_spmd.clone.clone.clone, body=%wide.region_22.39_spmd.sunk.clone.clone.clone.sunk | while | flops 20531916 | bytes 1168975 | solution.py:132
  143.0 0.6 gather_fusion.7
  143.6 0.6 gather_fusion.6
  145.9 0.7 compare_select_fusion.15
  146.6 2.8 fusion.177
  149.4 1.8 fusion.175
  151.2 0.7 compare_convert_fusion.5
  152.7 0.6 gather_fusion.7
  153.3 0.6 gather_fusion.6
  155.6 0.7 compare_select_fusion.15
  156.3 2.8 fusion.177
  159.1 1.8 fusion.175
  160.9 0.7 compare_convert_fusion.5
  165.3 0.7 compare_select_fusion.15
  166.0 2.8 fusion.177
  168.8 1.8 fusion.175
  170.7 0.7 compare_convert_fusion.5
  172.1 38.8 %collective-permute-start.9 = (f32[1,3,5,6,128]{4,3,2,1,0:T(8,128)S(1)}, f32[1,3,5,6,128]{4,3,2,1,0:T(8,128)S(1)}, u32[]{:S(2)}, u32[]{:S(2)}) collective-permute-start(f32[1,3,5,6,128]{4,3,2,1,0:T(8,128)S(1)} %bitcast.441), channel_id=1, source_target_pairs={{0,64},{64,128},{128,192},{192,256},{256,320},{320,384},{384,448},... | collective-permute-start | bytes 138248 | tf_op jit(solution)/shard_map/ppermute | solution.py:35
  211.0 1.2 collective-permute-done.9
  212.3 1.9 collective-permute-start.10
  214.2 11.1 %collective-permute-start.11 = (f32[1,1,5,6,128]{4,3,2,1,0:T(8,128)S(1)}, f32[1,1,5,6,128]{4,3,2,1,0:T(8,128)S(1)}, u32[]{:S(2)}, u32[]{:S(2)}) collective-permute-start(f32[1,1,5,6,128]{4,3,2,1,0:T(8,128)S(1)} %get-tuple-element.422), channel_id=1, source_target_pairs={{1,0},{2,1},{3,2},{4,3},{5,4},{6,5},{7,6},{8,7},{9,8},{10,9},{11,1... | collective-permute-start | bytes 46088 | tf_op jit(solution)/shard_map/ppermute | solution.py:25
  225.4 0.9 collective-permute-done.11
  227.6 118.6 %psum.7 = f32[10]{0:T(128)S(1)} all-reduce(f32[10]{0:T(128)S(1)} %concatenate.35), channel_id=1, replica_groups=mesh['gx'=16,'gy'=64] {'gx','gy'}, use_global_device_ids=true, to_apply=%region_42.45 | all-reduce | flops 10 | bytes 80 | tf_op jit(solution)/shard_map/psum | solution.py:160
  347.0 0.7 copy_subtract_fusion
  347.7 0.6 copy.82
  (258 shorter events, 18.7 us)
Async XLA Ops:
  0.6 1.4 copy-start.4
  0.6 1.4 copy-start
  2.1 0.7 copy-start.3
  2.8 22.1 %collective-permute-start = (f32[1,1,5,10,128]{4,3,2,1,0:T(8,128)S(1)}, f32[1,1,5,10,128]{4,3,2,1,0:T(8,128)S(1)}, u32[]{:S(2)}, u32[]{:S(2)}) collective-permute-start(f32[1,1,5,10,128]{4,3,2,1,0:T(8,128)S(1)} %get-tuple-element.429), channel_id=1, source_target_pairs={{1,0},{2,1},{3,2},{4,3},{5,4},{6,5},{7,6},{8,7},{9,8},{10,9},{11,1... | collective-permute-start | bytes 76808 | tf_op jit(solution)/shard_map/ppermute | solution.py:25
  23.0 8.1 %collective-permute-start.1 = (f32[1,1,5,10,128]{4,3,2,1,0:T(8,128)S(1)}, f32[1,1,5,10,128]{4,3,2,1,0:T(8,128)S(1)}, u32[]{:S(2)}, u32[]{:S(2)}) collective-permute-start(f32[1,1,5,10,128]{4,3,2,1,0:T(8,128)S(1)} %get-tuple-element.429), channel_id=1, source_target_pairs={{0,1},{1,2},{2,3},{3,4},{4,5},{5,6},{6,7},{7,8},{8,9},{9,10},{10,1... | collective-permute-start | bytes 76808 | tf_op jit(solution)/shard_map/ppermute | solution.py:23
  31.1 6.0 %collective-permute-start.2 = (f32[1,3,5,10,128]{4,3,2,1,0:T(8,128)S(1)}, f32[1,3,5,10,128]{4,3,2,1,0:T(8,128)S(1)}, u32[]{:S(2)}, u32[]{:S(2)}) collective-permute-start(f32[1,3,5,10,128]{4,3,2,1,0:T(8,128)S(1)} %pad_maximum_fusion), channel_id=1, source_target_pairs={{0,960},{64,0},{128,64},{192,128},{256,192},{320,256},{384,320},{4... | collective-permute-start | bytes 230408 | tf_op jit(solution)/shard_map/ppermute | solution.py:35
  33.8 0.7 copy-start.5
  37.1 0.7 copy-start.1
  37.1 0.7 copy-start.2
  66.9 40.1 %collective-permute-start.3 = (f32[1,3,5,6,128]{4,3,2,1,0:T(8,128)S(1)}, f32[1,3,5,6,128]{4,3,2,1,0:T(8,128)S(1)}, u32[]{:S(2)}, u32[]{:S(2)}) collective-permute-start(f32[1,3,5,6,128]{4,3,2,1,0:T(8,128)S(1)} %bitcast.440), channel_id=1, source_target_pairs={{0,64},{64,128},{128,192},{192,256},{256,320},{320,384},{384,448},... | collective-permute-start | bytes 138248 | tf_op jit(solution)/shard_map/ppermute | solution.py:35
  107.1 13.2 %collective-permute-start.4 = (f32[1,1,5,6,128]{4,3,2,1,0:T(8,128)S(1)}, f32[1,1,5,6,128]{4,3,2,1,0:T(8,128)S(1)}, u32[]{:S(2)}, u32[]{:S(2)}) collective-permute-start(f32[1,1,5,6,128]{4,3,2,1,0:T(8,128)S(1)} %get-tuple-element.425), channel_id=1, source_target_pairs={{0,1},{1,2},{2,3},{3,4},{4,5},{5,6},{6,7},{7,8},{8,9},{9,10},{10,1... | collective-permute-start | bytes 46088 | tf_op jit(solution)/shard_map/ppermute | solution.py:23
  109.0 12.1 %collective-permute-start.5 = (f32[1,1,5,6,128]{4,3,2,1,0:T(8,128)S(1)}, f32[1,1,5,6,128]{4,3,2,1,0:T(8,128)S(1)}, u32[]{:S(2)}, u32[]{:S(2)}) collective-permute-start(f32[1,1,5,6,128]{4,3,2,1,0:T(8,128)S(1)} %get-tuple-element.424), channel_id=1, source_target_pairs={{1,0},{2,1},{3,2},{4,3},{5,4},{6,5},{7,6},{8,7},{9,8},{10,9},{11,1... | collective-permute-start | bytes 46088 | tf_op jit(solution)/shard_map/ppermute | solution.py:25
  121.2 8.9 %collective-permute-start.6 = (f32[1,1,5,6,128]{4,0,3,2,1:T(1,128)S(1)}, f32[1,1,5,6,128]{4,0,3,2,1:T(1,128)S(1)}, u32[]{:S(2)}, u32[]{:S(2)}) collective-permute-start(f32[1,1,5,6,128]{4,0,3,2,1:T(1,128)S(1)} %fusion.129), channel_id=1, source_target_pairs={{1,0},{2,1},{3,2},{4,3},{5,4},{6,5},{7,6},{8,7},{9,8},{10,9},{11,1... | collective-permute-start | bytes 46088 | tf_op jit(solution)/shard_map/ppermute | solution.py:25
  128.1 7.8 %collective-permute-start.7 = (f32[1,1,5,6,128]{4,1,3,2,0:T(1,128)S(1)}, f32[1,1,5,6,128]{4,1,3,2,0:T(1,128)S(1)}, u32[]{:S(2)}, u32[]{:S(2)}) collective-permute-start(f32[1,1,5,6,128]{4,1,3,2,0:T(1,128)S(1)} %get-tuple-element.360), channel_id=1, source_target_pairs={{0,1},{1,2},{2,3},{3,4},{4,5},{5,6},{6,7},{7,8},{8,9},{9,10},{10,1... | collective-permute-start | bytes 46088 | tf_op jit(solution)/shard_map/ppermute | solution.py:23
  136.0 6.8 %collective-permute-start.8 = (f32[1,3,5,6,128]{4,1,3,2,0:T(4,128)S(1)}, f32[1,3,5,6,128]{4,1,3,2,0:T(4,128)S(1)}, u32[]{:S(2)}, u32[]{:S(2)}) collective-permute-start(f32[1,3,5,6,128]{4,1,3,2,0:T(4,128)S(1)} %pad_maximum_fusion.4), channel_id=1, source_target_pairs={{0,960},{64,0},{128,64},{192,128},{256,192},{320,256},{384,320},{4... | collective-permute-start | bytes 138248 | tf_op jit(solution)/shard_map/ppermute | solution.py:35
  172.1 40.1 %collective-permute-start.9 = (f32[1,3,5,6,128]{4,3,2,1,0:T(8,128)S(1)}, f32[1,3,5,6,128]{4,3,2,1,0:T(8,128)S(1)}, u32[]{:S(2)}, u32[]{:S(2)}) collective-permute-start(f32[1,3,5,6,128]{4,3,2,1,0:T(8,128)S(1)} %bitcast.441), channel_id=1, source_target_pairs={{0,64},{64,128},{128,192},{192,256},{256,320},{320,384},{384,448},... | collective-permute-start | bytes 138248 | tf_op jit(solution)/shard_map/ppermute | solution.py:35
  212.3 13.1 %collective-permute-start.10 = (f32[1,1,5,6,128]{4,3,2,1,0:T(8,128)S(1)}, f32[1,1,5,6,128]{4,3,2,1,0:T(8,128)S(1)}, u32[]{:S(2)}, u32[]{:S(2)}) collective-permute-start(f32[1,1,5,6,128]{4,3,2,1,0:T(8,128)S(1)} %get-tuple-element.423), channel_id=1, source_target_pairs={{0,1},{1,2},{2,3},{3,4},{4,5},{5,6},{6,7},{7,8},{8,9},{9,10},{10,1... | collective-permute-start | bytes 46088 | tf_op jit(solution)/shard_map/ppermute | solution.py:23
  214.2 12.0 %collective-permute-start.11 = (f32[1,1,5,6,128]{4,3,2,1,0:T(8,128)S(1)}, f32[1,1,5,6,128]{4,3,2,1,0:T(8,128)S(1)}, u32[]{:S(2)}, u32[]{:S(2)}) collective-permute-start(f32[1,1,5,6,128]{4,3,2,1,0:T(8,128)S(1)} %get-tuple-element.422), channel_id=1, source_target_pairs={{1,0},{2,1},{3,2},{4,3},{5,4},{6,5},{7,6},{8,7},{9,8},{10,9},{11,1... | collective-permute-start | bytes 46088 | tf_op jit(solution)/shard_map/ppermute | solution.py:25

commit v4 on v3

--- a/solution.py
+++ b/solution.py
@@ -8,7 +8,6 @@
 
 thole_factor = 0.39
 column_width = 8.0
-pair_batch = 8
 slot_shift_x = (0.0, 0.0, 1.0, 1.0, 1.0)
 slot_shift_y = (0.0, 1.0, -1.0, 0.0, 1.0)
 
@@ -51,7 +50,7 @@
     )
 
 
-def pair_fields(geom_i, geom_j, dip_i, dip_j, slot_ids, same_block):
+def pair_fields(geom_i, geom_j, dip_i, dip_j, slot_ids, same_block, two_way=True):
     chosen = (slot_ids[:, None] == jnp.arange(5, dtype=jnp.int32)[None, :]).astype(jnp.float32)
     offset_x = column_width * jnp.sum(
         chosen * jnp.array(slot_shift_x, jnp.float32)[None, :], axis=1
@@ -84,6 +83,8 @@
         ],
         axis=1,
     )
+    if not two_way:
+        return (forward, None)
     backward = jnp.concatenate(
         [
             tensor_apply(coef_three, coef_five, deltas, dip_i[:, 0:3], 1),
@@ -94,44 +95,94 @@
     return (forward, backward)
 
 
-def accumulate(geom_stack, dip_stack, entries, pair_total, live_turns, capacity_turns):
-    blocks = geom_stack.shape[0] // 5
-    atom_width = geom_stack.shape[2]
-    targets = jnp.arange(5 * blocks, dtype=jnp.int32)
-    padded = jnp.pad(entries, ((0, 0), (0, capacity_turns * pair_batch - entries.shape[1])))
-
-    def one_turn(turn_index, accumulated):
-        first_row = (turn_index * pair_batch).astype(jnp.int32)
-        group_rows = lax.dynamic_slice_in_dim(padded, first_row, pair_batch, 1)
-        own_block = group_rows[0]
-        slot_ids = group_rows[1]
-        other_block = group_rows[2]
-        source = slot_ids * blocks + other_block
-        live_rows = (first_row + jnp.arange(pair_batch, dtype=jnp.int32) < pair_total).astype(
-            jnp.float32
-        )
-        same_block = (slot_ids == 0) & (own_block == other_block)
+def pair_presence(entries, pair_total, blocks):
+    live = jnp.arange(entries.shape[1], dtype=jnp.int32) < pair_total
+    own_block, slot_ids, other_block = entries[0], entries[1], entries[2]
+    shift = other_block - own_block + 1
+    hit = (
+        live[:, None, None, None]
+        & (slot_ids[:, None, None, None] == jnp.arange(5, dtype=jnp.int32)[None, :, None, None])
+        & (shift[:, None, None, None] == jnp.arange(3, dtype=jnp.int32)[None, None, :, None])
+        & (own_block[:, None, None, None] == jnp.arange(blocks, dtype=jnp.int32)[None, None, None, :])
+    )
+    return jnp.sum(hit.astype(jnp.float32), axis=0)
+
+
+def shifted_batch(own, other, blocks):
+    first = jnp.concatenate([own[1:blocks], own, own[0 : blocks - 1]], axis=0)
+    second = jnp.concatenate([other[0 : blocks - 1], other, other[1:blocks]], axis=0)
+    return first, second
+
+
+def gated(values, present):
+    return jnp.where(present[:, None, None] > 0, values, 0.0)
+
+
+def accumulate(geom_stack, dip_stack, presence):
+    blocks = geom_stack.shape[1]
+    geom_own = geom_stack[0]
+    dip_own = dip_stack[0]
+    same, _ = pair_fields(
+        geom_own,
+        geom_own,
+        dip_own,
+        dip_own,
+        jnp.zeros((blocks,), jnp.int32),
+        jnp.ones((blocks,), bool),
+        two_way=False,
+    )
+    own_total = gated(same, presence[0, 1])
+    count = blocks - 1
+    forward, backward = pair_fields(
+        geom_own[0:count],
+        geom_own[1:blocks],
+        dip_own[0:count],
+        dip_own[1:blocks],
+        jnp.zeros((count,), jnp.int32),
+        jnp.zeros((count,), bool),
+    )
+    near = presence[0, 2, 0:count]
+    zero_block = jnp.zeros_like(own_total[0:1])
+    own_total = own_total + jnp.concatenate([gated(forward, near), zero_block], axis=0)
+    own_total = own_total + jnp.concatenate([zero_block, gated(backward, near)], axis=0)
+    own_i, _ = shifted_batch(geom_own, geom_own, blocks)
+    dip_i, _ = shifted_batch(dip_own, dip_own, blocks)
+    width = 3 * blocks - 2
+
+    def one_slot(slot_index, carry):
+        own_acc, other_acc = carry
+        geom_j = lax.dynamic_index_in_dim(geom_stack, slot_index, 0, keepdims=False)
+        dip_j = lax.dynamic_index_in_dim(dip_stack, slot_index, 0, keepdims=False)
+        _, geom_j = shifted_batch(geom_j, geom_j, blocks)
+        _, dip_j = shifted_batch(dip_j, dip_j, blocks)
+        listed = lax.dynamic_index_in_dim(presence, slot_index, 0, keepdims=False)
+        present = jnp.concatenate([listed[0, 1:blocks], listed[1], listed[2, 0:count]])
         forward, backward = pair_fields(
-            jnp.take(geom_stack, own_block, axis=0),
-            jnp.take(geom_stack, source, axis=0),
-            jnp.take(dip_stack, own_block, axis=0),
-            jnp.take(dip_stack, source, axis=0),
-            slot_ids,
-            same_block,
-        )
-        to_own = (own_block[:, None] == targets[None, :]).astype(jnp.float32) * live_rows[:, None]
-        twoway = live_rows * (1.0 - same_block.astype(jnp.float32))
-        to_other = (source[:, None] == targets[None, :]).astype(jnp.float32) * twoway[:, None]
-        accumulated = accumulated + jnp.einsum(
-            "gt,gca->tca", to_own, forward, precision=lax.Precision.HIGHEST
-        )
-        return accumulated + jnp.einsum(
-            "gt,gca->tca", to_other, backward, precision=lax.Precision.HIGHEST
-        )
-
-    return lax.fori_loop(
-        0, live_turns, one_turn, jnp.zeros((5 * blocks, 6, atom_width), jnp.float32)
-    )
+            own_i,
+            geom_j,
+            dip_i,
+            dip_j,
+            jnp.full((width,), slot_index, jnp.int32),
+            jnp.zeros((width,), bool),
+        )
+        forward = gated(forward, present)
+        backward = gated(backward, present)
+        own_acc = (
+            own_acc
+            + jnp.concatenate([zero_block, forward[0:count]], axis=0)
+            + forward[count : count + blocks]
+            + jnp.concatenate([forward[count + blocks : width], zero_block], axis=0)
+        )
+        other_sum = (
+            jnp.concatenate([backward[0:count], zero_block], axis=0)
+            + backward[count : count + blocks]
+            + jnp.concatenate([zero_block, backward[count + blocks : width]], axis=0)
+        )
+        other_acc = lax.dynamic_update_index_in_dim(other_acc, other_sum, slot_index - 1, 0)
+        return own_acc, other_acc
+
+    other_acc = jnp.zeros((4,) + own_total.shape, jnp.float32)
+    return lax.fori_loop(1, 5, one_slot, (own_total, other_acc))
 
 
 def neighbours(block_data):
@@ -170,24 +221,20 @@
     geometry = jnp.concatenate([positions[0, 0], pol_wide], axis=1)
     entries = pair_list[0, 0]
     pair_total = pair_count[0, 0]
-    capacity_turns = -(-entries.shape[1] // pair_batch)
-    live_turns = (pair_total + pair_batch - 1) // pair_batch
+    presence = pair_presence(entries, pair_total, blocks)
 
     def mutual_field(geom_stack, dip_stack):
-        accumulated = accumulate(
-            geom_stack, dip_stack, entries, pair_total, live_turns, capacity_turns
-        )
-        accumulated = accumulated.reshape(5, blocks, 6, atom_width)
-        return (accumulated[0] + send_back(accumulated[1:5])) * atom_mask[:, None, :]
+        own_total, other_acc = accumulate(geom_stack, dip_stack, presence)
+        return (own_total + send_back(other_acc)) * atom_mask[:, None, :]
 
     residual = direct_field[0, 0] * atom_mask[:, None, :]
     search = pol_wide * residual
     stacked = neighbours(jnp.concatenate([geometry, search], axis=1))
-    geom_stack = stacked[:, :, 0:4].reshape(5 * blocks, 4, atom_width)
-    dip_stack = stacked[:, :, 4:10].reshape(5 * blocks, 6, atom_width)
+    geom_stack = stacked[:, :, 0:4]
+    dip_stack = stacked[:, :, 4:10]
     image = search / pol_wide - mutual_field(geom_stack, dip_stack)
     scaled = pol_wide * image
-    scaled_dip = neighbours(scaled).reshape(5 * blocks, 6, atom_width)
+    scaled_dip = neighbours(scaled)
     image_scaled = scaled / pol_wide - mutual_field(geom_stack, scaled_dip)
     sums = global_sums(
         jnp.concatenate(

time: 349 us -> 257 us (0.74)
  starting transfers between devices: 140 us -> 56.5 us
  other arithmetic: 40.7 us -> 59.2 us
  local copies, waits for them, and re-layouts: 19.1 us -> 7.72 us
  waiting for transfers between devices: 22.8 us -> 12.5 us
  matrix products: 4.27 us -> 0 us
    ppermute x4, starting transfers between devices: 82.4 us -> 8.11 us  [from_behind(): return lax.ppermute(value, axis, pairs)]
    reduce_sum x12 -> x22, other arithmetic: 27.1 us -> 52.2 us  [tensor_apply(): jnp.sum(scaled * deltas[member] - coef_three * moments[member], axis=axis...]
    gather x24 -> x0, local copies, waits for them, and re-layouts: 13.6 us -> none  [the longest x6 3.45 us: one_turn(): jnp.take(geom_stack, source, axis=0)]
    ppermute x4, waiting for transfers between devices: 12 us -> 1.95 us  [padded_2(): lax.ppermute(tail, axis, [(i, (i + 1) % count) for i in range(count)])]
    ppermute x4, starting transfers between devices: 49.5 us -> 40.5 us  [padded_2(): lax.ppermute(head, axis, [((i + 1) % count, i) for i in range(count)])]
    dot_general x12 -> x0, matrix products: 4.27 us -> none  [the longest x6 2.14 us: one_turn(): jnp.einsum('gt,gca->tca', to_other, backward, precision=lax.Precision.HIG...]
    mul x10 -> x2, other arithmetic: 4.01 us -> 0.02 us  [the longest x1 0.01 us: pair_fields(): coef_five = keep_pair * 3.0 * lambda_five * inv_cube * inv_dist * inv_dist]
    convert_element_type x6 -> x0, other arithmetic: 3.91 us -> none  [one_turn(): (first_row + jnp.arange(pair_batch, dtype=jnp.int32) < pair_total).astype...]
  transfers between devices with their start and end apart: 12 -> 12, of which waited for: 8 -> 7; matrix products, arithmetic and copies ran while one was open for 0% -> 4% of each run, Pallas kernels for 0% -> 0%
where the time goes in v4:
time: 257 us; the launch traced here: 256 us
  blocking collectives  117 us (46%)
  other arithmetic  59.2 us (23%)
  starting transfers between devices  56.5 us (22%)
  waiting for transfers between devices  12.5 us (5%)
  local copies, waits for them, and re-layouts  7.72 us (3%)
    psum x1, blocking collectives, global_sums(): return lax.psum(local_values, ('gx', 'gy'))  117 us
    reduce_sum x22, other arithmetic, tensor_apply(): jnp.sum(scaled * deltas[member] - coef_three * moments[member], axis=axis...  52.2 us
    ppermute x4, starting transfers between devices, padded_2(): lax.ppermute(head, axis, [((i + 1) % count, i) for i in range(count)])  40.5 us
    ppermute x4, waiting for transfers between devices, from_behind(): return lax.ppermute(value, axis, pairs)  9.15 us
    ppermute x4, starting transfers between devices, from_behind(): return lax.ppermute(value, axis, pairs)  8.11 us
    ppermute x4, starting transfers between devices, padded_2(): lax.ppermute(tail, axis, [(i, (i + 1) % count) for i in range(count)])  7.86 us
  transfers between devices with their start and end apart: 12, of which 7 were waited for; matrix products, arithmetic and copies ran while one was open for 4% of the time, Pallas kernels for 0%

profile of v4, /device:TPU:1, one launch (start us, length us, event | category | flops | bytes accessed | tf_op | source)
XLA Modules:
  0.0 256.4 jit_solution(4351848561750266266)
XLA Ops:
  0.6 0.7 copy.197
  1.3 0.7 fusion.233
  2.1 0.7 copy-done.4
  2.8 20.2 %collective-permute-start = (f32[1,1,5,10,128]{4,3,2,1,0:T(8,128)S(1)}, f32[1,1,5,10,128]{4,3,2,1,0:T(8,128)S(1)}, u32[]{:S(2)}, u32[]{:S(2)}) collective-permute-start(f32[1,1,5,10,128]{4,3,2,1,0:T(8,128)S(1)} %get-tuple-element.1101), channel_id=1, source_target_pairs={{1,0},{2,1},{3,2},{4,3},{5,4},{6,5},{7,6},{8,7},{9,8},{10,9},{11,1... | collective-permute-start | bytes 76808 | tf_op jit(solution)/shard_map/ppermute | solution.py:24
  23.0 1.9 collective-permute-start.1
  25.0 0.7 copy-done.6
  25.7 0.6 copy-done.1
  26.3 0.1 select_reduce_fusion.6
  26.4 0.2 select_reduce_fusion.4
  27.4 0.1 convert_reduce_fusion
  27.5 0.2 fusion.236
  27.7 0.2 fusion.235
  28.0 0.8 fusion.202
  28.7 1.3 fusion.204
  30.3 1.4 fusion.132
  32.1 0.1 copy.36
  32.2 1.0 collective-permute-start.2
  33.2 3.8 %collective-permute-done.2 = f32[1,3,5,10,128]{4,3,2,1,0:T(8,128)S(1)} collective-permute-done((f32[1,3,5,10,128]{4,3,2,1,0:T(8,128)S(1)}, f32[1,3,5,10,128]{4,3,2,1,0:T(8,128)S(1)}, u32[]{:S(2)}, u32[]{:S(2)}) %collective-permute-start.2) | collective-permute-done | bytes 76832 | tf_op jit(solution)/shard_map/ppermute | solution.py:34
  37.1 0.6 copy-done.3
  37.8 26.2 %while.44 = (s32[]{:T(128)}, f32[5,6,128]{2,0,1:T(8,128)S(1)}, f32[4,5,6,128]{3,2,1,0:T(8,128)S(1)}, f32[5,3,5]{2,1,0:T(4,128)S(1)}, f32[5,5,4,128]{3,1,2,0:T(8,...) while((s32[]{:T(128)}, f32[5,6,128]{2,0,1:T(8,128)S(1)}, ...), condition=%wide.region_40.41_spmd.clone, body=%wide.region_25.40_spmd.sunk.clone.sunk | while | flops 25193012 | bytes 1431648 | solution.py:185
  38.1 3.5 %fusion.270 = (f32[13,128]{1,0:T(8,128)S(1)}, f32[13,128]{1,0:T(8,128)S(1)}, f32[13,128]{1,0:T(8,128)S(1)}, f32[13,128]{1,0:T(8,128)S(1)}, f32[13,128]{1,0:T(8,1...) fusion(f32[13,128]{1,0:T(8,128)S(1)} %get-tuple-element.1371, ...), kind=kLoop, calls=%fused_computation.71.clone.1 | loop fusion | flops 16385408 | bytes 173056 | tf_op jit(solution)/shard_map/while/body/eval_jaxpr/reduce_sum | solution.py:46
  41.8 2.2 fusion.272
  44.6 3.5 %fusion.270 = (f32[13,128]{1,0:T(8,128)S(1)}, f32[13,128]{1,0:T(8,128)S(1)}, f32[13,128]{1,0:T(8,128)S(1)}, f32[13,128]{1,0:T(8,128)S(1)}, f32[13,128]{1,0:T(8,1...) fusion(f32[13,128]{1,0:T(8,128)S(1)} %get-tuple-element.1371, ...), kind=kLoop, calls=%fused_computation.71.clone.1 | loop fusion | flops 16385408 | bytes 173056 | tf_op jit(solution)/shard_map/while/body/eval_jaxpr/reduce_sum | solution.py:46
  48.4 2.2 fusion.272
  51.2 3.5 %fusion.270 = (f32[13,128]{1,0:T(8,128)S(1)}, f32[13,128]{1,0:T(8,128)S(1)}, f32[13,128]{1,0:T(8,128)S(1)}, f32[13,128]{1,0:T(8,128)S(1)}, f32[13,128]{1,0:T(8,1...) fusion(f32[13,128]{1,0:T(8,128)S(1)} %get-tuple-element.1371, ...), kind=kLoop, calls=%fused_computation.71.clone.1 | loop fusion | flops 16385408 | bytes 173056 | tf_op jit(solution)/shard_map/while/body/eval_jaxpr/reduce_sum | solution.py:46
  54.9 2.2 fusion.272
  57.7 3.5 %fusion.270 = (f32[13,128]{1,0:T(8,128)S(1)}, f32[13,128]{1,0:T(8,128)S(1)}, f32[13,128]{1,0:T(8,128)S(1)}, f32[13,128]{1,0:T(8,128)S(1)}, f32[13,128]{1,0:T(8,1...) fusion(f32[13,128]{1,0:T(8,128)S(1)} %get-tuple-element.1371, ...), kind=kLoop, calls=%fused_computation.71.clone.1 | loop fusion | flops 16385408 | bytes 173056 | tf_op jit(solution)/shard_map/while/body/eval_jaxpr/reduce_sum | solution.py:46
  61.5 2.2 fusion.272
  64.0 2.7 %collective-permute-done.3 = f32[1,3,5,6,128]{4,3,2,1,0:T(8,128)S(1)} collective-permute-done((f32[1,3,5,6,128]{4,3,2,1,0:T(8,128)S(1)}, f32[1,3,5,6,128]{4,3,2,1,0:T(8,128)S(1)}, u32[]{:S(2)}, u32[]{:S(2)}) %collective-permute-start.3) | collective-permute-done | bytes 46112 | tf_op jit(solution)/shard_map/ppermute | solution.py:34
  66.7 1.9 collective-permute-start.4
  68.7 6.7 %collective-permute-start.5 = (f32[1,1,5,6,128]{4,3,2,1,0:T(8,128)S(1)}, f32[1,1,5,6,128]{4,3,2,1,0:T(8,128)S(1)}, u32[]{:S(2)}, u32[]{:S(2)}) collective-permute-start(f32[1,1,5,6,128]{4,3,2,1,0:T(8,128)S(1)} %get-tuple-element.1095), channel_id=1, source_target_pairs={{1,0},{2,1},{3,2},{4,3},{5,4},{6,5},{7,6},{8,7},{9,8},{10,9},{11,1... | collective-permute-start | bytes 46088 | tf_op jit(solution)/shard_map/ppermute | solution.py:24
  75.4 0.9 collective-permute-done.5
  76.3 7.0 %collective-permute-start.6 = (f32[1,1,5,6,128]{4,3,2,1,0:T(8,128)S(1)}, f32[1,1,5,6,128]{4,3,2,1,0:T(8,128)S(1)}, u32[]{:S(2)}, u32[]{:S(2)}) collective-permute-start(f32[1,1,5,6,128]{4,3,2,1,0:T(8,128)S(1)} %get-tuple-element.1103), channel_id=1, source_target_pairs={{1,0},{2,1},{3,2},{4,3},{5,4},{6,5},{7,6},{8,7},{9,8},{10,9},{11,1... | collective-permute-start | bytes 46088 | tf_op jit(solution)/shard_map/ppermute | solution.py:24
  83.3 2.1 collective-permute-start.7
  85.4 1.3 fusion.212
  86.8 1.4 fusion.136
  88.3 0.6 fusion.216
  89.2 1.9 collective-permute-done.7
  91.2 7.1 %collective-permute-start.8 = (f32[1,3,5,6,128]{4,3,2,1,0:T(8,128)S(1)}, f32[1,3,5,6,128]{4,3,2,1,0:T(8,128)S(1)}, u32[]{:S(2)}, u32[]{:S(2)}) collective-permute-start(f32[1,3,5,6,128]{4,3,2,1,0:T(8,128)S(1)} %pad_maximum_fusion.8), channel_id=1, source_target_pairs={{0,960},{64,0},{128,64},{192,128},{256,192},{320,256},{384,320},{4... | collective-permute-start | bytes 138248 | tf_op jit(solution)/shard_map/ppermute | solution.py:34
  98.3 0.9 collective-permute-done.8
  99.2 26.2 %while.45 = (s32[]{:T(128)}, f32[5,6,128]{2,0,1:T(8,128)S(1)}, f32[4,5,6,128]{3,2,1,0:T(8,128)S(1)}, f32[5,3,5]{2,1,0:T(4,128)S(1)}, f32[5,5,4,128]{3,1,2,0:T(8,...) while((s32[]{:T(128)}, f32[5,6,128]{2,0,1:T(8,128)S(1)}, ...), condition=%wide.region_82.83_spmd.clone, body=%wide.region_67.82_spmd.sunk.clone.sunk | while | flops 25193012 | bytes 1431648 | solution.py:185
  99.5 3.5 %fusion.277 = (f32[13,128]{1,0:T(8,128)S(1)}, f32[13,128]{1,0:T(8,128)S(1)}, f32[13,128]{1,0:T(8,128)S(1)}, f32[13,128]{1,0:T(8,128)S(1)}, f32[13,128]{1,0:T(8,1...) fusion(f32[13,128]{1,0:T(8,128)S(1)} %get-tuple-element.1425, ...), kind=kLoop, calls=%fused_computation.207.clone.1 | loop fusion | flops 16385408 | bytes 173056 | tf_op jit(solution)/shard_map/while/body/eval_jaxpr/reduce_sum | solution.py:46
  103.3 2.2 fusion.279
  106.1 3.5 %fusion.277 = (f32[13,128]{1,0:T(8,128)S(1)}, f32[13,128]{1,0:T(8,128)S(1)}, f32[13,128]{1,0:T(8,128)S(1)}, f32[13,128]{1,0:T(8,128)S(1)}, f32[13,128]{1,0:T(8,1...) fusion(f32[13,128]{1,0:T(8,128)S(1)} %get-tuple-element.1425, ...), kind=kLoop, calls=%fused_computation.207.clone.1 | loop fusion | flops 16385408 | bytes 173056 | tf_op jit(solution)/shard_map/while/body/eval_jaxpr/reduce_sum | solution.py:46
  109.9 2.2 fusion.279
  112.6 3.5 %fusion.277 = (f32[13,128]{1,0:T(8,128)S(1)}, f32[13,128]{1,0:T(8,128)S(1)}, f32[13,128]{1,0:T(8,128)S(1)}, f32[13,128]{1,0:T(8,128)S(1)}, f32[13,128]{1,0:T(8,1...) fusion(f32[13,128]{1,0:T(8,128)S(1)} %get-tuple-element.1425, ...), kind=kLoop, calls=%fused_computation.207.clone.1 | loop fusion | flops 16385408 | bytes 173056 | tf_op jit(solution)/shard_map/while/body/eval_jaxpr/reduce_sum | solution.py:46
  116.4 2.2 fusion.279
  119.2 3.5 %fusion.277 = (f32[13,128]{1,0:T(8,128)S(1)}, f32[13,128]{1,0:T(8,128)S(1)}, f32[13,128]{1,0:T(8,128)S(1)}, f32[13,128]{1,0:T(8,128)S(1)}, f32[13,128]{1,0:T(8,1...) fusion(f32[13,128]{1,0:T(8,128)S(1)} %get-tuple-element.1425, ...), kind=kLoop, calls=%fused_computation.207.clone.1 | loop fusion | flops 16385408 | bytes 173056 | tf_op jit(solution)/shard_map/while/body/eval_jaxpr/reduce_sum | solution.py:46
  123.0 2.2 fusion.279
  125.4 1.7 collective-permute-done.9
  127.2 1.9 collective-permute-start.10
  129.1 6.7 %collective-permute-start.11 = (f32[1,1,5,6,128]{4,3,2,1,0:T(8,128)S(1)}, f32[1,1,5,6,128]{4,3,2,1,0:T(8,128)S(1)}, u32[]{:S(2)}, u32[]{:S(2)}) collective-permute-start(f32[1,1,5,6,128]{4,3,2,1,0:T(8,128)S(1)} %get-tuple-element.1093), channel_id=1, source_target_pairs={{1,0},{2,1},{3,2},{4,3},{5,4},{6,5},{7,6},{8,7},{9,8},{10,9},{11,1... | collective-permute-start | bytes 46088 | tf_op jit(solution)/shard_map/ppermute | solution.py:24
  135.8 0.1 fusion.232
  136.0 0.1 reduce_sum.1103
  136.2 0.5 collective-permute-done.11
  136.7 0.2 multiply_reduce_fusion
  137.2 0.1 reduce_sum.1129
  137.3 0.1 reduce_sum.1132
  137.4 0.1 reduce_sum.1157
  137.5 0.1 reduce_sum.1160
  137.7 116.8 %psum.7 = f32[10]{0:T(128)S(1)} all-reduce(f32[10]{0:T(128)S(1)} %concatenate.296), channel_id=1, replica_groups=mesh['gx'=16,'gy'=64] {'gx','gy'}, use_global_device_ids=true, to_apply=%region_87.88 | all-reduce | flops 10 | bytes 80 | tf_op jit(solution)/shard_map/psum | solution.py:211
  255.1 0.1 multiply_subtract_fusion
  255.2 0.6 broadcast_in_dim.348
  255.8 0.6 broadcast_in_dim.349
  (426 shorter events, 7.7 us)
Async XLA Ops:
  0.6 1.4 copy-start.5
  0.6 1.4 copy-start
  2.1 0.7 copy-start.4
  2.8 29.4 %collective-permute-start = (f32[1,1,5,10,128]{4,3,2,1,0:T(8,128)S(1)}, f32[1,1,5,10,128]{4,3,2,1,0:T(8,128)S(1)}, u32[]{:S(2)}, u32[]{:S(2)}) collective-permute-start(f32[1,1,5,10,128]{4,3,2,1,0:T(8,128)S(1)} %get-tuple-element.1101), channel_id=1, source_target_pairs={{1,0},{2,1},{3,2},{4,3},{5,4},{6,5},{7,6},{8,7},{9,8},{10,9},{11,1... | collective-permute-start | bytes 76808 | tf_op jit(solution)/shard_map/ppermute | solution.py:24
  23.0 9.2 %collective-permute-start.1 = (f32[1,1,5,10,128]{4,3,2,1,0:T(8,128)S(1)}, f32[1,1,5,10,128]{4,3,2,1,0:T(8,128)S(1)}, u32[]{:S(2)}, u32[]{:S(2)}) collective-permute-start(f32[1,1,5,10,128]{4,3,2,1,0:T(8,128)S(1)} %get-tuple-element.1101), channel_id=1, source_target_pairs={{0,1},{1,2},{2,3},{3,4},{4,5},{5,6},{6,7},{7,8},{8,9},{9,10},{10,1... | collective-permute-start | bytes 76808 | tf_op jit(solution)/shard_map/ppermute | solution.py:22
  24.9 0.7 copy-start.6
  25.6 0.7 copy-start.1
  25.6 0.7 copy-start.2
  32.2 4.8 %collective-permute-start.2 = (f32[1,3,5,10,128]{4,3,2,1,0:T(8,128)S(1)}, f32[1,3,5,10,128]{4,3,2,1,0:T(8,128)S(1)}, u32[]{:S(2)}, u32[]{:S(2)}) collective-permute-start(f32[1,3,5,10,128]{4,3,2,1,0:T(8,128)S(1)} %pad_maximum_fusion.4), channel_id=1, source_target_pairs={{0,960},{64,0},{128,64},{192,128},{256,192},{320,256},{384,320},{4... | collective-permute-start | bytes 230408 | tf_op jit(solution)/shard_map/ppermute | solution.py:34
  37.1 0.7 copy-start.3
  63.9 2.8 %collective-permute-start.3 = (f32[1,3,5,6,128]{4,3,2,1,0:T(8,128)S(1)}, f32[1,3,5,6,128]{4,3,2,1,0:T(8,128)S(1)}, u32[]{:S(2)}, u32[]{:S(2)}) collective-permute-start(f32[1,3,5,6,128]{4,3,2,1,0:T(8,128)S(1)} %slice_bitcast_fusion.47), channel_id=1, source_target_pairs={{0,64},{64,128},{128,192},{192,256},{256,320},{320,384},{384,448},... | collective-permute-start | bytes 138248 | tf_op jit(solution)/shard_map/ppermute | solution.py:34
  66.7 8.6 %collective-permute-start.4 = (f32[1,1,5,6,128]{4,3,2,1,0:T(8,128)S(1)}, f32[1,1,5,6,128]{4,3,2,1,0:T(8,128)S(1)}, u32[]{:S(2)}, u32[]{:S(2)}) collective-permute-start(f32[1,1,5,6,128]{4,3,2,1,0:T(8,128)S(1)} %get-tuple-element.1096), channel_id=1, source_target_pairs={{0,1},{1,2},{2,3},{3,4},{4,5},{5,6},{6,7},{7,8},{8,9},{9,10},{10,1... | collective-permute-start | bytes 46088 | tf_op jit(solution)/shard_map/ppermute | solution.py:22
  68.7 7.6 %collective-permute-start.5 = (f32[1,1,5,6,128]{4,3,2,1,0:T(8,128)S(1)}, f32[1,1,5,6,128]{4,3,2,1,0:T(8,128)S(1)}, u32[]{:S(2)}, u32[]{:S(2)}) collective-permute-start(f32[1,1,5,6,128]{4,3,2,1,0:T(8,128)S(1)} %get-tuple-element.1095), channel_id=1, source_target_pairs={{1,0},{2,1},{3,2},{4,3},{5,4},{6,5},{7,6},{8,7},{9,8},{10,9},{11,1... | collective-permute-start | bytes 46088 | tf_op jit(solution)/shard_map/ppermute | solution.py:24
  76.3 12.9 %collective-permute-start.6 = (f32[1,1,5,6,128]{4,3,2,1,0:T(8,128)S(1)}, f32[1,1,5,6,128]{4,3,2,1,0:T(8,128)S(1)}, u32[]{:S(2)}, u32[]{:S(2)}) collective-permute-start(f32[1,1,5,6,128]{4,3,2,1,0:T(8,128)S(1)} %get-tuple-element.1103), channel_id=1, source_target_pairs={{1,0},{2,1},{3,2},{4,3},{5,4},{6,5},{7,6},{8,7},{9,8},{10,9},{11,1... | collective-permute-start | bytes 46088 | tf_op jit(solution)/shard_map/ppermute | solution.py:24
  83.3 7.8 %collective-permute-start.7 = (f32[1,1,5,6,128]{4,3,2,1,0:T(8,128)S(1)}, f32[1,1,5,6,128]{4,3,2,1,0:T(8,128)S(1)}, u32[]{:S(2)}, u32[]{:S(2)}) collective-permute-start(f32[1,1,5,6,128]{4,3,2,1,0:T(8,128)S(1)} %get-tuple-element.1103), channel_id=1, source_target_pairs={{0,1},{1,2},{2,3},{3,4},{4,5},{5,6},{6,7},{7,8},{8,9},{9,10},{10,1... | collective-permute-start | bytes 46088 | tf_op jit(solution)/shard_map/ppermute | solution.py:22
  91.2 8.0 %collective-permute-start.8 = (f32[1,3,5,6,128]{4,3,2,1,0:T(8,128)S(1)}, f32[1,3,5,6,128]{4,3,2,1,0:T(8,128)S(1)}, u32[]{:S(2)}, u32[]{:S(2)}) collective-permute-start(f32[1,3,5,6,128]{4,3,2,1,0:T(8,128)S(1)} %pad_maximum_fusion.8), channel_id=1, source_target_pairs={{0,960},{64,0},{128,64},{192,128},{256,192},{320,256},{384,320},{4... | collective-permute-start | bytes 138248 | tf_op jit(solution)/shard_map/ppermute | solution.py:34
  125.4 1.7 collective-permute-start.9
  127.2 9.0 %collective-permute-start.10 = (f32[1,1,5,6,128]{4,3,2,1,0:T(8,128)S(1)}, f32[1,1,5,6,128]{4,3,2,1,0:T(8,128)S(1)}, u32[]{:S(2)}, u32[]{:S(2)}) collective-permute-start(f32[1,1,5,6,128]{4,3,2,1,0:T(8,128)S(1)} %get-tuple-element.1094), channel_id=1, source_target_pairs={{0,1},{1,2},{2,3},{3,4},{4,5},{5,6},{6,7},{7,8},{8,9},{9,10},{10,1... | collective-permute-start | bytes 46088 | tf_op jit(solution)/shard_map/ppermute | solution.py:22
  129.1 7.6 %collective-permute-start.11 = (f32[1,1,5,6,128]{4,3,2,1,0:T(8,128)S(1)}, f32[1,1,5,6,128]{4,3,2,1,0:T(8,128)S(1)}, u32[]{:S(2)}, u32[]{:S(2)}) collective-permute-start(f32[1,1,5,6,128]{4,3,2,1,0:T(8,128)S(1)} %get-tuple-element.1093), channel_id=1, source_target_pairs={{1,0},{2,1},{3,2},{4,3},{5,4},{6,5},{7,6},{8,7},{9,8},{10,9},{11,1... | collective-permute-start | bytes 46088 | tf_op jit(solution)/shard_map/ppermute | solution.py:24

commit v5 on v4

--- a/solution.py
+++ b/solution.py
@@ -207,8 +207,18 @@
     return jnp.repeat(values, 3)[None, :, None]
 
 
+def butterfly_sum(values, axis):
+    count = lax.axis_size(axis)
+    stride = 1
+    while stride < count:
+        partner = lax.ppermute(values, axis, [(i, i ^ stride) for i in range(count)])
+        values = values + partner
+        stride *= 2
+    return values
+
+
 def global_sums(local_values):
-    return lax.psum(local_values, ("gx", "gy"))
+    return butterfly_sum(butterfly_sum(local_values, "gx"), "gy")
 
 
 def per_device(positions, polarity, direct_field, atom_count, pair_list, pair_count):

time: 257 us -> 209 us (0.81)
  the two profiles are of different devices: /device:TPU:1 before, /device:TPU:2 now
where the time goes in v5:
time: 209 us; the launch traced here: 208 us
  starting transfers between devices  75.2 us (36%)
  waiting for transfers between devices  62.2 us (30%)
  other arithmetic  59.2 us (28%)
  local copies, waits for them, and re-layouts  7.72 us (4%)
  between operations  2.15 us (1%)
    reduce_sum x22, other arithmetic, tensor_apply(): jnp.sum(scaled * deltas[member] - coef_three * moments[member], axis=axis...  52.2 us
    ppermute x10, waiting for transfers between devices, butterfly_sum(): lax.ppermute(values, axis, [(i, i ^ stride) for i in range(count)])  42.2 us
    ppermute x4, starting transfers between devices, padded_2(): lax.ppermute(head, axis, [((i + 1) % count, i) for i in range(count)])  37.7 us
    ppermute x10, starting transfers between devices, butterfly_sum(): lax.ppermute(values, axis, [(i, i ^ stride) for i in range(count)])  27.3 us
    ppermute x4, waiting for transfers between devices, from_behind(): return lax.ppermute(value, axis, pairs)  14.1 us
    ppermute x4, starting transfers between devices, padded_2(): lax.ppermute(tail, axis, [(i, (i + 1) % count) for i in range(count)])  7.86 us
  transfers between devices with their start and end apart: 22, of which 17 were waited for; matrix products, arithmetic and copies ran while one was open for 4% of the time, Pallas kernels for 0%

profile of v5, /device:TPU:2, one launch (start us, length us, event | category | flops | bytes accessed | tf_op | source)
XLA Modules:
  0.0 208.3 jit_solution(7452766516314234202)
XLA Ops:
  0.6 0.7 copy.197
  1.3 0.7 fusion.233
  2.1 0.7 copy-done.4
  2.8 15.1 %collective-permute-start = (f32[1,1,5,10,128]{4,3,2,1,0:T(8,128)S(1)}, f32[1,1,5,10,128]{4,3,2,1,0:T(8,128)S(1)}, u32[]{:S(2)}, u32[]{:S(2)}) collective-permute-start(f32[1,1,5,10,128]{4,3,2,1,0:T(8,128)S(1)} %get-tuple-element.1101), channel_id=1, source_target_pairs={{1,0},{2,1},{3,2},{4,3},{5,4},{6,5},{7,6},{8,7},{9,8},{10,9},{11,1... | collective-permute-start | bytes 76808 | tf_op jit(solution)/shard_map/ppermute | solution.py:24
  17.9 1.9 collective-permute-start.1
  19.9 0.7 copy-done.6
  20.6 0.6 copy-done.1
  22.9 0.8 fusion.202
  23.6 1.3 fusion.204
  25.2 1.4 fusion.132
  27.1 2.3 %collective-permute-start.2 = (f32[1,3,5,10,128]{4,3,2,1,0:T(8,128)S(1)}, f32[1,3,5,10,128]{4,3,2,1,0:T(8,128)S(1)}, u32[]{:S(2)}, u32[]{:S(2)}) collective-permute-start(f32[1,3,5,10,128]{4,3,2,1,0:T(8,128)S(1)} %pad_maximum_fusion.4), channel_id=1, source_target_pairs={{0,960},{64,0},{128,64},{192,128},{256,192},{320,256},{384,320},{4... | collective-permute-start | bytes 230408 | tf_op jit(solution)/shard_map/ppermute | solution.py:34
  29.5 2.4 %collective-permute-done.2 = f32[1,3,5,10,128]{4,3,2,1,0:T(8,128)S(1)} collective-permute-done((f32[1,3,5,10,128]{4,3,2,1,0:T(8,128)S(1)}, f32[1,3,5,10,128]{4,3,2,1,0:T(8,128)S(1)}, u32[]{:S(2)}, u32[]{:S(2)}) %collective-permute-start.2) | collective-permute-done | bytes 76832 | tf_op jit(solution)/shard_map/ppermute | solution.py:34
  32.6 26.2 %while.44 = (s32[]{:T(128)}, f32[5,6,128]{2,0,1:T(8,128)S(1)}, f32[4,5,6,128]{3,2,1,0:T(8,128)S(1)}, f32[5,3,5]{2,1,0:T(4,128)S(1)}, f32[5,5,4,128]{3,1,2,0:T(8,...) while((s32[]{:T(128)}, f32[5,6,128]{2,0,1:T(8,128)S(1)}, ...), condition=%wide.region_40.41_spmd.clone, body=%wide.region_25.40_spmd.sunk.clone.sunk | while | flops 25193012 | bytes 1431648 | solution.py:185
  32.9 3.5 %fusion.270 = (f32[13,128]{1,0:T(8,128)S(1)}, f32[13,128]{1,0:T(8,128)S(1)}, f32[13,128]{1,0:T(8,128)S(1)}, f32[13,128]{1,0:T(8,128)S(1)}, f32[13,128]{1,0:T(8,1...) fusion(f32[13,128]{1,0:T(8,128)S(1)} %get-tuple-element.1371, ...), kind=kLoop, calls=%fused_computation.71.clone.1 | loop fusion | flops 16385408 | bytes 173056 | tf_op jit(solution)/shard_map/while/body/eval_jaxpr/reduce_sum | solution.py:46
  36.7 2.2 %fusion.272 = (f32[13,128]{1,0:T(8,128)S(1)}, f32[13,128]{1,0:T(8,128)S(1)}, f32[13,128]{1,0:T(8,128)S(1)}) fusion(f32[13,128]{1,0:T(8,128)S(1)} %get-tuple-element.1404, f32[13,128]{1,0:T(8,128)S(1)} %get-tuple-element.1372, f32[13,128]{1,0:T(8,128)S(1)} %get-tuple-element.1379, f32[13,128]{1,0:T(8,128)S(1)} %get-tuple-element.1405, ...), kind=kLoop, calls=%fused_computation.65.clone.1 | loop fusion | flops 8727680 | bytes 93184 | tf_op jit(solution)/shard_map/while/body/eval_jaxpr/reduce_sum | solution.py:46
  39.5 3.5 %fusion.270 = (f32[13,128]{1,0:T(8,128)S(1)}, f32[13,128]{1,0:T(8,128)S(1)}, f32[13,128]{1,0:T(8,128)S(1)}, f32[13,128]{1,0:T(8,128)S(1)}, f32[13,128]{1,0:T(8,1...) fusion(f32[13,128]{1,0:T(8,128)S(1)} %get-tuple-element.1371, ...), kind=kLoop, calls=%fused_computation.71.clone.1 | loop fusion | flops 16385408 | bytes 173056 | tf_op jit(solution)/shard_map/while/body/eval_jaxpr/reduce_sum | solution.py:46
  43.2 2.2 %fusion.272 = (f32[13,128]{1,0:T(8,128)S(1)}, f32[13,128]{1,0:T(8,128)S(1)}, f32[13,128]{1,0:T(8,128)S(1)}) fusion(f32[13,128]{1,0:T(8,128)S(1)} %get-tuple-element.1404, f32[13,128]{1,0:T(8,128)S(1)} %get-tuple-element.1372, f32[13,128]{1,0:T(8,128)S(1)} %get-tuple-element.1379, f32[13,128]{1,0:T(8,128)S(1)} %get-tuple-element.1405, ...), kind=kLoop, calls=%fused_computation.65.clone.1 | loop fusion | flops 8727680 | bytes 93184 | tf_op jit(solution)/shard_map/while/body/eval_jaxpr/reduce_sum | solution.py:46
  46.0 3.5 %fusion.270 = (f32[13,128]{1,0:T(8,128)S(1)}, f32[13,128]{1,0:T(8,128)S(1)}, f32[13,128]{1,0:T(8,128)S(1)}, f32[13,128]{1,0:T(8,128)S(1)}, f32[13,128]{1,0:T(8,1...) fusion(f32[13,128]{1,0:T(8,128)S(1)} %get-tuple-element.1371, ...), kind=kLoop, calls=%fused_computation.71.clone.1 | loop fusion | flops 16385408 | bytes 173056 | tf_op jit(solution)/shard_map/while/body/eval_jaxpr/reduce_sum | solution.py:46
  49.8 2.2 %fusion.272 = (f32[13,128]{1,0:T(8,128)S(1)}, f32[13,128]{1,0:T(8,128)S(1)}, f32[13,128]{1,0:T(8,128)S(1)}) fusion(f32[13,128]{1,0:T(8,128)S(1)} %get-tuple-element.1404, f32[13,128]{1,0:T(8,128)S(1)} %get-tuple-element.1372, f32[13,128]{1,0:T(8,128)S(1)} %get-tuple-element.1379, f32[13,128]{1,0:T(8,128)S(1)} %get-tuple-element.1405, ...), kind=kLoop, calls=%fused_computation.65.clone.1 | loop fusion | flops 8727680 | bytes 93184 | tf_op jit(solution)/shard_map/while/body/eval_jaxpr/reduce_sum | solution.py:46
  52.6 3.5 %fusion.270 = (f32[13,128]{1,0:T(8,128)S(1)}, f32[13,128]{1,0:T(8,128)S(1)}, f32[13,128]{1,0:T(8,128)S(1)}, f32[13,128]{1,0:T(8,128)S(1)}, f32[13,128]{1,0:T(8,1...) fusion(f32[13,128]{1,0:T(8,128)S(1)} %get-tuple-element.1371, ...), kind=kLoop, calls=%fused_computation.71.clone.1 | loop fusion | flops 16385408 | bytes 173056 | tf_op jit(solution)/shard_map/while/body/eval_jaxpr/reduce_sum | solution.py:46
  56.3 2.2 %fusion.272 = (f32[13,128]{1,0:T(8,128)S(1)}, f32[13,128]{1,0:T(8,128)S(1)}, f32[13,128]{1,0:T(8,128)S(1)}) fusion(f32[13,128]{1,0:T(8,128)S(1)} %get-tuple-element.1404, f32[13,128]{1,0:T(8,128)S(1)} %get-tuple-element.1372, f32[13,128]{1,0:T(8,128)S(1)} %get-tuple-element.1379, f32[13,128]{1,0:T(8,128)S(1)} %get-tuple-element.1405, ...), kind=kLoop, calls=%fused_computation.65.clone.1 | loop fusion | flops 8727680 | bytes 93184 | tf_op jit(solution)/shard_map/while/body/eval_jaxpr/reduce_sum | solution.py:46
  58.8 5.0 %collective-permute-done.3 = f32[1,3,5,6,128]{4,3,2,1,0:T(8,128)S(1)} collective-permute-done((f32[1,3,5,6,128]{4,3,2,1,0:T(8,128)S(1)}, f32[1,3,5,6,128]{4,3,2,1,0:T(8,128)S(1)}, u32[]{:S(2)}, u32[]{:S(2)}) %collective-permute-start.3) | collective-permute-done | bytes 46112 | tf_op jit(solution)/shard_map/ppermute | solution.py:34
  63.8 1.9 collective-permute-start.4
  65.7 8.1 %collective-permute-start.5 = (f32[1,1,5,6,128]{4,3,2,1,0:T(8,128)S(1)}, f32[1,1,5,6,128]{4,3,2,1,0:T(8,128)S(1)}, u32[]{:S(2)}, u32[]{:S(2)}) collective-permute-start(f32[1,1,5,6,128]{4,3,2,1,0:T(8,128)S(1)} %get-tuple-element.1095), channel_id=1, source_target_pairs={{1,0},{2,1},{3,2},{4,3},{5,4},{6,5},{7,6},{8,7},{9,8},{10,9},{11,1... | collective-permute-start | bytes 46088 | tf_op jit(solution)/shard_map/ppermute | solution.py:24
  73.9 1.4 collective-permute-done.5
  75.4 7.2 %collective-permute-start.6 = (f32[1,1,5,6,128]{4,3,2,1,0:T(8,128)S(1)}, f32[1,1,5,6,128]{4,3,2,1,0:T(8,128)S(1)}, u32[]{:S(2)}, u32[]{:S(2)}) collective-permute-start(f32[1,1,5,6,128]{4,3,2,1,0:T(8,128)S(1)} %get-tuple-element.1103), channel_id=1, source_target_pairs={{1,0},{2,1},{3,2},{4,3},{5,4},{6,5},{7,6},{8,7},{9,8},{10,9},{11,1... | collective-permute-start | bytes 46088 | tf_op jit(solution)/shard_map/ppermute | solution.py:24
  82.6 2.1 %collective-permute-start.7 = (f32[1,1,5,6,128]{4,3,2,1,0:T(8,128)S(1)}, f32[1,1,5,6,128]{4,3,2,1,0:T(8,128)S(1)}, u32[]{:S(2)}, u32[]{:S(2)}) collective-permute-start(f32[1,1,5,6,128]{4,3,2,1,0:T(8,128)S(1)} %get-tuple-element.1103), channel_id=1, source_target_pairs={{0,1},{1,2},{2,3},{3,4},{4,5},{5,6},{6,7},{7,8},{8,9},{9,10},{10,1... | collective-permute-start | bytes 46088 | tf_op jit(solution)/shard_map/ppermute | solution.py:22
  84.8 1.3 fusion.212
  86.2 1.4 fusion.136
  88.5 3.4 %collective-permute-done.7 = f32[1,1,5,6,128]{4,3,2,1,0:T(8,128)S(1)} collective-permute-done((f32[1,1,5,6,128]{4,3,2,1,0:T(8,128)S(1)}, f32[1,1,5,6,128]{4,3,2,1,0:T(8,128)S(1)}, u32[]{:S(2)}, u32[]{:S(2)}) %collective-permute-start.7) | collective-permute-done | bytes 15392 | tf_op jit(solution)/shard_map/ppermute | solution.py:22
  92.0 1.8 collective-permute-done.8
  93.9 26.2 %while.45 = (s32[]{:T(128)}, f32[5,6,128]{2,0,1:T(8,128)S(1)}, f32[4,5,6,128]{3,2,1,0:T(8,128)S(1)}, f32[5,3,5]{2,1,0:T(4,128)S(1)}, f32[5,5,4,128]{3,1,2,0:T(8,...) while((s32[]{:T(128)}, f32[5,6,128]{2,0,1:T(8,128)S(1)}, ...), condition=%wide.region_82.83_spmd.clone, body=%wide.region_67.82_spmd.sunk.clone.sunk | while | flops 25193012 | bytes 1431648 | solution.py:185
  94.2 3.5 %fusion.277 = (f32[13,128]{1,0:T(8,128)S(1)}, f32[13,128]{1,0:T(8,128)S(1)}, f32[13,128]{1,0:T(8,128)S(1)}, f32[13,128]{1,0:T(8,128)S(1)}, f32[13,128]{1,0:T(8,1...) fusion(f32[13,128]{1,0:T(8,128)S(1)} %get-tuple-element.1425, ...), kind=kLoop, calls=%fused_computation.207.clone.1 | loop fusion | flops 16385408 | bytes 173056 | tf_op jit(solution)/shard_map/while/body/eval_jaxpr/reduce_sum | solution.py:46
  98.0 2.2 %fusion.279 = (f32[13,128]{1,0:T(8,128)S(1)}, f32[13,128]{1,0:T(8,128)S(1)}, f32[13,128]{1,0:T(8,128)S(1)}) fusion(f32[13,128]{1,0:T(8,128)S(1)} %get-tuple-element.1458, f32[13,128]{1,0:T(8,128)S(1)} %get-tuple-element.1426, f32[13,128]{1,0:T(8,128)S(1)} %get-tuple-element.1433, f32[13,128]{1,0:T(8,128)S(1)} %get-tuple-element.1459, ...), kind=kLoop, calls=%fused_computation.201.clone.1 | loop fusion | flops 8727680 | bytes 93184 | tf_op jit(solution)/shard_map/while/body/eval_jaxpr/reduce_sum | solution.py:46
  100.8 3.5 %fusion.277 = (f32[13,128]{1,0:T(8,128)S(1)}, f32[13,128]{1,0:T(8,128)S(1)}, f32[13,128]{1,0:T(8,128)S(1)}, f32[13,128]{1,0:T(8,128)S(1)}, f32[13,128]{1,0:T(8,1...) fusion(f32[13,128]{1,0:T(8,128)S(1)} %get-tuple-element.1425, ...), kind=kLoop, calls=%fused_computation.207.clone.1 | loop fusion | flops 16385408 | bytes 173056 | tf_op jit(solution)/shard_map/while/body/eval_jaxpr/reduce_sum | solution.py:46
  104.5 2.2 %fusion.279 = (f32[13,128]{1,0:T(8,128)S(1)}, f32[13,128]{1,0:T(8,128)S(1)}, f32[13,128]{1,0:T(8,128)S(1)}) fusion(f32[13,128]{1,0:T(8,128)S(1)} %get-tuple-element.1458, f32[13,128]{1,0:T(8,128)S(1)} %get-tuple-element.1426, f32[13,128]{1,0:T(8,128)S(1)} %get-tuple-element.1433, f32[13,128]{1,0:T(8,128)S(1)} %get-tuple-element.1459, ...), kind=kLoop, calls=%fused_computation.201.clone.1 | loop fusion | flops 8727680 | bytes 93184 | tf_op jit(solution)/shard_map/while/body/eval_jaxpr/reduce_sum | solution.py:46
  107.3 3.5 %fusion.277 = (f32[13,128]{1,0:T(8,128)S(1)}, f32[13,128]{1,0:T(8,128)S(1)}, f32[13,128]{1,0:T(8,128)S(1)}, f32[13,128]{1,0:T(8,128)S(1)}, f32[13,128]{1,0:T(8,1...) fusion(f32[13,128]{1,0:T(8,128)S(1)} %get-tuple-element.1425, ...), kind=kLoop, calls=%fused_computation.207.clone.1 | loop fusion | flops 16385408 | bytes 173056 | tf_op jit(solution)/shard_map/while/body/eval_jaxpr/reduce_sum | solution.py:46
  111.1 2.2 %fusion.279 = (f32[13,128]{1,0:T(8,128)S(1)}, f32[13,128]{1,0:T(8,128)S(1)}, f32[13,128]{1,0:T(8,128)S(1)}) fusion(f32[13,128]{1,0:T(8,128)S(1)} %get-tuple-element.1458, f32[13,128]{1,0:T(8,128)S(1)} %get-tuple-element.1426, f32[13,128]{1,0:T(8,128)S(1)} %get-tuple-element.1433, f32[13,128]{1,0:T(8,128)S(1)} %get-tuple-element.1459, ...), kind=kLoop, calls=%fused_computation.201.clone.1 | loop fusion | flops 8727680 | bytes 93184 | tf_op jit(solution)/shard_map/while/body/eval_jaxpr/reduce_sum | solution.py:46
  113.9 3.5 %fusion.277 = (f32[13,128]{1,0:T(8,128)S(1)}, f32[13,128]{1,0:T(8,128)S(1)}, f32[13,128]{1,0:T(8,128)S(1)}, f32[13,128]{1,0:T(8,128)S(1)}, f32[13,128]{1,0:T(8,1...) fusion(f32[13,128]{1,0:T(8,128)S(1)} %get-tuple-element.1425, ...), kind=kLoop, calls=%fused_computation.207.clone.1 | loop fusion | flops 16385408 | bytes 173056 | tf_op jit(solution)/shard_map/while/body/eval_jaxpr/reduce_sum | solution.py:46
  117.6 2.2 %fusion.279 = (f32[13,128]{1,0:T(8,128)S(1)}, f32[13,128]{1,0:T(8,128)S(1)}, f32[13,128]{1,0:T(8,128)S(1)}) fusion(f32[13,128]{1,0:T(8,128)S(1)} %get-tuple-element.1458, f32[13,128]{1,0:T(8,128)S(1)} %get-tuple-element.1426, f32[13,128]{1,0:T(8,128)S(1)} %get-tuple-element.1433, f32[13,128]{1,0:T(8,128)S(1)} %get-tuple-element.1459, ...), kind=kLoop, calls=%fused_computation.201.clone.1 | loop fusion | flops 8727680 | bytes 93184 | tf_op jit(solution)/shard_map/while/body/eval_jaxpr/reduce_sum | solution.py:46
  120.1 4.9 %collective-permute-done.9 = f32[1,3,5,6,128]{4,3,2,1,0:T(8,128)S(1)} collective-permute-done((f32[1,3,5,6,128]{4,3,2,1,0:T(8,128)S(1)}, f32[1,3,5,6,128]{4,3,2,1,0:T(8,128)S(1)}, u32[]{:S(2)}, u32[]{:S(2)}) %collective-permute-start.9) | collective-permute-done | bytes 46112 | tf_op jit(solution)/shard_map/ppermute | solution.py:34
  125.0 1.9 collective-permute-start.10
  127.0 7.2 %collective-permute-start.11 = (f32[1,1,5,6,128]{4,3,2,1,0:T(8,128)S(1)}, f32[1,1,5,6,128]{4,3,2,1,0:T(8,128)S(1)}, u32[]{:S(2)}, u32[]{:S(2)}) collective-permute-start(f32[1,1,5,6,128]{4,3,2,1,0:T(8,128)S(1)} %get-tuple-element.1093), channel_id=1, source_target_pairs={{1,0},{2,1},{3,2},{4,3},{5,4},{6,5},{7,6},{8,7},{9,8},{10,9},{11,1... | collective-permute-start | bytes 46088 | tf_op jit(solution)/shard_map/ppermute | solution.py:24
  134.6 1.1 collective-permute-done.11
  136.7 1.9 collective-permute-start.12
  138.6 1.1 collective-permute-done.12
  139.7 1.9 collective-permute-start.13
  141.6 3.5 %collective-permute-done.13 = f32[10]{0:T(128)S(1)} collective-permute-done((f32[10]{0:T(128)S(1)}, f32[10]{0:T(128)S(1)}, u32[]{:S(2)}, u32[]{:S(2)}) %collective-permute-start.13) | collective-permute-done | bytes 72 | tf_op jit(solution)/shard_map/ppermute | solution.py:214
  145.2 1.9 collective-permute-start.14
  147.1 4.4 %collective-permute-done.14 = f32[10]{0:T(128)S(1)} collective-permute-done((f32[10]{0:T(128)S(1)}, f32[10]{0:T(128)S(1)}, u32[]{:S(2)}, u32[]{:S(2)}) %collective-permute-start.14) | collective-permute-done | bytes 72 | tf_op jit(solution)/shard_map/ppermute | solution.py:214
  151.5 4.8 %collective-permute-start.15 = (f32[10]{0:T(128)S(1)}, f32[10]{0:T(128)S(1)}, u32[]{:S(2)}, u32[]{:S(2)}) collective-permute-start(f32[10]{0:T(128)S(1)} %add.1160), channel_id=1, source_target_pairs={{0,512},{64,576},{128,640},{192,704},{256,768},{320,832},{384,896}... | collective-permute-start | bytes 128 | tf_op jit(solution)/shard_map/ppermute | solution.py:214
  156.3 4.6 %collective-permute-done.15 = f32[10]{0:T(128)S(1)} collective-permute-done((f32[10]{0:T(128)S(1)}, f32[10]{0:T(128)S(1)}, u32[]{:S(2)}, u32[]{:S(2)}) %collective-permute-start.15) | collective-permute-done | bytes 72 | tf_op jit(solution)/shard_map/ppermute | solution.py:214
  160.8 7.2 %collective-permute-start.16 = (f32[10]{0:T(128)S(1)}, f32[10]{0:T(128)S(1)}, u32[]{:S(2)}, u32[]{:S(2)}) collective-permute-start(f32[10]{0:T(128)S(1)} %add.1161), channel_id=1, source_target_pairs={{0,1},{1,0},{2,3},{3,2},{4,5},{5,4},{6,7},{7,6},{8,9},{9,8},{10,11... | collective-permute-start | bytes 128 | tf_op jit(solution)/shard_map/ppermute | solution.py:214
  168.1 1.5 collective-permute-done.16
  169.6 1.9 collective-permute-start.17
  171.5 4.4 %collective-permute-done.17 = f32[10]{0:T(128)S(1)} collective-permute-done((f32[10]{0:T(128)S(1)}, f32[10]{0:T(128)S(1)}, u32[]{:S(2)}, u32[]{:S(2)}) %collective-permute-start.17) | collective-permute-done | bytes 72 | tf_op jit(solution)/shard_map/ppermute | solution.py:214
  175.9 1.9 collective-permute-start.18
  177.8 7.4 %collective-permute-done.18 = f32[10]{0:T(128)S(1)} collective-permute-done((f32[10]{0:T(128)S(1)}, f32[10]{0:T(128)S(1)}, u32[]{:S(2)}, u32[]{:S(2)}) %collective-permute-start.18) | collective-permute-done | bytes 72 | tf_op jit(solution)/shard_map/ppermute | solution.py:214
  185.2 1.9 collective-permute-start.19
  187.1 3.5 %collective-permute-done.19 = f32[10]{0:T(128)S(1)} collective-permute-done((f32[10]{0:T(128)S(1)}, f32[10]{0:T(128)S(1)}, u32[]{:S(2)}, u32[]{:S(2)}) %collective-permute-start.19) | collective-permute-done | bytes 72 | tf_op jit(solution)/shard_map/ppermute | solution.py:214
  190.7 1.9 collective-permute-start.20
  192.6 4.4 %collective-permute-done.20 = f32[10]{0:T(128)S(1)} collective-permute-done((f32[10]{0:T(128)S(1)}, f32[10]{0:T(128)S(1)}, u32[]{:S(2)}, u32[]{:S(2)}) %collective-permute-start.20) | collective-permute-done | bytes 72 | tf_op jit(solution)/shard_map/ppermute | solution.py:214
  197.0 2.0 collective-permute-start.21
  198.9 7.4 %collective-permute-done.21 = f32[10]{0:T(128)S(1)} collective-permute-done((f32[10]{0:T(128)S(1)}, f32[10]{0:T(128)S(1)}, u32[]{:S(2)}, u32[]{:S(2)}) %collective-permute-start.21) | collective-permute-done | bytes 72 | tf_op jit(solution)/shard_map/ppermute | solution.py:214
  (455 shorter events, 12.1 us)
Async XLA Ops:
  0.6 1.4 copy-start.5
  0.6 1.4 copy-start
  2.1 0.7 copy-start.4
  2.8 24.3 %collective-permute-start = (f32[1,1,5,10,128]{4,3,2,1,0:T(8,128)S(1)}, f32[1,1,5,10,128]{4,3,2,1,0:T(8,128)S(1)}, u32[]{:S(2)}, u32[]{:S(2)}) collective-permute-start(f32[1,1,5,10,128]{4,3,2,1,0:T(8,128)S(1)} %get-tuple-element.1101), channel_id=1, source_target_pairs={{1,0},{2,1},{3,2},{4,3},{5,4},{6,5},{7,6},{8,7},{9,8},{10,9},{11,1... | collective-permute-start | bytes 76808 | tf_op jit(solution)/shard_map/ppermute | solution.py:24
  17.9 9.2 %collective-permute-start.1 = (f32[1,1,5,10,128]{4,3,2,1,0:T(8,128)S(1)}, f32[1,1,5,10,128]{4,3,2,1,0:T(8,128)S(1)}, u32[]{:S(2)}, u32[]{:S(2)}) collective-permute-start(f32[1,1,5,10,128]{4,3,2,1,0:T(8,128)S(1)} %get-tuple-element.1101), channel_id=1, source_target_pairs={{0,1},{1,2},{2,3},{3,4},{4,5},{5,6},{6,7},{7,8},{8,9},{9,10},{10,1... | collective-permute-start | bytes 76808 | tf_op jit(solution)/shard_map/ppermute | solution.py:22
  19.9 0.7 copy-start.6
  20.5 0.7 copy-start.1
  20.6 0.7 copy-start.2
  27.1 4.7 %collective-permute-start.2 = (f32[1,3,5,10,128]{4,3,2,1,0:T(8,128)S(1)}, f32[1,3,5,10,128]{4,3,2,1,0:T(8,128)S(1)}, u32[]{:S(2)}, u32[]{:S(2)}) collective-permute-start(f32[1,3,5,10,128]{4,3,2,1,0:T(8,128)S(1)} %pad_maximum_fusion.4), channel_id=1, source_target_pairs={{0,960},{64,0},{128,64},{192,128},{256,192},{320,256},{384,320},{4... | collective-permute-start | bytes 230408 | tf_op jit(solution)/shard_map/ppermute | solution.py:34
  31.9 0.7 copy-start.3
  58.8 5.0 %collective-permute-start.3 = (f32[1,3,5,6,128]{4,3,2,1,0:T(8,128)S(1)}, f32[1,3,5,6,128]{4,3,2,1,0:T(8,128)S(1)}, u32[]{:S(2)}, u32[]{:S(2)}) collective-permute-start(f32[1,3,5,6,128]{4,3,2,1,0:T(8,128)S(1)} %slice_bitcast_fusion.47), channel_id=1, source_target_pairs={{0,64},{64,128},{128,192},{192,256},{256,320},{320,384},{384,448},... | collective-permute-start | bytes 138248 | tf_op jit(solution)/shard_map/ppermute | solution.py:34
  63.8 10.0 %collective-permute-start.4 = (f32[1,1,5,6,128]{4,3,2,1,0:T(8,128)S(1)}, f32[1,1,5,6,128]{4,3,2,1,0:T(8,128)S(1)}, u32[]{:S(2)}, u32[]{:S(2)}) collective-permute-start(f32[1,1,5,6,128]{4,3,2,1,0:T(8,128)S(1)} %get-tuple-element.1096), channel_id=1, source_target_pairs={{0,1},{1,2},{2,3},{3,4},{4,5},{5,6},{6,7},{7,8},{8,9},{9,10},{10,1... | collective-permute-start | bytes 46088 | tf_op jit(solution)/shard_map/ppermute | solution.py:22
  65.7 9.6 %collective-permute-start.5 = (f32[1,1,5,6,128]{4,3,2,1,0:T(8,128)S(1)}, f32[1,1,5,6,128]{4,3,2,1,0:T(8,128)S(1)}, u32[]{:S(2)}, u32[]{:S(2)}) collective-permute-start(f32[1,1,5,6,128]{4,3,2,1,0:T(8,128)S(1)} %get-tuple-element.1095), channel_id=1, source_target_pairs={{1,0},{2,1},{3,2},{4,3},{5,4},{6,5},{7,6},{8,7},{9,8},{10,9},{11,1... | collective-permute-start | bytes 46088 | tf_op jit(solution)/shard_map/ppermute | solution.py:24
  75.4 13.1 %collective-permute-start.6 = (f32[1,1,5,6,128]{4,3,2,1,0:T(8,128)S(1)}, f32[1,1,5,6,128]{4,3,2,1,0:T(8,128)S(1)}, u32[]{:S(2)}, u32[]{:S(2)}) collective-permute-start(f32[1,1,5,6,128]{4,3,2,1,0:T(8,128)S(1)} %get-tuple-element.1103), channel_id=1, source_target_pairs={{1,0},{2,1},{3,2},{4,3},{5,4},{6,5},{7,6},{8,7},{9,8},{10,9},{11,1... | collective-permute-start | bytes 46088 | tf_op jit(solution)/shard_map/ppermute | solution.py:24
  82.6 9.3 %collective-permute-start.7 = (f32[1,1,5,6,128]{4,3,2,1,0:T(8,128)S(1)}, f32[1,1,5,6,128]{4,3,2,1,0:T(8,128)S(1)}, u32[]{:S(2)}, u32[]{:S(2)}) collective-permute-start(f32[1,1,5,6,128]{4,3,2,1,0:T(8,128)S(1)} %get-tuple-element.1103), channel_id=1, source_target_pairs={{0,1},{1,2},{2,3},{3,4},{4,5},{5,6},{6,7},{7,8},{8,9},{9,10},{10,1... | collective-permute-start | bytes 46088 | tf_op jit(solution)/shard_map/ppermute | solution.py:22
  91.9 1.9 collective-permute-start.8
  120.1 4.9 %collective-permute-start.9 = (f32[1,3,5,6,128]{4,3,2,1,0:T(8,128)S(1)}, f32[1,3,5,6,128]{4,3,2,1,0:T(8,128)S(1)}, u32[]{:S(2)}, u32[]{:S(2)}) collective-permute-start(f32[1,3,5,6,128]{4,3,2,1,0:T(8,128)S(1)} %slice_bitcast_fusion.46), channel_id=1, source_target_pairs={{0,64},{64,128},{128,192},{192,256},{256,320},{320,384},{384,448},... | collective-permute-start | bytes 138248 | tf_op jit(solution)/shard_map/ppermute | solution.py:34
  125.0 9.5 %collective-permute-start.10 = (f32[1,1,5,6,128]{4,3,2,1,0:T(8,128)S(1)}, f32[1,1,5,6,128]{4,3,2,1,0:T(8,128)S(1)}, u32[]{:S(2)}, u32[]{:S(2)}) collective-permute-start(f32[1,1,5,6,128]{4,3,2,1,0:T(8,128)S(1)} %get-tuple-element.1094), channel_id=1, source_target_pairs={{0,1},{1,2},{2,3},{3,4},{4,5},{5,6},{6,7},{7,8},{8,9},{9,10},{10,1... | collective-permute-start | bytes 46088 | tf_op jit(solution)/shard_map/ppermute | solution.py:22
  127.0 8.7 %collective-permute-start.11 = (f32[1,1,5,6,128]{4,3,2,1,0:T(8,128)S(1)}, f32[1,1,5,6,128]{4,3,2,1,0:T(8,128)S(1)}, u32[]{:S(2)}, u32[]{:S(2)}) collective-permute-start(f32[1,1,5,6,128]{4,3,2,1,0:T(8,128)S(1)} %get-tuple-element.1093), channel_id=1, source_target_pairs={{1,0},{2,1},{3,2},{4,3},{5,4},{6,5},{7,6},{8,7},{9,8},{10,9},{11,1... | collective-permute-start | bytes 46088 | tf_op jit(solution)/shard_map/ppermute | solution.py:24
  136.7 3.0 %collective-permute-start.12 = (f32[10]{0:T(128)S(1)}, f32[10]{0:T(128)S(1)}, u32[]{:S(2)}, u32[]{:S(2)}) collective-permute-start(f32[10]{0:T(128)S(1)} %concatenate.296), channel_id=1, source_target_pairs={{0,64},{64,0},{128,192},{192,128},{256,320},{320,256},{384,448},{4... | collective-permute-start | bytes 128 | tf_op jit(solution)/shard_map/ppermute | solution.py:214
  139.7 5.4 %collective-permute-start.13 = (f32[10]{0:T(128)S(1)}, f32[10]{0:T(128)S(1)}, u32[]{:S(2)}, u32[]{:S(2)}) collective-permute-start(f32[10]{0:T(128)S(1)} %add.1158), channel_id=1, source_target_pairs={{0,128},{64,192},{128,0},{192,64},{256,384},{320,448},{384,256},{4... | collective-permute-start | bytes 128 | tf_op jit(solution)/shard_map/ppermute | solution.py:214
  145.2 6.3 %collective-permute-start.14 = (f32[10]{0:T(128)S(1)}, f32[10]{0:T(128)S(1)}, u32[]{:S(2)}, u32[]{:S(2)}) collective-permute-start(f32[10]{0:T(128)S(1)} %add.1159), channel_id=1, source_target_pairs={{0,256},{64,320},{128,384},{192,448},{256,0},{320,64},{384,128},{4... | collective-permute-start | bytes 128 | tf_op jit(solution)/shard_map/ppermute | solution.py:214
  151.5 9.3 %collective-permute-start.15 = (f32[10]{0:T(128)S(1)}, f32[10]{0:T(128)S(1)}, u32[]{:S(2)}, u32[]{:S(2)}) collective-permute-start(f32[10]{0:T(128)S(1)} %add.1160), channel_id=1, source_target_pairs={{0,512},{64,576},{128,640},{192,704},{256,768},{320,832},{384,896}... | collective-permute-start | bytes 128 | tf_op jit(solution)/shard_map/ppermute | solution.py:214
  160.8 8.7 %collective-permute-start.16 = (f32[10]{0:T(128)S(1)}, f32[10]{0:T(128)S(1)}, u32[]{:S(2)}, u32[]{:S(2)}) collective-permute-start(f32[10]{0:T(128)S(1)} %add.1161), channel_id=1, source_target_pairs={{0,1},{1,0},{2,3},{3,2},{4,5},{5,4},{6,7},{7,6},{8,9},{9,8},{10,11... | collective-permute-start | bytes 128 | tf_op jit(solution)/shard_map/ppermute | solution.py:214
  169.6 6.3 %collective-permute-start.17 = (f32[10]{0:T(128)S(1)}, f32[10]{0:T(128)S(1)}, u32[]{:S(2)}, u32[]{:S(2)}) collective-permute-start(f32[10]{0:T(128)S(1)} %add.1162), channel_id=1, source_target_pairs={{0,2},{1,3},{2,0},{3,1},{4,6},{5,7},{6,4},{7,5},{8,10},{9,11},{10,... | collective-permute-start | bytes 128 | tf_op jit(solution)/shard_map/ppermute | solution.py:214
  175.9 9.3 %collective-permute-start.18 = (f32[10]{0:T(128)S(1)}, f32[10]{0:T(128)S(1)}, u32[]{:S(2)}, u32[]{:S(2)}) collective-permute-start(f32[10]{0:T(128)S(1)} %add.1163), channel_id=1, source_target_pairs={{0,4},{1,5},{2,6},{3,7},{4,0},{5,1},{6,2},{7,3},{8,12},{9,13},{10,... | collective-permute-start | bytes 128 | tf_op jit(solution)/shard_map/ppermute | solution.py:214
  185.2 5.4 %collective-permute-start.19 = (f32[10]{0:T(128)S(1)}, f32[10]{0:T(128)S(1)}, u32[]{:S(2)}, u32[]{:S(2)}) collective-permute-start(f32[10]{0:T(128)S(1)} %add.1164), channel_id=1, source_target_pairs={{0,8},{1,9},{2,10},{3,11},{4,12},{5,13},{6,14},{7,15},{8,0},{9,1},... | collective-permute-start | bytes 128 | tf_op jit(solution)/shard_map/ppermute | solution.py:214
  190.7 6.3 %collective-permute-start.20 = (f32[10]{0:T(128)S(1)}, f32[10]{0:T(128)S(1)}, u32[]{:S(2)}, u32[]{:S(2)}) collective-permute-start(f32[10]{0:T(128)S(1)} %add.1165), channel_id=1, source_target_pairs={{0,16},{1,17},{2,18},{3,19},{4,20},{5,21},{6,22},{7,23},{8,24},{9,... | collective-permute-start | bytes 128 | tf_op jit(solution)/shard_map/ppermute | solution.py:214
  197.0 9.3 %collective-permute-start.21 = (f32[10]{0:T(128)S(1)}, f32[10]{0:T(128)S(1)}, u32[]{:S(2)}, u32[]{:S(2)}) collective-permute-start(f32[10]{0:T(128)S(1)} %add.1166), channel_id=1, source_target_pairs={{0,32},{1,33},{2,34},{3,35},{4,36},{5,37},{6,38},{7,39},{8,40},{9,... | collective-permute-start | bytes 128 | tf_op jit(solution)/shard_map/ppermute | solution.py:214

commit v6 on v5

--- a/solution.py
+++ b/solution.py
@@ -185,17 +185,37 @@
     return lax.fori_loop(1, 5, one_slot, (own_total, other_acc))
 
 
+slot_moves = ((0, 1), (1, -1), (1, 0), (1, 1))
+
+
+def shifted_from(value, move_x, move_y):
+    count_x = lax.axis_size("gx")
+    count_y = lax.axis_size("gy")
+    if move_x == 0:
+        pairs = [(source, (source - move_y) % count_y) for source in range(count_y)]
+        return lax.ppermute(value, "gy", pairs)
+    pairs = [
+        (
+            source_x * count_y + source_y,
+            ((source_x - move_x) % count_x) * count_y + (source_y - move_y) % count_y,
+        )
+        for source_x in range(count_x)
+        for source_y in range(count_y)
+    ]
+    return lax.ppermute(value, ("gx", "gy"), pairs)
+
+
 def neighbours(block_data):
-    column = padded_2(block_data[None, None], (("gy", 1),), 1)
-    across = from_behind(column, "gx", -1)
-    return jnp.concatenate([block_data[None], column[0, 2:3], across[0]], axis=0)
+    gathered = [shifted_from(block_data, move_x, move_y) for move_x, move_y in slot_moves]
+    return jnp.stack([block_data] + gathered, axis=0)
 
 
 def send_back(partials):
-    received = from_behind(partials[None, 1:4], "gx", 1)
-    paired = jnp.stack([received[0, 0], received[0, 2] + partials[0]], axis=0)[None]
-    column = padded_2(paired, (("gy", 1),), 1)
-    return column[0, 0] + column[0, 3] + received[0, 1]
+    returned = [
+        shifted_from(partials[index], -move_x, -move_y)
+        for index, (move_x, move_y) in enumerate(slot_moves)
+    ]
+    return (returned[0] + returned[1]) + (returned[2] + returned[3])
 
 
 def set_sums(first_vec, second_vec):

time: 209 us -> 221 us (1.057)
  starting transfers between devices: 75.2 us -> 89.4 us
  waiting for transfers between devices: 62.2 us -> 59.6 us
    ppermute x12 -> x16, starting transfers between devices: 47.9 us -> 62.5 us  [the longest x12 36 us: shifted_from(): return lax.ppermute(value, ('gx', 'gy'), pairs)]
    ppermute x12 -> x16, waiting for transfers between devices: 20 us -> 16.7 us  [the longest x12 16.7 us: shifted_from(): return lax.ppermute(value, ('gx', 'gy'), pairs)]
  transfers between devices with their start and end apart: 22 -> 26, of which waited for: 17 -> 14; matrix products, arithmetic and copies ran while one was open for 4% -> 4% of each run, Pallas kernels for 0% -> 0%
where the time goes in v6:
time: 221 us; the launch traced here: 220 us
  starting transfers between devices  89.4 us (40%)
  waiting for transfers between devices  59.6 us (27%)
  other arithmetic  59.1 us (27%)
  local copies, waits for them, and re-layouts  7.8 us (4%)
  between operations  2.31 us (1%)
    reduce_sum x22, other arithmetic, tensor_apply(): jnp.sum(scaled * deltas[member] - coef_three * moments[member], axis=axis...  52.1 us
    ppermute x10, waiting for transfers between devices, butterfly_sum(): lax.ppermute(values, axis, [(i, i ^ stride) for i in range(count)])  42.9 us
    ppermute x12, starting transfers between devices, shifted_from(): return lax.ppermute(value, ('gx', 'gy'), pairs)  36 us
    ppermute x10, starting transfers between devices, butterfly_sum(): lax.ppermute(values, axis, [(i, i ^ stride) for i in range(count)])  26.8 us
    ppermute x4, starting transfers between devices, shifted_from(): return lax.ppermute(value, 'gy', pairs)  26.5 us
    ppermute x12, waiting for transfers between devices, shifted_from(): return lax.ppermute(value, ('gx', 'gy'), pairs)  16.7 us
  transfers between devices with their start and end apart: 26, of which 14 were waited for; matrix products, arithmetic and copies ran while one was open for 4% of the time, Pallas kernels for 0%

profile of v6, /device:TPU:2, one launch (start us, length us, event | category | flops | bytes accessed | tf_op | source)
XLA Modules:
  0.0 220.0 jit_solution(14742007803627273340)
XLA Ops:
  0.6 0.7 copy.213
  1.3 0.7 fusion.225
  2.1 0.7 copy-done.4
  2.8 15.1 %collective-permute-start = (f32[5,10,128]{2,1,0:T(8,128)S(1)}, f32[5,10,128]{2,1,0:T(8,128)S(1)}, u32[]{:S(2)}, u32[]{:S(2)}) collective-permute-start(f32[5,10,128]{2,1,0:T(8,128)S(1)} %get-tuple-element.1105), channel_id=1, source_target_pairs={{0,63},{1,0},{2,1},{3,2},{4,3},{5,4},{6,5},{7,6},{8,7},{9,8},{10,9... | collective-permute-start | bytes 76808 | tf_op jit(solution)/shard_map/ppermute | solution.py:196
  17.9 1.9 collective-permute-start.1
  19.9 10.8 %collective-permute-start.3 = (f32[5,10,128]{2,1,0:T(8,128)S(1)}, f32[5,10,128]{2,1,0:T(8,128)S(1)}, u32[]{:S(2)}, u32[]{:S(2)}) collective-permute-start(f32[5,10,128]{2,1,0:T(8,128)S(1)} %get-tuple-element.1105), channel_id=1, source_target_pairs={{0,1023},{1,960},{2,961},{3,962},{4,963},{5,964},{6,965},{7,966},{... | collective-permute-start | bytes 76808 | tf_op jit(solution)/shard_map/ppermute | solution.py:205
  31.7 0.7 copy-done.6
  33.8 1.4 fusion.132
  35.4 1.3 fusion.204
  36.7 0.8 fusion.202
  38.1 0.6 copy-done.3
  38.8 26.2 %while.44 = (s32[]{:T(128)}, f32[5,6,128]{2,0,1:T(8,128)S(1)}, f32[4,5,6,128]{3,2,1,0:T(8,128)S(1)}, f32[5,3,5]{2,1,0:T(4,128)S(1)}, f32[5,5,4,128]{3,1,2,0:T(8,...) while((s32[]{:T(128)}, f32[5,6,128]{2,0,1:T(8,128)S(1)}, ...), condition=%wide.region_40.41_spmd.clone, body=%wide.region_25.40_spmd.sunk.clone.sunk | while | flops 25193012 | bytes 1431648 | solution.py:185
  39.1 2.1 fusion.261
  41.3 3.5 %fusion.259 = (f32[13,128]{1,0:T(8,128)S(1)}, f32[13,128]{1,0:T(8,128)S(1)}, f32[13,128]{1,0:T(8,128)S(1)}, f32[13,128]{1,0:T(8,128)S(1)}, f32[13,128]{1,0:T(8,1...) fusion(f32[13,128]{1,0:T(8,128)S(1)} %get-tuple-element.1373, ...), kind=kLoop, calls=%fused_computation.71.clone.1 | loop fusion | flops 16385408 | bytes 173056 | tf_op jit(solution)/shard_map/while/body/eval_jaxpr/reduce_sum | solution.py:46
  45.6 2.1 fusion.261
  47.8 3.5 %fusion.259 = (f32[13,128]{1,0:T(8,128)S(1)}, f32[13,128]{1,0:T(8,128)S(1)}, f32[13,128]{1,0:T(8,128)S(1)}, f32[13,128]{1,0:T(8,128)S(1)}, f32[13,128]{1,0:T(8,1...) fusion(f32[13,128]{1,0:T(8,128)S(1)} %get-tuple-element.1373, ...), kind=kLoop, calls=%fused_computation.71.clone.1 | loop fusion | flops 16385408 | bytes 173056 | tf_op jit(solution)/shard_map/while/body/eval_jaxpr/reduce_sum | solution.py:46
  52.2 2.1 fusion.261
  54.4 3.5 %fusion.259 = (f32[13,128]{1,0:T(8,128)S(1)}, f32[13,128]{1,0:T(8,128)S(1)}, f32[13,128]{1,0:T(8,128)S(1)}, f32[13,128]{1,0:T(8,128)S(1)}, f32[13,128]{1,0:T(8,1...) fusion(f32[13,128]{1,0:T(8,128)S(1)} %get-tuple-element.1373, ...), kind=kLoop, calls=%fused_computation.71.clone.1 | loop fusion | flops 16385408 | bytes 173056 | tf_op jit(solution)/shard_map/while/body/eval_jaxpr/reduce_sum | solution.py:46
  58.7 2.1 fusion.261
  60.9 3.5 %fusion.259 = (f32[13,128]{1,0:T(8,128)S(1)}, f32[13,128]{1,0:T(8,128)S(1)}, f32[13,128]{1,0:T(8,128)S(1)}, f32[13,128]{1,0:T(8,128)S(1)}, f32[13,128]{1,0:T(8,1...) fusion(f32[13,128]{1,0:T(8,128)S(1)} %get-tuple-element.1373, ...), kind=kLoop, calls=%fused_computation.71.clone.1 | loop fusion | flops 16385408 | bytes 173056 | tf_op jit(solution)/shard_map/while/body/eval_jaxpr/reduce_sum | solution.py:46
  64.9 1.9 collective-permute-start.4
  66.9 7.1 %collective-permute-start.5 = (f32[5,6,128]{2,1,0:T(8,128)S(1)}, f32[5,6,128]{2,1,0:T(8,128)S(1)}, u32[]{:S(2)}, u32[]{:S(2)}) collective-permute-start(f32[5,6,128]{2,1,0:T(8,128)S(1)} %get-tuple-element.1095), channel_id=1, source_target_pairs={{0,127},{1,64},{2,65},{3,66},{4,67},{5,68},{6,69},{7,70},{8,71},{9... | collective-permute-start | bytes 46088 | tf_op jit(solution)/shard_map/ppermute | solution.py:205
  74.3 1.9 collective-permute-start.7
  76.2 2.2 collective-permute-done.6
  78.4 6.4 %collective-permute-done.7 = f32[5,6,128]{2,1,0:T(8,128)S(1)} collective-permute-done((f32[5,6,128]{2,1,0:T(8,128)S(1)}, f32[5,6,128]{2,1,0:T(8,128)S(1)}, u32[]{:S(2)}, u32[]{:S(2)}) %collective-permute-start.7) | collective-permute-done | bytes 15392 | tf_op jit(solution)/shard_map/ppermute | solution.py:205
  84.9 7.2 %collective-permute-start.8 = (f32[5,6,128]{2,1,0:T(8,128)S(1)}, f32[5,6,128]{2,1,0:T(8,128)S(1)}, u32[]{:S(2)}, u32[]{:S(2)}) collective-permute-start(f32[5,6,128]{2,1,0:T(8,128)S(1)} %broadcast_multiply_fusion.5), channel_id=1, source_target_pairs={{0,63},{1,0},{2,1},{3,2},{4,3},{5,4},{6,5},{7,6},{8,7},{9,8},{10,9... | collective-permute-start | bytes 46088 | tf_op jit(solution)/shard_map/ppermute | solution.py:196
  92.1 1.9 collective-permute-start.9
  94.4 4.2 %collective-permute-start.11 = (f32[5,6,128]{2,1,0:T(8,128)S(1)}, f32[5,6,128]{2,1,0:T(8,128)S(1)}, u32[]{:S(2)}, u32[]{:S(2)}) collective-permute-start(f32[5,6,128]{2,1,0:T(8,128)S(1)} %broadcast_multiply_fusion.5), channel_id=1, source_target_pairs={{0,1023},{1,960},{2,961},{3,962},{4,963},{5,964},{6,965},{7,966},{... | collective-permute-start | bytes 46088 | tf_op jit(solution)/shard_map/ppermute | solution.py:205
  98.7 1.4 fusion.136
  100.1 1.3 fusion.212
  102.6 26.2 %while.45 = (s32[]{:T(128)}, f32[5,6,128]{2,0,1:T(8,128)S(1)}, f32[4,5,6,128]{3,2,1,0:T(8,128)S(1)}, f32[5,3,5]{2,1,0:T(4,128)S(1)}, f32[5,5,4,128]{3,1,2,0:T(8,...) while((s32[]{:T(128)}, f32[5,6,128]{2,0,1:T(8,128)S(1)}, ...), condition=%wide.region_82.83_spmd.clone, body=%wide.region_67.82_spmd.sunk.clone.sunk | while | flops 25193012 | bytes 1431648 | solution.py:185
  102.9 2.1 fusion.268
  105.1 3.5 %fusion.266 = (f32[13,128]{1,0:T(8,128)S(1)}, f32[13,128]{1,0:T(8,128)S(1)}, f32[13,128]{1,0:T(8,128)S(1)}, f32[13,128]{1,0:T(8,128)S(1)}, f32[13,128]{1,0:T(8,1...) fusion(f32[13,128]{1,0:T(8,128)S(1)} %get-tuple-element.1427, ...), kind=kLoop, calls=%fused_computation.207.clone.1 | loop fusion | flops 16385408 | bytes 173056 | tf_op jit(solution)/shard_map/while/body/eval_jaxpr/reduce_sum | solution.py:46
  109.5 2.1 fusion.268
  111.7 3.5 %fusion.266 = (f32[13,128]{1,0:T(8,128)S(1)}, f32[13,128]{1,0:T(8,128)S(1)}, f32[13,128]{1,0:T(8,128)S(1)}, f32[13,128]{1,0:T(8,128)S(1)}, f32[13,128]{1,0:T(8,1...) fusion(f32[13,128]{1,0:T(8,128)S(1)} %get-tuple-element.1427, ...), kind=kLoop, calls=%fused_computation.207.clone.1 | loop fusion | flops 16385408 | bytes 173056 | tf_op jit(solution)/shard_map/while/body/eval_jaxpr/reduce_sum | solution.py:46
  116.0 2.1 fusion.268
  118.2 3.5 %fusion.266 = (f32[13,128]{1,0:T(8,128)S(1)}, f32[13,128]{1,0:T(8,128)S(1)}, f32[13,128]{1,0:T(8,128)S(1)}, f32[13,128]{1,0:T(8,128)S(1)}, f32[13,128]{1,0:T(8,1...) fusion(f32[13,128]{1,0:T(8,128)S(1)} %get-tuple-element.1427, ...), kind=kLoop, calls=%fused_computation.207.clone.1 | loop fusion | flops 16385408 | bytes 173056 | tf_op jit(solution)/shard_map/while/body/eval_jaxpr/reduce_sum | solution.py:46
  122.6 2.1 fusion.268
  124.8 3.5 %fusion.266 = (f32[13,128]{1,0:T(8,128)S(1)}, f32[13,128]{1,0:T(8,128)S(1)}, f32[13,128]{1,0:T(8,128)S(1)}, f32[13,128]{1,0:T(8,128)S(1)}, f32[13,128]{1,0:T(8,1...) fusion(f32[13,128]{1,0:T(8,128)S(1)} %get-tuple-element.1427, ...), kind=kLoop, calls=%fused_computation.207.clone.1 | loop fusion | flops 16385408 | bytes 173056 | tf_op jit(solution)/shard_map/while/body/eval_jaxpr/reduce_sum | solution.py:46
  128.8 2.3 %collective-permute-start.12 = (f32[5,6,128]{2,1,0:T(8,128)S(1)}, f32[5,6,128]{2,1,0:T(8,128)S(1)}, u32[]{:S(2)}, u32[]{:S(2)}) collective-permute-start(f32[5,6,128]{2,1,0:T(8,128)S(1)} %get-tuple-element.1093), channel_id=1, source_target_pairs={{0,1},{1,2},{2,3},{3,4},{4,5},{5,6},{6,7},{7,8},{8,9},{9,10},{10,1... | collective-permute-start | bytes 46088 | tf_op jit(solution)/shard_map/ppermute | solution.py:196
  131.1 5.1 %collective-permute-start.13 = (f32[5,6,128]{2,1,0:T(8,128)S(1)}, f32[5,6,128]{2,1,0:T(8,128)S(1)}, u32[]{:S(2)}, u32[]{:S(2)}) collective-permute-start(f32[5,6,128]{2,1,0:T(8,128)S(1)} %get-tuple-element.1091), channel_id=1, source_target_pairs={{0,127},{1,64},{2,65},{3,66},{4,67},{5,68},{6,69},{7,70},{8,71},{9... | collective-permute-start | bytes 46088 | tf_op jit(solution)/shard_map/ppermute | solution.py:205
  136.7 1.9 collective-permute-start.15
  139.0 1.7 collective-permute-done.14
  140.7 6.5 %collective-permute-done.15 = f32[5,6,128]{2,1,0:T(8,128)S(1)} collective-permute-done((f32[5,6,128]{2,1,0:T(8,128)S(1)}, f32[5,6,128]{2,1,0:T(8,128)S(1)}, u32[]{:S(2)}, u32[]{:S(2)}) %collective-permute-start.15) | collective-permute-done | bytes 15392 | tf_op jit(solution)/shard_map/ppermute | solution.py:205
  148.2 1.9 collective-permute-start.16
  150.1 1.1 collective-permute-done.16
  151.2 1.9 collective-permute-start.17
  153.1 3.5 %collective-permute-done.17 = f32[10]{0:T(128)S(1)} collective-permute-done((f32[10]{0:T(128)S(1)}, f32[10]{0:T(128)S(1)}, u32[]{:S(2)}, u32[]{:S(2)}) %collective-permute-start.17) | collective-permute-done | bytes 72 | tf_op jit(solution)/shard_map/ppermute | solution.py:234
  156.6 1.9 collective-permute-start.18
  158.5 4.4 %collective-permute-done.18 = f32[10]{0:T(128)S(1)} collective-permute-done((f32[10]{0:T(128)S(1)}, f32[10]{0:T(128)S(1)}, u32[]{:S(2)}, u32[]{:S(2)}) %collective-permute-start.18) | collective-permute-done | bytes 72 | tf_op jit(solution)/shard_map/ppermute | solution.py:234
  162.9 4.1 %collective-permute-start.19 = (f32[10]{0:T(128)S(1)}, f32[10]{0:T(128)S(1)}, u32[]{:S(2)}, u32[]{:S(2)}) collective-permute-start(f32[10]{0:T(128)S(1)} %add.1148), channel_id=1, source_target_pairs={{0,512},{64,576},{128,640},{192,704},{256,768},{320,832},{384,896}... | collective-permute-start | bytes 128 | tf_op jit(solution)/shard_map/ppermute | solution.py:234
  167.0 5.2 %collective-permute-done.19 = f32[10]{0:T(128)S(1)} collective-permute-done((f32[10]{0:T(128)S(1)}, f32[10]{0:T(128)S(1)}, u32[]{:S(2)}, u32[]{:S(2)}) %collective-permute-start.19) | collective-permute-done | bytes 72 | tf_op jit(solution)/shard_map/ppermute | solution.py:234
  172.3 7.5 %collective-permute-start.20 = (f32[10]{0:T(128)S(1)}, f32[10]{0:T(128)S(1)}, u32[]{:S(2)}, u32[]{:S(2)}) collective-permute-start(f32[10]{0:T(128)S(1)} %add.1149), channel_id=1, source_target_pairs={{0,1},{1,0},{2,3},{3,2},{4,5},{5,4},{6,7},{7,6},{8,9},{9,8},{10,11... | collective-permute-start | bytes 128 | tf_op jit(solution)/shard_map/ppermute | solution.py:234
  179.7 1.5 collective-permute-done.20
  181.2 1.9 collective-permute-start.21
  183.2 4.4 %collective-permute-done.21 = f32[10]{0:T(128)S(1)} collective-permute-done((f32[10]{0:T(128)S(1)}, f32[10]{0:T(128)S(1)}, u32[]{:S(2)}, u32[]{:S(2)}) %collective-permute-start.21) | collective-permute-done | bytes 72 | tf_op jit(solution)/shard_map/ppermute | solution.py:234
  187.6 1.9 collective-permute-start.22
  189.5 7.4 %collective-permute-done.22 = f32[10]{0:T(128)S(1)} collective-permute-done((f32[10]{0:T(128)S(1)}, f32[10]{0:T(128)S(1)}, u32[]{:S(2)}, u32[]{:S(2)}) %collective-permute-start.22) | collective-permute-done | bytes 72 | tf_op jit(solution)/shard_map/ppermute | solution.py:234
  196.9 1.9 collective-permute-start.23
  198.8 3.5 %collective-permute-done.23 = f32[10]{0:T(128)S(1)} collective-permute-done((f32[10]{0:T(128)S(1)}, f32[10]{0:T(128)S(1)}, u32[]{:S(2)}, u32[]{:S(2)}) %collective-permute-start.23) | collective-permute-done | bytes 72 | tf_op jit(solution)/shard_map/ppermute | solution.py:234
  202.3 1.9 collective-permute-start.24
  204.3 4.4 %collective-permute-done.24 = f32[10]{0:T(128)S(1)} collective-permute-done((f32[10]{0:T(128)S(1)}, f32[10]{0:T(128)S(1)}, u32[]{:S(2)}, u32[]{:S(2)}) %collective-permute-start.24) | collective-permute-done | bytes 72 | tf_op jit(solution)/shard_map/ppermute | solution.py:234
  208.7 1.9 collective-permute-start.25
  210.6 7.4 %collective-permute-done.25 = f32[10]{0:T(128)S(1)} collective-permute-done((f32[10]{0:T(128)S(1)}, f32[10]{0:T(128)S(1)}, u32[]{:S(2)}, u32[]{:S(2)}) %collective-permute-start.25) | collective-permute-done | bytes 72 | tf_op jit(solution)/shard_map/ppermute | solution.py:234
  (461 shorter events, 13.2 us)
Async XLA Ops:
  0.6 1.4 copy-start.5
  0.6 1.4 copy-start
  2.1 0.7 copy-start.4
  2.8 35.2 %collective-permute-start = (f32[5,10,128]{2,1,0:T(8,128)S(1)}, f32[5,10,128]{2,1,0:T(8,128)S(1)}, u32[]{:S(2)}, u32[]{:S(2)}) collective-permute-start(f32[5,10,128]{2,1,0:T(8,128)S(1)} %get-tuple-element.1105), channel_id=1, source_target_pairs={{0,63},{1,0},{2,1},{3,2},{4,3},{5,4},{6,5},{7,6},{8,7},{9,8},{10,9... | collective-permute-start | bytes 76808 | tf_op jit(solution)/shard_map/ppermute | solution.py:196
  17.9 20.1 %collective-permute-start.1 = (f32[5,10,128]{2,1,0:T(8,128)S(1)}, f32[5,10,128]{2,1,0:T(8,128)S(1)}, u32[]{:S(2)}, u32[]{:S(2)}) collective-permute-start(f32[5,10,128]{2,1,0:T(8,128)S(1)} %get-tuple-element.1105), channel_id=1, source_target_pairs={{0,961},{1,962},{2,963},{3,964},{4,965},{5,966},{6,967},{7,968},{8... | collective-permute-start | bytes 76808 | tf_op jit(solution)/shard_map/ppermute | solution.py:205
  19.8 18.2 %collective-permute-start.2 = (f32[5,10,128]{2,1,0:T(8,128)S(1)}, f32[5,10,128]{2,1,0:T(8,128)S(1)}, u32[]{:S(2)}, u32[]{:S(2)}) collective-permute-start(f32[5,10,128]{2,1,0:T(8,128)S(1)} %get-tuple-element.1105), channel_id=1, source_target_pairs={{0,960},{1,961},{2,962},{3,963},{4,964},{5,965},{6,966},{7,967},{8... | collective-permute-start | bytes 76808 | tf_op jit(solution)/shard_map/ppermute | solution.py:205
  19.9 18.2 %collective-permute-start.3 = (f32[5,10,128]{2,1,0:T(8,128)S(1)}, f32[5,10,128]{2,1,0:T(8,128)S(1)}, u32[]{:S(2)}, u32[]{:S(2)}) collective-permute-start(f32[5,10,128]{2,1,0:T(8,128)S(1)} %get-tuple-element.1105), channel_id=1, source_target_pairs={{0,1023},{1,960},{2,961},{3,962},{4,963},{5,964},{6,965},{7,966},{... | collective-permute-start | bytes 76808 | tf_op jit(solution)/shard_map/ppermute | solution.py:205
  30.7 0.7 copy-start.1
  30.7 0.7 copy-start.2
  31.7 0.7 copy-start.6
  38.1 0.7 copy-start.3
  64.9 11.3 %collective-permute-start.4 = (f32[5,6,128]{2,1,0:T(8,128)S(1)}, f32[5,6,128]{2,1,0:T(8,128)S(1)}, u32[]{:S(2)}, u32[]{:S(2)}) collective-permute-start(f32[5,6,128]{2,1,0:T(8,128)S(1)} %get-tuple-element.1097), channel_id=1, source_target_pairs={{0,1},{1,2},{2,3},{3,4},{4,5},{5,6},{6,7},{7,8},{8,9},{9,10},{10,1... | collective-permute-start | bytes 46088 | tf_op jit(solution)/shard_map/ppermute | solution.py:196
  66.9 9.4 %collective-permute-start.5 = (f32[5,6,128]{2,1,0:T(8,128)S(1)}, f32[5,6,128]{2,1,0:T(8,128)S(1)}, u32[]{:S(2)}, u32[]{:S(2)}) collective-permute-start(f32[5,6,128]{2,1,0:T(8,128)S(1)} %get-tuple-element.1095), channel_id=1, source_target_pairs={{0,127},{1,64},{2,65},{3,66},{4,67},{5,68},{6,69},{7,70},{8,71},{9... | collective-permute-start | bytes 46088 | tf_op jit(solution)/shard_map/ppermute | solution.py:205
  74.0 4.4 %collective-permute-start.6 = (f32[5,6,128]{2,1,0:T(8,128)S(1)}, f32[5,6,128]{2,1,0:T(8,128)S(1)}, u32[]{:S(2)}, u32[]{:S(2)}) collective-permute-start(f32[5,6,128]{2,1,0:T(8,128)S(1)} %get-tuple-element.1096), channel_id=1, source_target_pairs={{0,64},{1,65},{2,66},{3,67},{4,68},{5,69},{6,70},{7,71},{8,72},{9,... | collective-permute-start | bytes 46088 | tf_op jit(solution)/shard_map/ppermute | solution.py:205
  74.3 10.5 %collective-permute-start.7 = (f32[5,6,128]{2,1,0:T(8,128)S(1)}, f32[5,6,128]{2,1,0:T(8,128)S(1)}, u32[]{:S(2)}, u32[]{:S(2)}) collective-permute-start(f32[5,6,128]{2,1,0:T(8,128)S(1)} %get-tuple-element.1098), channel_id=1, source_target_pairs={{0,65},{1,66},{2,67},{3,68},{4,69},{5,70},{6,71},{7,72},{8,73},{9,... | collective-permute-start | bytes 46088 | tf_op jit(solution)/shard_map/ppermute | solution.py:205
  84.9 17.6 %collective-permute-start.8 = (f32[5,6,128]{2,1,0:T(8,128)S(1)}, f32[5,6,128]{2,1,0:T(8,128)S(1)}, u32[]{:S(2)}, u32[]{:S(2)}) collective-permute-start(f32[5,6,128]{2,1,0:T(8,128)S(1)} %broadcast_multiply_fusion.5), channel_id=1, source_target_pairs={{0,63},{1,0},{2,1},{3,2},{4,3},{5,4},{6,5},{7,6},{8,7},{9,8},{10,9... | collective-permute-start | bytes 46088 | tf_op jit(solution)/shard_map/ppermute | solution.py:196
  92.1 10.4 %collective-permute-start.9 = (f32[5,6,128]{2,1,0:T(8,128)S(1)}, f32[5,6,128]{2,1,0:T(8,128)S(1)}, u32[]{:S(2)}, u32[]{:S(2)}) collective-permute-start(f32[5,6,128]{2,1,0:T(8,128)S(1)} %broadcast_multiply_fusion.5), channel_id=1, source_target_pairs={{0,961},{1,962},{2,963},{3,964},{4,965},{5,966},{6,967},{7,968},{8... | collective-permute-start | bytes 46088 | tf_op jit(solution)/shard_map/ppermute | solution.py:205
  94.1 8.5 %collective-permute-start.10 = (f32[5,6,128]{2,1,0:T(8,128)S(1)}, f32[5,6,128]{2,1,0:T(8,128)S(1)}, u32[]{:S(2)}, u32[]{:S(2)}) collective-permute-start(f32[5,6,128]{2,1,0:T(8,128)S(1)} %broadcast_multiply_fusion.5), channel_id=1, source_target_pairs={{0,960},{1,961},{2,962},{3,963},{4,964},{5,965},{6,966},{7,967},{8... | collective-permute-start | bytes 46088 | tf_op jit(solution)/shard_map/ppermute | solution.py:205
  94.4 8.2 %collective-permute-start.11 = (f32[5,6,128]{2,1,0:T(8,128)S(1)}, f32[5,6,128]{2,1,0:T(8,128)S(1)}, u32[]{:S(2)}, u32[]{:S(2)}) collective-permute-start(f32[5,6,128]{2,1,0:T(8,128)S(1)} %broadcast_multiply_fusion.5), channel_id=1, source_target_pairs={{0,1023},{1,960},{2,961},{3,962},{4,963},{5,964},{6,965},{7,966},{... | collective-permute-start | bytes 46088 | tf_op jit(solution)/shard_map/ppermute | solution.py:205
  128.8 10.2 %collective-permute-start.12 = (f32[5,6,128]{2,1,0:T(8,128)S(1)}, f32[5,6,128]{2,1,0:T(8,128)S(1)}, u32[]{:S(2)}, u32[]{:S(2)}) collective-permute-start(f32[5,6,128]{2,1,0:T(8,128)S(1)} %get-tuple-element.1093), channel_id=1, source_target_pairs={{0,1},{1,2},{2,3},{3,4},{4,5},{5,6},{6,7},{7,8},{8,9},{9,10},{10,1... | collective-permute-start | bytes 46088 | tf_op jit(solution)/shard_map/ppermute | solution.py:196
  131.1 7.9 %collective-permute-start.13 = (f32[5,6,128]{2,1,0:T(8,128)S(1)}, f32[5,6,128]{2,1,0:T(8,128)S(1)}, u32[]{:S(2)}, u32[]{:S(2)}) collective-permute-start(f32[5,6,128]{2,1,0:T(8,128)S(1)} %get-tuple-element.1091), channel_id=1, source_target_pairs={{0,127},{1,64},{2,65},{3,66},{4,67},{5,68},{6,69},{7,70},{8,71},{9... | collective-permute-start | bytes 46088 | tf_op jit(solution)/shard_map/ppermute | solution.py:205
  136.2 4.4 %collective-permute-start.14 = (f32[5,6,128]{2,1,0:T(8,128)S(1)}, f32[5,6,128]{2,1,0:T(8,128)S(1)}, u32[]{:S(2)}, u32[]{:S(2)}) collective-permute-start(f32[5,6,128]{2,1,0:T(8,128)S(1)} %get-tuple-element.1092), channel_id=1, source_target_pairs={{0,64},{1,65},{2,66},{3,67},{4,68},{5,69},{6,70},{7,71},{8,72},{9,... | collective-permute-start | bytes 46088 | tf_op jit(solution)/shard_map/ppermute | solution.py:205
  136.7 10.4 %collective-permute-start.15 = (f32[5,6,128]{2,1,0:T(8,128)S(1)}, f32[5,6,128]{2,1,0:T(8,128)S(1)}, u32[]{:S(2)}, u32[]{:S(2)}) collective-permute-start(f32[5,6,128]{2,1,0:T(8,128)S(1)} %get-tuple-element.1094), channel_id=1, source_target_pairs={{0,65},{1,66},{2,67},{3,68},{4,69},{5,70},{6,71},{7,72},{8,73},{9,... | collective-permute-start | bytes 46088 | tf_op jit(solution)/shard_map/ppermute | solution.py:205
  148.2 3.0 %collective-permute-start.16 = (f32[10]{0:T(128)S(1)}, f32[10]{0:T(128)S(1)}, u32[]{:S(2)}, u32[]{:S(2)}) collective-permute-start(f32[10]{0:T(128)S(1)} %concatenate.280), channel_id=1, source_target_pairs={{0,64},{64,0},{128,192},{192,128},{256,320},{320,256},{384,448},{4... | collective-permute-start | bytes 128 | tf_op jit(solution)/shard_map/ppermute | solution.py:234
  151.2 5.4 %collective-permute-start.17 = (f32[10]{0:T(128)S(1)}, f32[10]{0:T(128)S(1)}, u32[]{:S(2)}, u32[]{:S(2)}) collective-permute-start(f32[10]{0:T(128)S(1)} %add.1146), channel_id=1, source_target_pairs={{0,128},{64,192},{128,0},{192,64},{256,384},{320,448},{384,256},{4... | collective-permute-start | bytes 128 | tf_op jit(solution)/shard_map/ppermute | solution.py:234
  156.6 6.3 %collective-permute-start.18 = (f32[10]{0:T(128)S(1)}, f32[10]{0:T(128)S(1)}, u32[]{:S(2)}, u32[]{:S(2)}) collective-permute-start(f32[10]{0:T(128)S(1)} %add.1147), channel_id=1, source_target_pairs={{0,256},{64,320},{128,384},{192,448},{256,0},{320,64},{384,128},{4... | collective-permute-start | bytes 128 | tf_op jit(solution)/shard_map/ppermute | solution.py:234
  162.9 9.3 %collective-permute-start.19 = (f32[10]{0:T(128)S(1)}, f32[10]{0:T(128)S(1)}, u32[]{:S(2)}, u32[]{:S(2)}) collective-permute-start(f32[10]{0:T(128)S(1)} %add.1148), channel_id=1, source_target_pairs={{0,512},{64,576},{128,640},{192,704},{256,768},{320,832},{384,896}... | collective-permute-start | bytes 128 | tf_op jit(solution)/shard_map/ppermute | solution.py:234
  172.3 9.0 %collective-permute-start.20 = (f32[10]{0:T(128)S(1)}, f32[10]{0:T(128)S(1)}, u32[]{:S(2)}, u32[]{:S(2)}) collective-permute-start(f32[10]{0:T(128)S(1)} %add.1149), channel_id=1, source_target_pairs={{0,1},{1,0},{2,3},{3,2},{4,5},{5,4},{6,7},{7,6},{8,9},{9,8},{10,11... | collective-permute-start | bytes 128 | tf_op jit(solution)/shard_map/ppermute | solution.py:234
  181.2 6.3 %collective-permute-start.21 = (f32[10]{0:T(128)S(1)}, f32[10]{0:T(128)S(1)}, u32[]{:S(2)}, u32[]{:S(2)}) collective-permute-start(f32[10]{0:T(128)S(1)} %add.1150), channel_id=1, source_target_pairs={{0,2},{1,3},{2,0},{3,1},{4,6},{5,7},{6,4},{7,5},{8,10},{9,11},{10,... | collective-permute-start | bytes 128 | tf_op jit(solution)/shard_map/ppermute | solution.py:234
  187.6 9.3 %collective-permute-start.22 = (f32[10]{0:T(128)S(1)}, f32[10]{0:T(128)S(1)}, u32[]{:S(2)}, u32[]{:S(2)}) collective-permute-start(f32[10]{0:T(128)S(1)} %add.1151), channel_id=1, source_target_pairs={{0,4},{1,5},{2,6},{3,7},{4,0},{5,1},{6,2},{7,3},{8,12},{9,13},{10,... | collective-permute-start | bytes 128 | tf_op jit(solution)/shard_map/ppermute | solution.py:234
  196.9 5.4 %collective-permute-start.23 = (f32[10]{0:T(128)S(1)}, f32[10]{0:T(128)S(1)}, u32[]{:S(2)}, u32[]{:S(2)}) collective-permute-start(f32[10]{0:T(128)S(1)} %add.1152), channel_id=1, source_target_pairs={{0,8},{1,9},{2,10},{3,11},{4,12},{5,13},{6,14},{7,15},{8,0},{9,1},... | collective-permute-start | bytes 128 | tf_op jit(solution)/shard_map/ppermute | solution.py:234
  202.3 6.3 %collective-permute-start.24 = (f32[10]{0:T(128)S(1)}, f32[10]{0:T(128)S(1)}, u32[]{:S(2)}, u32[]{:S(2)}) collective-permute-start(f32[10]{0:T(128)S(1)} %add.1153), channel_id=1, source_target_pairs={{0,16},{1,17},{2,18},{3,19},{4,20},{5,21},{6,22},{7,23},{8,24},{9,... | collective-permute-start | bytes 128 | tf_op jit(solution)/shard_map/ppermute | solution.py:234
  208.7 9.3 %collective-permute-start.25 = (f32[10]{0:T(128)S(1)}, f32[10]{0:T(128)S(1)}, u32[]{:S(2)}, u32[]{:S(2)}) collective-permute-start(f32[10]{0:T(128)S(1)} %add.1154), channel_id=1, source_target_pairs={{0,32},{1,33},{2,34},{3,35},{4,36},{5,37},{6,38},{7,39},{8,40},{9,... | collective-permute-start | bytes 128 | tf_op jit(solution)/shard_map/ppermute | solution.py:234

commit v7 on v5

--- a/solution.py
+++ b/solution.py
@@ -217,6 +217,13 @@
     return values
 
 
+def field_dot(values, own_total, other_acc):
+    total = set_sums(values[0], own_total)
+    for slot_index in range(other_acc.shape[0]):
+        total = total + set_sums(values[slot_index + 1], other_acc[slot_index])
+    return total
+
+
 def global_sums(local_values):
     return butterfly_sum(butterfly_sum(local_values, "gx"), "gy")
 
@@ -245,15 +252,18 @@
     image = search / pol_wide - mutual_field(geom_stack, dip_stack)
     scaled = pol_wide * image
     scaled_dip = neighbours(scaled)
-    image_scaled = scaled / pol_wide - mutual_field(geom_stack, scaled_dip)
+    own_second, other_second = accumulate(geom_stack, scaled_dip, presence)
+    search_field = field_dot(dip_stack, own_second, other_second)
+    scaled_field = field_dot(scaled_dip, own_second, other_second)
+    image_scaled = scaled / pol_wide - (own_second + send_back(other_second)) * atom_mask[:, None, :]
     sums = global_sums(
         jnp.concatenate(
             [
                 set_sums(residual, search),
                 set_sums(search, image),
                 set_sums(image, scaled),
-                set_sums(search, image_scaled),
-                set_sums(scaled, image_scaled),
+                set_sums(search, scaled / pol_wide) - search_field,
+                set_sums(scaled, scaled / pol_wide) - scaled_field,
             ]
         )
     )

time: 209 us -> 207 us (level)
  waiting for transfers between devices: 62.2 us -> 58.4 us
    ppermute x4, waiting for transfers between devices: 14.1 us -> 11.7 us  [from_behind(): return lax.ppermute(value, axis, pairs)]
  transfers between devices with their start and end apart: 22 -> 22, of which waited for: 17 -> 16; matrix products, arithmetic and copies ran while one was open for 4% -> 6% of each run, Pallas kernels for 0% -> 0%
where the time goes in v7:
time: 207 us
  starting transfers between devices  75.2 us (36%)
  other arithmetic  60.7 us (29%)
  waiting for transfers between devices  58.4 us (28%)
  local copies, waits for them, and re-layouts  8.54 us (4%)
  between operations  2.16 us (1%)
    reduce_sum x22, other arithmetic, tensor_apply(): jnp.sum(scaled * deltas[member] - coef_three * moments[member], axis=axis...  52.1 us
    ppermute x10, waiting for transfers between devices, butterfly_sum(): lax.ppermute(values, axis, [(i, i ^ stride) for i in range(count)])  42.2 us
    ppermute x4, starting transfers between devices, padded_2(): lax.ppermute(head, axis, [((i + 1) % count, i) for i in range(count)])  37.7 us
    ppermute x10, starting transfers between devices, butterfly_sum(): lax.ppermute(values, axis, [(i, i ^ stride) for i in range(count)])  27.3 us
    ppermute x4, waiting for transfers between devices, from_behind(): return lax.ppermute(value, axis, pairs)  11.7 us
    ppermute x4, starting transfers between devices, padded_2(): lax.ppermute(tail, axis, [(i, (i + 1) % count) for i in range(count)])  7.86 us
  transfers between devices with their start and end apart: 22, of which 16 were waited for; matrix products, arithmetic and copies ran while one was open for 6% of the time, Pallas kernels for 0%

profile of v7, /device:TPU:2, one launch (start us, length us, event | category | flops | bytes accessed | tf_op | source)
XLA Modules:
  0.0 206.7 jit_solution(17899097736151920343)
XLA Ops:
  0.6 0.7 copy.228
  1.3 0.7 fusion.246
  2.1 0.7 copy-done.4
  2.8 15.1 %collective-permute-start = (f32[1,1,5,10,128]{4,3,2,1,0:T(8,128)S(1)}, f32[1,1,5,10,128]{4,3,2,1,0:T(8,128)S(1)}, u32[]{:S(2)}, u32[]{:S(2)}) collective-permute-start(f32[1,1,5,10,128]{4,3,2,1,0:T(8,128)S(1)} %get-tuple-element.1113), channel_id=1, source_target_pairs={{1,0},{2,1},{3,2},{4,3},{5,4},{6,5},{7,6},{8,7},{9,8},{10,9},{11,1... | collective-permute-start | bytes 76808 | tf_op jit(solution)/shard_map/ppermute | solution.py:24
  17.9 1.9 collective-permute-start.1
  19.9 0.7 copy-done.6
  20.6 0.6 copy-done.1
  22.9 0.7 fusion.202
  23.6 1.3 fusion.204
  25.2 1.4 fusion.132
  27.1 2.3 %collective-permute-start.2 = (f32[1,3,5,10,128]{4,3,2,1,0:T(8,128)S(1)}, f32[1,3,5,10,128]{4,3,2,1,0:T(8,128)S(1)}, u32[]{:S(2)}, u32[]{:S(2)}) collective-permute-start(f32[1,3,5,10,128]{4,3,2,1,0:T(8,128)S(1)} %pad_maximum_fusion.4), channel_id=1, source_target_pairs={{0,960},{64,0},{128,64},{192,128},{256,192},{320,256},{384,320},{4... | collective-permute-start | bytes 230408 | tf_op jit(solution)/shard_map/ppermute | solution.py:34
  29.5 2.4 %collective-permute-done.2 = f32[1,3,5,10,128]{4,3,2,1,0:T(8,128)S(1)} collective-permute-done((f32[1,3,5,10,128]{4,3,2,1,0:T(8,128)S(1)}, f32[1,3,5,10,128]{4,3,2,1,0:T(8,128)S(1)}, u32[]{:S(2)}, u32[]{:S(2)}) %collective-permute-start.2) | collective-permute-done | bytes 76832 | tf_op jit(solution)/shard_map/ppermute | solution.py:34
  32.0 0.6 copy-done.3
  32.6 26.2 %while.44 = (s32[]{:T(128)}, f32[5,6,128]{2,0,1:T(8,128)S(1)}, f32[4,5,6,128]{3,2,1,0:T(8,128)S(1)}, f32[5,3,5]{2,1,0:T(4,128)S(1)}, f32[5,5,4,128]{3,1,2,0:T(8,...) while((s32[]{:T(128)}, f32[5,6,128]{2,0,1:T(8,128)S(1)}, ...), condition=%wide.region_40.41_spmd.clone, body=%wide.region_25.40_spmd.sunk.clone.sunk | while | flops 25193012 | bytes 1431648 | solution.py:185
  32.9 3.5 %fusion.282 = (f32[13,128]{1,0:T(8,128)S(1)}, f32[13,128]{1,0:T(8,128)S(1)}, f32[13,128]{1,0:T(8,128)S(1)}, f32[13,128]{1,0:T(8,128)S(1)}, f32[13,128]{1,0:T(8,1...) fusion(f32[13,128]{1,0:T(8,128)S(1)} %get-tuple-element.1384, ...), kind=kLoop, calls=%fused_computation.71.clone.1 | loop fusion | flops 16385408 | bytes 173056 | tf_op jit(solution)/shard_map/while/body/eval_jaxpr/reduce_sum | solution.py:46
  36.7 2.2 %fusion.284 = (f32[13,128]{1,0:T(8,128)S(1)}, f32[13,128]{1,0:T(8,128)S(1)}, f32[13,128]{1,0:T(8,128)S(1)}) fusion(f32[13,128]{1,0:T(8,128)S(1)} %get-tuple-element.1417, f32[13,128]{1,0:T(8,128)S(1)} %get-tuple-element.1385, f32[13,128]{1,0:T(8,128)S(1)} %get-tuple-element.1392, f32[13,128]{1,0:T(8,128)S(1)} %get-tuple-element.1418, ...), kind=kLoop, calls=%fused_computation.65.clone.1 | loop fusion | flops 8727680 | bytes 93184 | tf_op jit(solution)/shard_map/while/body/eval_jaxpr/reduce_sum | solution.py:46
  39.5 3.5 %fusion.282 = (f32[13,128]{1,0:T(8,128)S(1)}, f32[13,128]{1,0:T(8,128)S(1)}, f32[13,128]{1,0:T(8,128)S(1)}, f32[13,128]{1,0:T(8,128)S(1)}, f32[13,128]{1,0:T(8,1...) fusion(f32[13,128]{1,0:T(8,128)S(1)} %get-tuple-element.1384, ...), kind=kLoop, calls=%fused_computation.71.clone.1 | loop fusion | flops 16385408 | bytes 173056 | tf_op jit(solution)/shard_map/while/body/eval_jaxpr/reduce_sum | solution.py:46
  43.2 2.2 %fusion.284 = (f32[13,128]{1,0:T(8,128)S(1)}, f32[13,128]{1,0:T(8,128)S(1)}, f32[13,128]{1,0:T(8,128)S(1)}) fusion(f32[13,128]{1,0:T(8,128)S(1)} %get-tuple-element.1417, f32[13,128]{1,0:T(8,128)S(1)} %get-tuple-element.1385, f32[13,128]{1,0:T(8,128)S(1)} %get-tuple-element.1392, f32[13,128]{1,0:T(8,128)S(1)} %get-tuple-element.1418, ...), kind=kLoop, calls=%fused_computation.65.clone.1 | loop fusion | flops 8727680 | bytes 93184 | tf_op jit(solution)/shard_map/while/body/eval_jaxpr/reduce_sum | solution.py:46
  46.0 3.5 %fusion.282 = (f32[13,128]{1,0:T(8,128)S(1)}, f32[13,128]{1,0:T(8,128)S(1)}, f32[13,128]{1,0:T(8,128)S(1)}, f32[13,128]{1,0:T(8,128)S(1)}, f32[13,128]{1,0:T(8,1...) fusion(f32[13,128]{1,0:T(8,128)S(1)} %get-tuple-element.1384, ...), kind=kLoop, calls=%fused_computation.71.clone.1 | loop fusion | flops 16385408 | bytes 173056 | tf_op jit(solution)/shard_map/while/body/eval_jaxpr/reduce_sum | solution.py:46
  49.8 2.2 %fusion.284 = (f32[13,128]{1,0:T(8,128)S(1)}, f32[13,128]{1,0:T(8,128)S(1)}, f32[13,128]{1,0:T(8,128)S(1)}) fusion(f32[13,128]{1,0:T(8,128)S(1)} %get-tuple-element.1417, f32[13,128]{1,0:T(8,128)S(1)} %get-tuple-element.1385, f32[13,128]{1,0:T(8,128)S(1)} %get-tuple-element.1392, f32[13,128]{1,0:T(8,128)S(1)} %get-tuple-element.1418, ...), kind=kLoop, calls=%fused_computation.65.clone.1 | loop fusion | flops 8727680 | bytes 93184 | tf_op jit(solution)/shard_map/while/body/eval_jaxpr/reduce_sum | solution.py:46
  52.6 3.5 %fusion.282 = (f32[13,128]{1,0:T(8,128)S(1)}, f32[13,128]{1,0:T(8,128)S(1)}, f32[13,128]{1,0:T(8,128)S(1)}, f32[13,128]{1,0:T(8,128)S(1)}, f32[13,128]{1,0:T(8,1...) fusion(f32[13,128]{1,0:T(8,128)S(1)} %get-tuple-element.1384, ...), kind=kLoop, calls=%fused_computation.71.clone.1 | loop fusion | flops 16385408 | bytes 173056 | tf_op jit(solution)/shard_map/while/body/eval_jaxpr/reduce_sum | solution.py:46
  56.3 2.2 %fusion.284 = (f32[13,128]{1,0:T(8,128)S(1)}, f32[13,128]{1,0:T(8,128)S(1)}, f32[13,128]{1,0:T(8,128)S(1)}) fusion(f32[13,128]{1,0:T(8,128)S(1)} %get-tuple-element.1417, f32[13,128]{1,0:T(8,128)S(1)} %get-tuple-element.1385, f32[13,128]{1,0:T(8,128)S(1)} %get-tuple-element.1392, f32[13,128]{1,0:T(8,128)S(1)} %get-tuple-element.1418, ...), kind=kLoop, calls=%fused_computation.65.clone.1 | loop fusion | flops 8727680 | bytes 93184 | tf_op jit(solution)/shard_map/while/body/eval_jaxpr/reduce_sum | solution.py:46
  58.8 5.0 %collective-permute-done.3 = f32[1,3,5,6,128]{4,3,2,1,0:T(8,128)S(1)} collective-permute-done((f32[1,3,5,6,128]{4,3,2,1,0:T(8,128)S(1)}, f32[1,3,5,6,128]{4,3,2,1,0:T(8,128)S(1)}, u32[]{:S(2)}, u32[]{:S(2)}) %collective-permute-start.3) | collective-permute-done | bytes 46112 | tf_op jit(solution)/shard_map/ppermute | solution.py:34
  63.8 1.9 collective-permute-start.4
  65.8 8.1 %collective-permute-start.5 = (f32[1,1,5,6,128]{4,3,2,1,0:T(8,128)S(1)}, f32[1,1,5,6,128]{4,3,2,1,0:T(8,128)S(1)}, u32[]{:S(2)}, u32[]{:S(2)}) collective-permute-start(f32[1,1,5,6,128]{4,3,2,1,0:T(8,128)S(1)} %get-tuple-element.1107), channel_id=1, source_target_pairs={{1,0},{2,1},{3,2},{4,3},{5,4},{6,5},{7,6},{8,7},{9,8},{10,9},{11,1... | collective-permute-start | bytes 46088 | tf_op jit(solution)/shard_map/ppermute | solution.py:24
  74.2 1.1 collective-permute-done.5
  75.4 7.2 %collective-permute-start.6 = (f32[1,1,5,6,128]{4,3,2,1,0:T(8,128)S(1)}, f32[1,1,5,6,128]{4,3,2,1,0:T(8,128)S(1)}, u32[]{:S(2)}, u32[]{:S(2)}) collective-permute-start(f32[1,1,5,6,128]{4,3,2,1,0:T(8,128)S(1)} %get-tuple-element.1116), channel_id=1, source_target_pairs={{1,0},{2,1},{3,2},{4,3},{5,4},{6,5},{7,6},{8,7},{9,8},{10,9},{11,1... | collective-permute-start | bytes 46088 | tf_op jit(solution)/shard_map/ppermute | solution.py:24
  82.7 2.1 %collective-permute-start.7 = (f32[1,1,5,6,128]{4,3,2,1,0:T(8,128)S(1)}, f32[1,1,5,6,128]{4,3,2,1,0:T(8,128)S(1)}, u32[]{:S(2)}, u32[]{:S(2)}) collective-permute-start(f32[1,1,5,6,128]{4,3,2,1,0:T(8,128)S(1)} %get-tuple-element.1116), channel_id=1, source_target_pairs={{0,1},{1,2},{2,3},{3,4},{4,5},{5,6},{6,7},{7,8},{8,9},{9,10},{10,1... | collective-permute-start | bytes 46088 | tf_op jit(solution)/shard_map/ppermute | solution.py:22
  84.8 1.3 fusion.212
  86.2 1.4 fusion.136
  88.6 3.4 %collective-permute-done.7 = f32[1,1,5,6,128]{4,3,2,1,0:T(8,128)S(1)} collective-permute-done((f32[1,1,5,6,128]{4,3,2,1,0:T(8,128)S(1)}, f32[1,1,5,6,128]{4,3,2,1,0:T(8,128)S(1)}, u32[]{:S(2)}, u32[]{:S(2)}) %collective-permute-start.7) | collective-permute-done | bytes 15392 | tf_op jit(solution)/shard_map/ppermute | solution.py:22
  92.0 1.8 collective-permute-done.8
  93.9 26.1 %while.45 = (s32[]{:T(128)}, f32[5,6,128]{2,0,1:T(8,128)S(1)}, f32[4,5,6,128]{3,2,1,0:T(8,128)S(1)}, f32[5,3,5]{2,1,0:T(4,128)S(1)}, f32[5,5,4,128]{3,1,2,0:T(8,...) while((s32[]{:T(128)}, f32[5,6,128]{2,0,1:T(8,128)S(1)}, ...), condition=%wide.region_84.85_spmd.clone, body=%wide.region_69.84_spmd.sunk.clone.sunk | while | flops 25193012 | bytes 1431648 | solution.py:185
  94.2 3.5 %fusion.289 = (f32[13,128]{1,0:T(8,128)S(1)}, f32[13,128]{1,0:T(8,128)S(1)}, f32[13,128]{1,0:T(8,128)S(1)}, f32[13,128]{1,0:T(8,128)S(1)}, f32[13,128]{1,0:T(8,1...) fusion(f32[13,128]{1,0:T(8,128)S(1)} %get-tuple-element.1438, ...), kind=kLoop, calls=%fused_computation.207.clone.1 | loop fusion | flops 16385408 | bytes 173056 | tf_op jit(solution)/shard_map/while/body/eval_jaxpr/reduce_sum | solution.py:46
  98.0 2.1 %fusion.291 = (f32[13,128]{1,0:T(8,128)S(1)}, f32[13,128]{1,0:T(8,128)S(1)}, f32[13,128]{1,0:T(8,128)S(1)}) fusion(f32[13,128]{1,0:T(8,128)S(1)} %get-tuple-element.1471, f32[13,128]{1,0:T(8,128)S(1)} %get-tuple-element.1439, f32[13,128]{1,0:T(8,128)S(1)} %get-tuple-element.1446, f32[13,128]{1,0:T(8,128)S(1)} %get-tuple-element.1472, ...), kind=kLoop, calls=%fused_computation.201.clone.1 | loop fusion | flops 8727680 | bytes 93184 | tf_op jit(solution)/shard_map/while/body/eval_jaxpr/reduce_sum | solution.py:46
  100.8 3.5 %fusion.289 = (f32[13,128]{1,0:T(8,128)S(1)}, f32[13,128]{1,0:T(8,128)S(1)}, f32[13,128]{1,0:T(8,128)S(1)}, f32[13,128]{1,0:T(8,128)S(1)}, f32[13,128]{1,0:T(8,1...) fusion(f32[13,128]{1,0:T(8,128)S(1)} %get-tuple-element.1438, ...), kind=kLoop, calls=%fused_computation.207.clone.1 | loop fusion | flops 16385408 | bytes 173056 | tf_op jit(solution)/shard_map/while/body/eval_jaxpr/reduce_sum | solution.py:46
  104.5 2.1 %fusion.291 = (f32[13,128]{1,0:T(8,128)S(1)}, f32[13,128]{1,0:T(8,128)S(1)}, f32[13,128]{1,0:T(8,128)S(1)}) fusion(f32[13,128]{1,0:T(8,128)S(1)} %get-tuple-element.1471, f32[13,128]{1,0:T(8,128)S(1)} %get-tuple-element.1439, f32[13,128]{1,0:T(8,128)S(1)} %get-tuple-element.1446, f32[13,128]{1,0:T(8,128)S(1)} %get-tuple-element.1472, ...), kind=kLoop, calls=%fused_computation.201.clone.1 | loop fusion | flops 8727680 | bytes 93184 | tf_op jit(solution)/shard_map/while/body/eval_jaxpr/reduce_sum | solution.py:46
  107.3 3.5 %fusion.289 = (f32[13,128]{1,0:T(8,128)S(1)}, f32[13,128]{1,0:T(8,128)S(1)}, f32[13,128]{1,0:T(8,128)S(1)}, f32[13,128]{1,0:T(8,128)S(1)}, f32[13,128]{1,0:T(8,1...) fusion(f32[13,128]{1,0:T(8,128)S(1)} %get-tuple-element.1438, ...), kind=kLoop, calls=%fused_computation.207.clone.1 | loop fusion | flops 16385408 | bytes 173056 | tf_op jit(solution)/shard_map/while/body/eval_jaxpr/reduce_sum | solution.py:46
  111.0 2.1 %fusion.291 = (f32[13,128]{1,0:T(8,128)S(1)}, f32[13,128]{1,0:T(8,128)S(1)}, f32[13,128]{1,0:T(8,128)S(1)}) fusion(f32[13,128]{1,0:T(8,128)S(1)} %get-tuple-element.1471, f32[13,128]{1,0:T(8,128)S(1)} %get-tuple-element.1439, f32[13,128]{1,0:T(8,128)S(1)} %get-tuple-element.1446, f32[13,128]{1,0:T(8,128)S(1)} %get-tuple-element.1472, ...), kind=kLoop, calls=%fused_computation.201.clone.1 | loop fusion | flops 8727680 | bytes 93184 | tf_op jit(solution)/shard_map/while/body/eval_jaxpr/reduce_sum | solution.py:46
  113.8 3.5 %fusion.289 = (f32[13,128]{1,0:T(8,128)S(1)}, f32[13,128]{1,0:T(8,128)S(1)}, f32[13,128]{1,0:T(8,128)S(1)}, f32[13,128]{1,0:T(8,128)S(1)}, f32[13,128]{1,0:T(8,1...) fusion(f32[13,128]{1,0:T(8,128)S(1)} %get-tuple-element.1438, ...), kind=kLoop, calls=%fused_computation.207.clone.1 | loop fusion | flops 16385408 | bytes 173056 | tf_op jit(solution)/shard_map/while/body/eval_jaxpr/reduce_sum | solution.py:46
  117.5 2.1 %fusion.291 = (f32[13,128]{1,0:T(8,128)S(1)}, f32[13,128]{1,0:T(8,128)S(1)}, f32[13,128]{1,0:T(8,128)S(1)}) fusion(f32[13,128]{1,0:T(8,128)S(1)} %get-tuple-element.1471, f32[13,128]{1,0:T(8,128)S(1)} %get-tuple-element.1439, f32[13,128]{1,0:T(8,128)S(1)} %get-tuple-element.1446, f32[13,128]{1,0:T(8,128)S(1)} %get-tuple-element.1472, ...), kind=kLoop, calls=%fused_computation.201.clone.1 | loop fusion | flops 8727680 | bytes 93184 | tf_op jit(solution)/shard_map/while/body/eval_jaxpr/reduce_sum | solution.py:46
  122.4 2.5 %collective-permute-done.19 = f32[1,3,5,6,128]{4,3,2,1,0:T(8,128)S(1)} collective-permute-done((f32[1,3,5,6,128]{4,3,2,1,0:T(8,128)S(1)}, f32[1,3,5,6,128]{4,3,2,1,0:T(8,128)S(1)}, u32[]{:S(2)}, u32[]{:S(2)}) %collective-permute-start.19) | collective-permute-done | bytes 46112 | tf_op jit(solution)/shard_map/ppermute | solution.py:34
  125.1 1.9 collective-permute-start.20
  127.0 7.2 %collective-permute-start.21 = (f32[1,1,5,6,128]{4,3,2,1,0:T(8,128)S(1)}, f32[1,1,5,6,128]{4,3,2,1,0:T(8,128)S(1)}, u32[]{:S(2)}, u32[]{:S(2)}) collective-permute-start(f32[1,1,5,6,128]{4,3,2,1,0:T(8,128)S(1)} %get-tuple-element.1105), channel_id=1, source_target_pairs={{1,0},{2,1},{3,2},{4,3},{5,4},{6,5},{7,6},{8,7},{9,8},{10,9},{11,1... | collective-permute-start | bytes 46088 | tf_op jit(solution)/shard_map/ppermute | solution.py:24
  135.2 1.9 collective-permute-start.9
  137.1 1.1 collective-permute-done.9
  138.2 1.9 collective-permute-start.10
  140.1 3.5 %collective-permute-done.10 = f32[10]{0:T(128)S(1)} collective-permute-done((f32[10]{0:T(128)S(1)}, f32[10]{0:T(128)S(1)}, u32[]{:S(2)}, u32[]{:S(2)}) %collective-permute-start.10) | collective-permute-done | bytes 72 | tf_op jit(solution)/shard_map/ppermute | solution.py:214
  143.6 1.9 collective-permute-start.11
  145.5 4.4 %collective-permute-done.11 = f32[10]{0:T(128)S(1)} collective-permute-done((f32[10]{0:T(128)S(1)}, f32[10]{0:T(128)S(1)}, u32[]{:S(2)}, u32[]{:S(2)}) %collective-permute-start.11) | collective-permute-done | bytes 72 | tf_op jit(solution)/shard_map/ppermute | solution.py:214
  149.9 4.8 %collective-permute-start.12 = (f32[10]{0:T(128)S(1)}, f32[10]{0:T(128)S(1)}, u32[]{:S(2)}, u32[]{:S(2)}) collective-permute-start(f32[10]{0:T(128)S(1)} %add.1187), channel_id=1, source_target_pairs={{0,512},{64,576},{128,640},{192,704},{256,768},{320,832},{384,896}... | collective-permute-start | bytes 128 | tf_op jit(solution)/shard_map/ppermute | solution.py:214
  154.7 4.6 %collective-permute-done.12 = f32[10]{0:T(128)S(1)} collective-permute-done((f32[10]{0:T(128)S(1)}, f32[10]{0:T(128)S(1)}, u32[]{:S(2)}, u32[]{:S(2)}) %collective-permute-start.12) | collective-permute-done | bytes 72 | tf_op jit(solution)/shard_map/ppermute | solution.py:214
  159.3 7.2 %collective-permute-start.13 = (f32[10]{0:T(128)S(1)}, f32[10]{0:T(128)S(1)}, u32[]{:S(2)}, u32[]{:S(2)}) collective-permute-start(f32[10]{0:T(128)S(1)} %add.1188), channel_id=1, source_target_pairs={{0,1},{1,0},{2,3},{3,2},{4,5},{5,4},{6,7},{7,6},{8,9},{9,8},{10,11... | collective-permute-start | bytes 128 | tf_op jit(solution)/shard_map/ppermute | solution.py:214
  166.5 1.5 collective-permute-done.13
  168.0 1.9 collective-permute-start.14
  169.9 4.4 %collective-permute-done.14 = f32[10]{0:T(128)S(1)} collective-permute-done((f32[10]{0:T(128)S(1)}, f32[10]{0:T(128)S(1)}, u32[]{:S(2)}, u32[]{:S(2)}) %collective-permute-start.14) | collective-permute-done | bytes 72 | tf_op jit(solution)/shard_map/ppermute | solution.py:214
  174.3 1.9 collective-permute-start.15
  176.3 7.4 %collective-permute-done.15 = f32[10]{0:T(128)S(1)} collective-permute-done((f32[10]{0:T(128)S(1)}, f32[10]{0:T(128)S(1)}, u32[]{:S(2)}, u32[]{:S(2)}) %collective-permute-start.15) | collective-permute-done | bytes 72 | tf_op jit(solution)/shard_map/ppermute | solution.py:214
  183.7 1.9 collective-permute-start.16
  185.6 3.5 %collective-permute-done.16 = f32[10]{0:T(128)S(1)} collective-permute-done((f32[10]{0:T(128)S(1)}, f32[10]{0:T(128)S(1)}, u32[]{:S(2)}, u32[]{:S(2)}) %collective-permute-start.16) | collective-permute-done | bytes 72 | tf_op jit(solution)/shard_map/ppermute | solution.py:214
  189.1 1.9 collective-permute-start.17
  191.0 4.4 %collective-permute-done.17 = f32[10]{0:T(128)S(1)} collective-permute-done((f32[10]{0:T(128)S(1)}, f32[10]{0:T(128)S(1)}, u32[]{:S(2)}, u32[]{:S(2)}) %collective-permute-start.17) | collective-permute-done | bytes 72 | tf_op jit(solution)/shard_map/ppermute | solution.py:214
  195.4 1.9 collective-permute-start.18
  197.3 7.4 %collective-permute-done.18 = f32[10]{0:T(128)S(1)} collective-permute-done((f32[10]{0:T(128)S(1)}, f32[10]{0:T(128)S(1)}, u32[]{:S(2)}, u32[]{:S(2)}) %collective-permute-start.18) | collective-permute-done | bytes 72 | tf_op jit(solution)/shard_map/ppermute | solution.py:214
  (478 shorter events, 13.8 us)
Async XLA Ops:
  0.6 1.4 copy-start.5
  0.6 1.4 copy-start
  2.1 0.7 copy-start.4
  2.8 24.3 %collective-permute-start = (f32[1,1,5,10,128]{4,3,2,1,0:T(8,128)S(1)}, f32[1,1,5,10,128]{4,3,2,1,0:T(8,128)S(1)}, u32[]{:S(2)}, u32[]{:S(2)}) collective-permute-start(f32[1,1,5,10,128]{4,3,2,1,0:T(8,128)S(1)} %get-tuple-element.1113), channel_id=1, source_target_pairs={{1,0},{2,1},{3,2},{4,3},{5,4},{6,5},{7,6},{8,7},{9,8},{10,9},{11,1... | collective-permute-start | bytes 76808 | tf_op jit(solution)/shard_map/ppermute | solution.py:24
  17.9 9.2 %collective-permute-start.1 = (f32[1,1,5,10,128]{4,3,2,1,0:T(8,128)S(1)}, f32[1,1,5,10,128]{4,3,2,1,0:T(8,128)S(1)}, u32[]{:S(2)}, u32[]{:S(2)}) collective-permute-start(f32[1,1,5,10,128]{4,3,2,1,0:T(8,128)S(1)} %get-tuple-element.1113), channel_id=1, source_target_pairs={{0,1},{1,2},{2,3},{3,4},{4,5},{5,6},{6,7},{7,8},{8,9},{9,10},{10,1... | collective-permute-start | bytes 76808 | tf_op jit(solution)/shard_map/ppermute | solution.py:22
  19.9 0.7 copy-start.6
  20.5 0.7 copy-start.1
  20.6 0.7 copy-start.2
  27.1 4.7 %collective-permute-start.2 = (f32[1,3,5,10,128]{4,3,2,1,0:T(8,128)S(1)}, f32[1,3,5,10,128]{4,3,2,1,0:T(8,128)S(1)}, u32[]{:S(2)}, u32[]{:S(2)}) collective-permute-start(f32[1,3,5,10,128]{4,3,2,1,0:T(8,128)S(1)} %pad_maximum_fusion.4), channel_id=1, source_target_pairs={{0,960},{64,0},{128,64},{192,128},{256,192},{320,256},{384,320},{4... | collective-permute-start | bytes 230408 | tf_op jit(solution)/shard_map/ppermute | solution.py:34
  31.9 0.7 copy-start.3
  58.8 5.0 %collective-permute-start.3 = (f32[1,3,5,6,128]{4,3,2,1,0:T(8,128)S(1)}, f32[1,3,5,6,128]{4,3,2,1,0:T(8,128)S(1)}, u32[]{:S(2)}, u32[]{:S(2)}) collective-permute-start(f32[1,3,5,6,128]{4,3,2,1,0:T(8,128)S(1)} %slice_bitcast_fusion.47), channel_id=1, source_target_pairs={{0,64},{64,128},{128,192},{192,256},{256,320},{320,384},{384,448},... | collective-permute-start | bytes 138248 | tf_op jit(solution)/shard_map/ppermute | solution.py:34
  63.8 10.4 %collective-permute-start.4 = (f32[1,1,5,6,128]{4,3,2,1,0:T(8,128)S(1)}, f32[1,1,5,6,128]{4,3,2,1,0:T(8,128)S(1)}, u32[]{:S(2)}, u32[]{:S(2)}) collective-permute-start(f32[1,1,5,6,128]{4,3,2,1,0:T(8,128)S(1)} %get-tuple-element.1108), channel_id=1, source_target_pairs={{0,1},{1,2},{2,3},{3,4},{4,5},{5,6},{6,7},{7,8},{8,9},{9,10},{10,1... | collective-permute-start | bytes 46088 | tf_op jit(solution)/shard_map/ppermute | solution.py:22
  65.8 9.6 %collective-permute-start.5 = (f32[1,1,5,6,128]{4,3,2,1,0:T(8,128)S(1)}, f32[1,1,5,6,128]{4,3,2,1,0:T(8,128)S(1)}, u32[]{:S(2)}, u32[]{:S(2)}) collective-permute-start(f32[1,1,5,6,128]{4,3,2,1,0:T(8,128)S(1)} %get-tuple-element.1107), channel_id=1, source_target_pairs={{1,0},{2,1},{3,2},{4,3},{5,4},{6,5},{7,6},{8,7},{9,8},{10,9},{11,1... | collective-permute-start | bytes 46088 | tf_op jit(solution)/shard_map/ppermute | solution.py:24
  75.4 13.2 %collective-permute-start.6 = (f32[1,1,5,6,128]{4,3,2,1,0:T(8,128)S(1)}, f32[1,1,5,6,128]{4,3,2,1,0:T(8,128)S(1)}, u32[]{:S(2)}, u32[]{:S(2)}) collective-permute-start(f32[1,1,5,6,128]{4,3,2,1,0:T(8,128)S(1)} %get-tuple-element.1116), channel_id=1, source_target_pairs={{1,0},{2,1},{3,2},{4,3},{5,4},{6,5},{7,6},{8,7},{9,8},{10,9},{11,1... | collective-permute-start | bytes 46088 | tf_op jit(solution)/shard_map/ppermute | solution.py:24
  82.7 9.3 %collective-permute-start.7 = (f32[1,1,5,6,128]{4,3,2,1,0:T(8,128)S(1)}, f32[1,1,5,6,128]{4,3,2,1,0:T(8,128)S(1)}, u32[]{:S(2)}, u32[]{:S(2)}) collective-permute-start(f32[1,1,5,6,128]{4,3,2,1,0:T(8,128)S(1)} %get-tuple-element.1116), channel_id=1, source_target_pairs={{0,1},{1,2},{2,3},{3,4},{4,5},{5,6},{6,7},{7,8},{8,9},{9,10},{10,1... | collective-permute-start | bytes 46088 | tf_op jit(solution)/shard_map/ppermute | solution.py:22
  92.0 1.9 collective-permute-start.8
  120.0 4.9 %collective-permute-start.19 = (f32[1,3,5,6,128]{4,3,2,1,0:T(8,128)S(1)}, f32[1,3,5,6,128]{4,3,2,1,0:T(8,128)S(1)}, u32[]{:S(2)}, u32[]{:S(2)}) collective-permute-start(f32[1,3,5,6,128]{4,3,2,1,0:T(8,128)S(1)} %slice_bitcast_fusion.46), channel_id=1, source_target_pairs={{0,64},{64,128},{128,192},{192,256},{256,320},{320,384},{384,448},... | collective-permute-start | bytes 138248 | tf_op jit(solution)/shard_map/ppermute | solution.py:34
  125.1 80.3 %collective-permute-start.20 = (f32[1,1,5,6,128]{4,3,2,1,0:T(8,128)S(1)}, f32[1,1,5,6,128]{4,3,2,1,0:T(8,128)S(1)}, u32[]{:S(2)}, u32[]{:S(2)}) collective-permute-start(f32[1,1,5,6,128]{4,3,2,1,0:T(8,128)S(1)} %get-tuple-element.1106), channel_id=1, source_target_pairs={{0,1},{1,2},{2,3},{3,4},{4,5},{5,6},{6,7},{7,8},{8,9},{9,10},{10,1... | collective-permute-start | bytes 46088 | tf_op jit(solution)/shard_map/ppermute | solution.py:22
  127.0 78.4 %collective-permute-start.21 = (f32[1,1,5,6,128]{4,3,2,1,0:T(8,128)S(1)}, f32[1,1,5,6,128]{4,3,2,1,0:T(8,128)S(1)}, u32[]{:S(2)}, u32[]{:S(2)}) collective-permute-start(f32[1,1,5,6,128]{4,3,2,1,0:T(8,128)S(1)} %get-tuple-element.1105), channel_id=1, source_target_pairs={{1,0},{2,1},{3,2},{4,3},{5,4},{6,5},{7,6},{8,7},{9,8},{10,9},{11,1... | collective-permute-start | bytes 46088 | tf_op jit(solution)/shard_map/ppermute | solution.py:24
  135.2 3.0 %collective-permute-start.9 = (f32[10]{0:T(128)S(1)}, f32[10]{0:T(128)S(1)}, u32[]{:S(2)}, u32[]{:S(2)}) collective-permute-start(f32[10]{0:T(128)S(1)} %concatenate.296), channel_id=1, source_target_pairs={{0,64},{64,0},{128,192},{192,128},{256,320},{320,256},{384,448},{4... | collective-permute-start | bytes 128 | tf_op jit(solution)/shard_map/ppermute | solution.py:214
  138.2 5.4 %collective-permute-start.10 = (f32[10]{0:T(128)S(1)}, f32[10]{0:T(128)S(1)}, u32[]{:S(2)}, u32[]{:S(2)}) collective-permute-start(f32[10]{0:T(128)S(1)} %add.1185), channel_id=1, source_target_pairs={{0,128},{64,192},{128,0},{192,64},{256,384},{320,448},{384,256},{4... | collective-permute-start | bytes 128 | tf_op jit(solution)/shard_map/ppermute | solution.py:214
  143.6 6.3 %collective-permute-start.11 = (f32[10]{0:T(128)S(1)}, f32[10]{0:T(128)S(1)}, u32[]{:S(2)}, u32[]{:S(2)}) collective-permute-start(f32[10]{0:T(128)S(1)} %add.1186), channel_id=1, source_target_pairs={{0,256},{64,320},{128,384},{192,448},{256,0},{320,64},{384,128},{4... | collective-permute-start | bytes 128 | tf_op jit(solution)/shard_map/ppermute | solution.py:214
  149.9 9.3 %collective-permute-start.12 = (f32[10]{0:T(128)S(1)}, f32[10]{0:T(128)S(1)}, u32[]{:S(2)}, u32[]{:S(2)}) collective-permute-start(f32[10]{0:T(128)S(1)} %add.1187), channel_id=1, source_target_pairs={{0,512},{64,576},{128,640},{192,704},{256,768},{320,832},{384,896}... | collective-permute-start | bytes 128 | tf_op jit(solution)/shard_map/ppermute | solution.py:214
  159.3 8.7 %collective-permute-start.13 = (f32[10]{0:T(128)S(1)}, f32[10]{0:T(128)S(1)}, u32[]{:S(2)}, u32[]{:S(2)}) collective-permute-start(f32[10]{0:T(128)S(1)} %add.1188), channel_id=1, source_target_pairs={{0,1},{1,0},{2,3},{3,2},{4,5},{5,4},{6,7},{7,6},{8,9},{9,8},{10,11... | collective-permute-start | bytes 128 | tf_op jit(solution)/shard_map/ppermute | solution.py:214
  168.0 6.3 %collective-permute-start.14 = (f32[10]{0:T(128)S(1)}, f32[10]{0:T(128)S(1)}, u32[]{:S(2)}, u32[]{:S(2)}) collective-permute-start(f32[10]{0:T(128)S(1)} %add.1189), channel_id=1, source_target_pairs={{0,2},{1,3},{2,0},{3,1},{4,6},{5,7},{6,4},{7,5},{8,10},{9,11},{10,... | collective-permute-start | bytes 128 | tf_op jit(solution)/shard_map/ppermute | solution.py:214
  174.3 9.3 %collective-permute-start.15 = (f32[10]{0:T(128)S(1)}, f32[10]{0:T(128)S(1)}, u32[]{:S(2)}, u32[]{:S(2)}) collective-permute-start(f32[10]{0:T(128)S(1)} %add.1190), channel_id=1, source_target_pairs={{0,4},{1,5},{2,6},{3,7},{4,0},{5,1},{6,2},{7,3},{8,12},{9,13},{10,... | collective-permute-start | bytes 128 | tf_op jit(solution)/shard_map/ppermute | solution.py:214
  183.7 5.4 %collective-permute-start.16 = (f32[10]{0:T(128)S(1)}, f32[10]{0:T(128)S(1)}, u32[]{:S(2)}, u32[]{:S(2)}) collective-permute-start(f32[10]{0:T(128)S(1)} %add.1191), channel_id=1, source_target_pairs={{0,8},{1,9},{2,10},{3,11},{4,12},{5,13},{6,14},{7,15},{8,0},{9,1},... | collective-permute-start | bytes 128 | tf_op jit(solution)/shard_map/ppermute | solution.py:214
  189.1 6.3 %collective-permute-start.17 = (f32[10]{0:T(128)S(1)}, f32[10]{0:T(128)S(1)}, u32[]{:S(2)}, u32[]{:S(2)}) collective-permute-start(f32[10]{0:T(128)S(1)} %add.1192), channel_id=1, source_target_pairs={{0,16},{1,17},{2,18},{3,19},{4,20},{5,21},{6,22},{7,23},{8,24},{9,... | collective-permute-start | bytes 128 | tf_op jit(solution)/shard_map/ppermute | solution.py:214
  195.4 9.3 %collective-permute-start.18 = (f32[10]{0:T(128)S(1)}, f32[10]{0:T(128)S(1)}, u32[]{:S(2)}, u32[]{:S(2)}) collective-permute-start(f32[10]{0:T(128)S(1)} %add.1193), channel_id=1, source_target_pairs={{0,32},{1,33},{2,34},{3,35},{4,36},{5,37},{6,38},{7,39},{8,40},{9,... | collective-permute-start | bytes 128 | tf_op jit(solution)/shard_map/ppermute | solution.py:214

commit v8 on v7

--- a/solution.py
+++ b/solution.py
@@ -207,10 +207,11 @@
     return jnp.repeat(values, 3)[None, :, None]
 
 
-def butterfly_sum(values, axis):
+def butterfly_sum(values, axis, first=1, last=None):
     count = lax.axis_size(axis)
-    stride = 1
-    while stride < count:
+    bound = count if last is None else min(last, count)
+    stride = first
+    while stride < bound:
         partner = lax.ppermute(values, axis, [(i, i ^ stride) for i in range(count)])
         values = values + partner
         stride *= 2
@@ -255,8 +256,7 @@
     own_second, other_second = accumulate(geom_stack, scaled_dip, presence)
     search_field = field_dot(dip_stack, own_second, other_second)
     scaled_field = field_dot(scaled_dip, own_second, other_second)
-    image_scaled = scaled / pol_wide - (own_second + send_back(other_second)) * atom_mask[:, None, :]
-    sums = global_sums(
+    sums = butterfly_sum(
         jnp.concatenate(
             [
                 set_sums(residual, search),
@@ -265,8 +265,18 @@
                 set_sums(search, scaled / pol_wide) - search_field,
                 set_sums(scaled, scaled / pol_wide) - scaled_field,
             ]
-        )
-    )
+        ),
+        "gx",
+    )
+    sums, other_second = lax.optimization_barrier((sums, other_second))
+    received = from_behind(other_second[None, 1:4], "gx", 1)
+    sums = butterfly_sum(sums, "gy", last=4)
+    sums, received = lax.optimization_barrier((sums, received))
+    paired = jnp.stack([received[0, 0], received[0, 2] + other_second[0]], axis=0)[None]
+    column = padded_2(paired, (("gy", 1),), 1)
+    sums = butterfly_sum(sums, "gy", first=4)
+    returned = column[0, 0] + column[0, 3] + received[0, 1]
+    image_scaled = scaled / pol_wide - (own_second + returned) * atom_mask[:, None, :]
     rho_now = sums[0:2]
     curv_now = sums[2:4]
     image_pre = sums[4:6]

time: 207 us -> 206 us (level)
  the two profiles are of different devices: /device:TPU:2 before, /device:TPU:48 now
where the time goes in v8:
time: 206 us; the launch traced here: 205 us
  starting transfers between devices  78.9 us (38%)
  other arithmetic  60.8 us (30%)
  waiting for transfers between devices  53.1 us (26%)
  local copies, waits for them, and re-layouts  8.5 us (4%)
  between operations  2.16 us (1%)
    reduce_sum x22, other arithmetic, tensor_apply(): jnp.sum(scaled * deltas[member] - coef_three * moments[member], axis=axis...  52.1 us
    ppermute x10, waiting for transfers between devices, butterfly_sum(): lax.ppermute(values, axis, [(i, i ^ stride) for i in range(count)])  43.7 us
    ppermute x4, starting transfers between devices, padded_2(): lax.ppermute(head, axis, [((i + 1) % count, i) for i in range(count)])  41.6 us
    ppermute x10, starting transfers between devices, butterfly_sum(): lax.ppermute(values, axis, [(i, i ^ stride) for i in range(count)])  26.2 us
    ppermute x4, starting transfers between devices, padded_2(): lax.ppermute(tail, axis, [(i, (i + 1) % count) for i in range(count)])  7.86 us
    ppermute x4, waiting for transfers between devices, from_behind(): return lax.ppermute(value, axis, pairs)  5.13 us
  transfers between devices with their start and end apart: 22, of which 15 were waited for; matrix products, arithmetic and copies ran while one was open for 5% of the time, Pallas kernels for 0%

profile of v8, /device:TPU:48, one launch (start us, length us, event | category | flops | bytes accessed | tf_op | source)
XLA Modules:
  0.0 205.0 jit_solution(5949054455828366184)
XLA Ops:
  0.6 0.7 copy.227
  1.3 0.7 fusion.244
  2.1 0.7 copy-done.4
  2.8 19.6 %collective-permute-start = (f32[1,1,5,10,128]{4,3,2,1,0:T(8,128)S(1)}, f32[1,1,5,10,128]{4,3,2,1,0:T(8,128)S(1)}, u32[]{:S(2)}, u32[]{:S(2)}) collective-permute-start(f32[1,1,5,10,128]{4,3,2,1,0:T(8,128)S(1)} %get-tuple-element.1120), channel_id=1, source_target_pairs={{1,0},{2,1},{3,2},{4,3},{5,4},{6,5},{7,6},{8,7},{9,8},{10,9},{11,1... | collective-permute-start | bytes 76808 | tf_op jit(solution)/shard_map/ppermute | solution.py:24
  22.4 1.9 collective-permute-start.1
  24.4 0.7 copy-done.6
  25.1 0.6 copy-done.1
  27.4 0.7 fusion.203
  28.2 1.3 fusion.205
  29.7 1.4 fusion.133
  31.7 2.4 %collective-permute-done.2 = f32[1,3,5,10,128]{4,3,2,1,0:T(8,128)S(1)} collective-permute-done((f32[1,3,5,10,128]{4,3,2,1,0:T(8,128)S(1)}, f32[1,3,5,10,128]{4,3,2,1,0:T(8,128)S(1)}, u32[]{:S(2)}, u32[]{:S(2)}) %collective-permute-start.2) | collective-permute-done | bytes 76832 | tf_op jit(solution)/shard_map/ppermute | solution.py:34
  34.2 0.6 copy-done.3
  34.8 26.2 %while.44 = (s32[]{:T(128)}, f32[5,6,128]{2,0,1:T(8,128)S(1)}, f32[4,5,6,128]{3,2,1,0:T(8,128)S(1)}, f32[5,3,5]{2,1,0:T(4,128)S(1)}, f32[5,5,4,128]{3,1,2,0:T(8,...) while((s32[]{:T(128)}, f32[5,6,128]{2,0,1:T(8,128)S(1)}, ...), condition=%wide.region_40.41_spmd.clone, body=%wide.region_25.40_spmd.sunk.clone.sunk | while | flops 25193012 | bytes 1431648 | solution.py:185
  35.1 3.5 %fusion.280 = (f32[13,128]{1,0:T(8,128)S(1)}, f32[13,128]{1,0:T(8,128)S(1)}, f32[13,128]{1,0:T(8,128)S(1)}, f32[13,128]{1,0:T(8,128)S(1)}, f32[13,128]{1,0:T(8,1...) fusion(f32[13,128]{1,0:T(8,128)S(1)} %get-tuple-element.1391, ...), kind=kLoop, calls=%fused_computation.71.clone.1 | loop fusion | flops 16385408 | bytes 173056 | tf_op jit(solution)/shard_map/while/body/eval_jaxpr/reduce_sum | solution.py:46
  38.9 2.2 %fusion.282 = (f32[13,128]{1,0:T(8,128)S(1)}, f32[13,128]{1,0:T(8,128)S(1)}, f32[13,128]{1,0:T(8,128)S(1)}) fusion(f32[13,128]{1,0:T(8,128)S(1)} %get-tuple-element.1424, f32[13,128]{1,0:T(8,128)S(1)} %get-tuple-element.1392, f32[13,128]{1,0:T(8,128)S(1)} %get-tuple-element.1399, f32[13,128]{1,0:T(8,128)S(1)} %get-tuple-element.1425, ...), kind=kLoop, calls=%fused_computation.65.clone.1 | loop fusion | flops 8727680 | bytes 93184 | tf_op jit(solution)/shard_map/while/body/eval_jaxpr/reduce_sum | solution.py:46
  41.7 3.5 %fusion.280 = (f32[13,128]{1,0:T(8,128)S(1)}, f32[13,128]{1,0:T(8,128)S(1)}, f32[13,128]{1,0:T(8,128)S(1)}, f32[13,128]{1,0:T(8,128)S(1)}, f32[13,128]{1,0:T(8,1...) fusion(f32[13,128]{1,0:T(8,128)S(1)} %get-tuple-element.1391, ...), kind=kLoop, calls=%fused_computation.71.clone.1 | loop fusion | flops 16385408 | bytes 173056 | tf_op jit(solution)/shard_map/while/body/eval_jaxpr/reduce_sum | solution.py:46
  45.5 2.2 %fusion.282 = (f32[13,128]{1,0:T(8,128)S(1)}, f32[13,128]{1,0:T(8,128)S(1)}, f32[13,128]{1,0:T(8,128)S(1)}) fusion(f32[13,128]{1,0:T(8,128)S(1)} %get-tuple-element.1424, f32[13,128]{1,0:T(8,128)S(1)} %get-tuple-element.1392, f32[13,128]{1,0:T(8,128)S(1)} %get-tuple-element.1399, f32[13,128]{1,0:T(8,128)S(1)} %get-tuple-element.1425, ...), kind=kLoop, calls=%fused_computation.65.clone.1 | loop fusion | flops 8727680 | bytes 93184 | tf_op jit(solution)/shard_map/while/body/eval_jaxpr/reduce_sum | solution.py:46
  48.3 3.5 %fusion.280 = (f32[13,128]{1,0:T(8,128)S(1)}, f32[13,128]{1,0:T(8,128)S(1)}, f32[13,128]{1,0:T(8,128)S(1)}, f32[13,128]{1,0:T(8,128)S(1)}, f32[13,128]{1,0:T(8,1...) fusion(f32[13,128]{1,0:T(8,128)S(1)} %get-tuple-element.1391, ...), kind=kLoop, calls=%fused_computation.71.clone.1 | loop fusion | flops 16385408 | bytes 173056 | tf_op jit(solution)/shard_map/while/body/eval_jaxpr/reduce_sum | solution.py:46
  52.0 2.2 %fusion.282 = (f32[13,128]{1,0:T(8,128)S(1)}, f32[13,128]{1,0:T(8,128)S(1)}, f32[13,128]{1,0:T(8,128)S(1)}) fusion(f32[13,128]{1,0:T(8,128)S(1)} %get-tuple-element.1424, f32[13,128]{1,0:T(8,128)S(1)} %get-tuple-element.1392, f32[13,128]{1,0:T(8,128)S(1)} %get-tuple-element.1399, f32[13,128]{1,0:T(8,128)S(1)} %get-tuple-element.1425, ...), kind=kLoop, calls=%fused_computation.65.clone.1 | loop fusion | flops 8727680 | bytes 93184 | tf_op jit(solution)/shard_map/while/body/eval_jaxpr/reduce_sum | solution.py:46
  54.8 3.5 %fusion.280 = (f32[13,128]{1,0:T(8,128)S(1)}, f32[13,128]{1,0:T(8,128)S(1)}, f32[13,128]{1,0:T(8,128)S(1)}, f32[13,128]{1,0:T(8,128)S(1)}, f32[13,128]{1,0:T(8,1...) fusion(f32[13,128]{1,0:T(8,128)S(1)} %get-tuple-element.1391, ...), kind=kLoop, calls=%fused_computation.71.clone.1 | loop fusion | flops 16385408 | bytes 173056 | tf_op jit(solution)/shard_map/while/body/eval_jaxpr/reduce_sum | solution.py:46
  58.6 2.2 %fusion.282 = (f32[13,128]{1,0:T(8,128)S(1)}, f32[13,128]{1,0:T(8,128)S(1)}, f32[13,128]{1,0:T(8,128)S(1)}) fusion(f32[13,128]{1,0:T(8,128)S(1)} %get-tuple-element.1424, f32[13,128]{1,0:T(8,128)S(1)} %get-tuple-element.1392, f32[13,128]{1,0:T(8,128)S(1)} %get-tuple-element.1399, f32[13,128]{1,0:T(8,128)S(1)} %get-tuple-element.1425, ...), kind=kLoop, calls=%fused_computation.65.clone.1 | loop fusion | flops 8727680 | bytes 93184 | tf_op jit(solution)/shard_map/while/body/eval_jaxpr/reduce_sum | solution.py:46
  61.0 3.1 %collective-permute-start.3 = (f32[1,3,5,6,128]{4,3,2,1,0:T(8,128)S(1)}, f32[1,3,5,6,128]{4,3,2,1,0:T(8,128)S(1)}, u32[]{:S(2)}, u32[]{:S(2)}) collective-permute-start(f32[1,3,5,6,128]{4,3,2,1,0:T(8,128)S(1)} %slice_bitcast_fusion.47), channel_id=1, source_target_pairs={{0,64},{64,128},{128,192},{192,256},{256,320},{320,384},{384,448},... | collective-permute-start | bytes 138248 | tf_op jit(solution)/shard_map/ppermute | solution.py:34
  64.2 0.9 collective-permute-done.3
  65.1 1.9 collective-permute-start.4
  67.0 7.2 %collective-permute-start.5 = (f32[1,1,5,6,128]{4,3,2,1,0:T(8,128)S(1)}, f32[1,1,5,6,128]{4,3,2,1,0:T(8,128)S(1)}, u32[]{:S(2)}, u32[]{:S(2)}) collective-permute-start(f32[1,1,5,6,128]{4,3,2,1,0:T(8,128)S(1)} %get-tuple-element.1114), channel_id=1, source_target_pairs={{1,0},{2,1},{3,2},{4,3},{5,4},{6,5},{7,6},{8,7},{9,8},{10,9},{11,1... | collective-permute-start | bytes 46088 | tf_op jit(solution)/shard_map/ppermute | solution.py:24
  74.6 1.1 collective-permute-done.5
  75.8 7.5 %collective-permute-start.6 = (f32[1,1,5,6,128]{4,3,2,1,0:T(8,128)S(1)}, f32[1,1,5,6,128]{4,3,2,1,0:T(8,128)S(1)}, u32[]{:S(2)}, u32[]{:S(2)}) collective-permute-start(f32[1,1,5,6,128]{4,3,2,1,0:T(8,128)S(1)} %get-tuple-element.1123), channel_id=1, source_target_pairs={{1,0},{2,1},{3,2},{4,3},{5,4},{6,5},{7,6},{8,7},{9,8},{10,9},{11,1... | collective-permute-start | bytes 46088 | tf_op jit(solution)/shard_map/ppermute | solution.py:24
  83.4 2.1 %collective-permute-start.7 = (f32[1,1,5,6,128]{4,3,2,1,0:T(8,128)S(1)}, f32[1,1,5,6,128]{4,3,2,1,0:T(8,128)S(1)}, u32[]{:S(2)}, u32[]{:S(2)}) collective-permute-start(f32[1,1,5,6,128]{4,3,2,1,0:T(8,128)S(1)} %get-tuple-element.1123), channel_id=1, source_target_pairs={{0,1},{1,2},{2,3},{3,4},{4,5},{5,6},{6,7},{7,8},{8,9},{9,10},{10,1... | collective-permute-start | bytes 46088 | tf_op jit(solution)/shard_map/ppermute | solution.py:22
  85.5 1.3 fusion.213
  86.9 1.4 fusion.137
  88.4 0.6 fusion.217
  89.3 3.1 %collective-permute-done.7 = f32[1,1,5,6,128]{4,3,2,1,0:T(8,128)S(1)} collective-permute-done((f32[1,1,5,6,128]{4,3,2,1,0:T(8,128)S(1)}, f32[1,1,5,6,128]{4,3,2,1,0:T(8,128)S(1)}, u32[]{:S(2)}, u32[]{:S(2)}) %collective-permute-start.7) | collective-permute-done | bytes 15392 | tf_op jit(solution)/shard_map/ppermute | solution.py:22
  92.4 1.8 collective-permute-done.8
  94.3 26.0 %while.45 = (s32[]{:T(128)}, f32[5,6,128]{2,0,1:T(8,128)S(1)}, f32[4,5,6,128]{3,1,2,0:T(8,128)S(1)}, f32[5,3,5]{2,1,0:T(4,128)S(1)}, f32[5,5,4,128]{3,1,2,0:T(8,...) while((s32[]{:T(128)}, f32[5,6,128]{2,0,1:T(8,128)S(1)}, ...), condition=%wide.region_84.85_spmd.clone, body=%wide.region_69.84_spmd.sunk.clone.sunk | while | flops 25193012 | bytes 1414747 | solution.py:185
  94.6 3.5 %fusion.287 = (f32[13,128]{1,0:T(8,128)S(1)}, f32[13,128]{1,0:T(8,128)S(1)}, f32[13,128]{1,0:T(8,128)S(1)}, f32[13,128]{1,0:T(8,128)S(1)}, f32[13,128]{1,0:T(8,1...) fusion(f32[13,128]{1,0:T(8,128)S(1)} %get-tuple-element.1445, ...), kind=kLoop, calls=%fused_computation.207.clone.1 | loop fusion | flops 16385408 | bytes 173056 | tf_op jit(solution)/shard_map/while/body/eval_jaxpr/reduce_sum | solution.py:46
  98.4 2.1 %fusion.289 = (f32[13,128]{1,0:T(8,128)S(1)}, f32[13,128]{1,0:T(8,128)S(1)}, f32[13,128]{1,0:T(8,128)S(1)}) fusion(f32[13,128]{1,0:T(8,128)S(1)} %get-tuple-element.1478, f32[13,128]{1,0:T(8,128)S(1)} %get-tuple-element.1446, f32[13,128]{1,0:T(8,128)S(1)} %get-tuple-element.1453, f32[13,128]{1,0:T(8,128)S(1)} %get-tuple-element.1479, ...), kind=kLoop, calls=%fused_computation.201.clone.1 | loop fusion | flops 8727680 | bytes 93184 | tf_op jit(solution)/shard_map/while/body/eval_jaxpr/reduce_sum | solution.py:46
  101.1 3.5 %fusion.287 = (f32[13,128]{1,0:T(8,128)S(1)}, f32[13,128]{1,0:T(8,128)S(1)}, f32[13,128]{1,0:T(8,128)S(1)}, f32[13,128]{1,0:T(8,128)S(1)}, f32[13,128]{1,0:T(8,1...) fusion(f32[13,128]{1,0:T(8,128)S(1)} %get-tuple-element.1445, ...), kind=kLoop, calls=%fused_computation.207.clone.1 | loop fusion | flops 16385408 | bytes 173056 | tf_op jit(solution)/shard_map/while/body/eval_jaxpr/reduce_sum | solution.py:46
  104.9 2.1 %fusion.289 = (f32[13,128]{1,0:T(8,128)S(1)}, f32[13,128]{1,0:T(8,128)S(1)}, f32[13,128]{1,0:T(8,128)S(1)}) fusion(f32[13,128]{1,0:T(8,128)S(1)} %get-tuple-element.1478, f32[13,128]{1,0:T(8,128)S(1)} %get-tuple-element.1446, f32[13,128]{1,0:T(8,128)S(1)} %get-tuple-element.1453, f32[13,128]{1,0:T(8,128)S(1)} %get-tuple-element.1479, ...), kind=kLoop, calls=%fused_computation.201.clone.1 | loop fusion | flops 8727680 | bytes 93184 | tf_op jit(solution)/shard_map/while/body/eval_jaxpr/reduce_sum | solution.py:46
  107.6 3.5 %fusion.287 = (f32[13,128]{1,0:T(8,128)S(1)}, f32[13,128]{1,0:T(8,128)S(1)}, f32[13,128]{1,0:T(8,128)S(1)}, f32[13,128]{1,0:T(8,128)S(1)}, f32[13,128]{1,0:T(8,1...) fusion(f32[13,128]{1,0:T(8,128)S(1)} %get-tuple-element.1445, ...), kind=kLoop, calls=%fused_computation.207.clone.1 | loop fusion | flops 16385408 | bytes 173056 | tf_op jit(solution)/shard_map/while/body/eval_jaxpr/reduce_sum | solution.py:46
  111.3 2.1 %fusion.289 = (f32[13,128]{1,0:T(8,128)S(1)}, f32[13,128]{1,0:T(8,128)S(1)}, f32[13,128]{1,0:T(8,128)S(1)}) fusion(f32[13,128]{1,0:T(8,128)S(1)} %get-tuple-element.1478, f32[13,128]{1,0:T(8,128)S(1)} %get-tuple-element.1446, f32[13,128]{1,0:T(8,128)S(1)} %get-tuple-element.1453, f32[13,128]{1,0:T(8,128)S(1)} %get-tuple-element.1479, ...), kind=kLoop, calls=%fused_computation.201.clone.1 | loop fusion | flops 8727680 | bytes 93184 | tf_op jit(solution)/shard_map/while/body/eval_jaxpr/reduce_sum | solution.py:46
  114.1 3.5 %fusion.287 = (f32[13,128]{1,0:T(8,128)S(1)}, f32[13,128]{1,0:T(8,128)S(1)}, f32[13,128]{1,0:T(8,128)S(1)}, f32[13,128]{1,0:T(8,128)S(1)}, f32[13,128]{1,0:T(8,1...) fusion(f32[13,128]{1,0:T(8,128)S(1)} %get-tuple-element.1445, ...), kind=kLoop, calls=%fused_computation.207.clone.1 | loop fusion | flops 16385408 | bytes 173056 | tf_op jit(solution)/shard_map/while/body/eval_jaxpr/reduce_sum | solution.py:46
  117.8 2.1 %fusion.289 = (f32[13,128]{1,0:T(8,128)S(1)}, f32[13,128]{1,0:T(8,128)S(1)}, f32[13,128]{1,0:T(8,128)S(1)}) fusion(f32[13,128]{1,0:T(8,128)S(1)} %get-tuple-element.1478, f32[13,128]{1,0:T(8,128)S(1)} %get-tuple-element.1446, f32[13,128]{1,0:T(8,128)S(1)} %get-tuple-element.1453, f32[13,128]{1,0:T(8,128)S(1)} %get-tuple-element.1479, ...), kind=kLoop, calls=%fused_computation.201.clone.1 | loop fusion | flops 8727680 | bytes 93184 | tf_op jit(solution)/shard_map/while/body/eval_jaxpr/reduce_sum | solution.py:46
  123.8 5.9 %collective-permute-start.9 = (f32[10]{0:T(128)S(1)}, f32[10]{0:T(128)S(1)}, u32[]{:S(2)}, u32[]{:S(2)}) collective-permute-start(f32[10]{0:T(128)S(1)} %concatenate.296), channel_id=1, source_target_pairs={{0,64},{64,0},{128,192},{192,128},{256,320},{320,256},{384,448},{4... | collective-permute-start | bytes 128 | tf_op jit(solution)/shard_map/ppermute | solution.py:215
  129.7 0.8 collective-permute-done.9
  130.5 1.9 collective-permute-start.10
  132.4 3.5 %collective-permute-done.10 = f32[10]{0:T(128)S(1)} collective-permute-done((f32[10]{0:T(128)S(1)}, f32[10]{0:T(128)S(1)}, u32[]{:S(2)}, u32[]{:S(2)}) %collective-permute-start.10) | collective-permute-done | bytes 72 | tf_op jit(solution)/shard_map/ppermute | solution.py:215
  135.9 1.9 collective-permute-start.11
  137.8 4.4 %collective-permute-done.11 = f32[10]{0:T(128)S(1)} collective-permute-done((f32[10]{0:T(128)S(1)}, f32[10]{0:T(128)S(1)}, u32[]{:S(2)}, u32[]{:S(2)}) %collective-permute-start.11) | collective-permute-done | bytes 72 | tf_op jit(solution)/shard_map/ppermute | solution.py:215
  142.2 5.0 %collective-permute-start.12 = (f32[10]{0:T(128)S(1)}, f32[10]{0:T(128)S(1)}, u32[]{:S(2)}, u32[]{:S(2)}) collective-permute-start(f32[10]{0:T(128)S(1)} %add.1187), channel_id=1, source_target_pairs={{0,512},{64,576},{128,640},{192,704},{256,768},{320,832},{384,896}... | collective-permute-start | bytes 128 | tf_op jit(solution)/shard_map/ppermute | solution.py:215
  147.2 4.4 %collective-permute-done.12 = f32[10]{0:T(128)S(1)} collective-permute-done((f32[10]{0:T(128)S(1)}, f32[10]{0:T(128)S(1)}, u32[]{:S(2)}, u32[]{:S(2)}) %collective-permute-start.12) | collective-permute-done | bytes 72 | tf_op jit(solution)/shard_map/ppermute | solution.py:215
  151.6 1.9 collective-permute-start.13
  153.6 3.5 %collective-permute-done.13 = f32[10]{0:T(128)S(1)} collective-permute-done((f32[10]{0:T(128)S(1)}, f32[10]{0:T(128)S(1)}, u32[]{:S(2)}, u32[]{:S(2)}) %collective-permute-start.13) | collective-permute-done | bytes 72 | tf_op jit(solution)/shard_map/ppermute | solution.py:215
  157.1 1.9 collective-permute-start.14
  159.0 4.4 %collective-permute-done.14 = f32[10]{0:T(128)S(1)} collective-permute-done((f32[10]{0:T(128)S(1)}, f32[10]{0:T(128)S(1)}, u32[]{:S(2)}, u32[]{:S(2)}) %collective-permute-start.14) | collective-permute-done | bytes 72 | tf_op jit(solution)/shard_map/ppermute | solution.py:215
  163.4 1.9 collective-permute-start.20
  165.4 7.2 %collective-permute-start.21 = (f32[1,1,5,6,128]{4,3,2,1,0:T(8,128)S(1)}, f32[1,1,5,6,128]{4,3,2,1,0:T(8,128)S(1)}, u32[]{:S(2)}, u32[]{:S(2)}) collective-permute-start(f32[1,1,5,6,128]{4,3,2,1,0:T(8,128)S(1)} %get-tuple-element.1112), channel_id=1, source_target_pairs={{1,0},{2,1},{3,2},{4,3},{5,4},{6,5},{7,6},{8,7},{9,8},{10,9},{11,1... | collective-permute-start | bytes 46088 | tf_op jit(solution)/shard_map/ppermute | solution.py:24
  172.6 1.9 collective-permute-start.16
  174.6 7.4 %collective-permute-done.16 = f32[10]{0:T(128)S(1)} collective-permute-done((f32[10]{0:T(128)S(1)}, f32[10]{0:T(128)S(1)}, u32[]{:S(2)}, u32[]{:S(2)}) %collective-permute-start.16) | collective-permute-done | bytes 72 | tf_op jit(solution)/shard_map/ppermute | solution.py:215
  182.0 1.9 collective-permute-start.17
  183.9 3.5 %collective-permute-done.17 = f32[10]{0:T(128)S(1)} collective-permute-done((f32[10]{0:T(128)S(1)}, f32[10]{0:T(128)S(1)}, u32[]{:S(2)}, u32[]{:S(2)}) %collective-permute-start.17) | collective-permute-done | bytes 72 | tf_op jit(solution)/shard_map/ppermute | solution.py:215
  187.4 1.9 collective-permute-start.18
  189.3 4.4 %collective-permute-done.18 = f32[10]{0:T(128)S(1)} collective-permute-done((f32[10]{0:T(128)S(1)}, f32[10]{0:T(128)S(1)}, u32[]{:S(2)}, u32[]{:S(2)}) %collective-permute-start.18) | collective-permute-done | bytes 72 | tf_op jit(solution)/shard_map/ppermute | solution.py:215
  193.7 1.9 collective-permute-start.19
  195.6 7.4 %collective-permute-done.19 = f32[10]{0:T(128)S(1)} collective-permute-done((f32[10]{0:T(128)S(1)}, f32[10]{0:T(128)S(1)}, u32[]{:S(2)}, u32[]{:S(2)}) %collective-permute-start.19) | collective-permute-done | bytes 72 | tf_op jit(solution)/shard_map/ppermute | solution.py:215
  (477 shorter events, 13.2 us)
Async XLA Ops:
  0.6 1.4 copy-start.5
  0.6 1.4 copy-start
  2.1 0.7 copy-start.4
  2.8 28.8 %collective-permute-start = (f32[1,1,5,10,128]{4,3,2,1,0:T(8,128)S(1)}, f32[1,1,5,10,128]{4,3,2,1,0:T(8,128)S(1)}, u32[]{:S(2)}, u32[]{:S(2)}) collective-permute-start(f32[1,1,5,10,128]{4,3,2,1,0:T(8,128)S(1)} %get-tuple-element.1120), channel_id=1, source_target_pairs={{1,0},{2,1},{3,2},{4,3},{5,4},{6,5},{7,6},{8,7},{9,8},{10,9},{11,1... | collective-permute-start | bytes 76808 | tf_op jit(solution)/shard_map/ppermute | solution.py:24
  22.4 9.2 %collective-permute-start.1 = (f32[1,1,5,10,128]{4,3,2,1,0:T(8,128)S(1)}, f32[1,1,5,10,128]{4,3,2,1,0:T(8,128)S(1)}, u32[]{:S(2)}, u32[]{:S(2)}) collective-permute-start(f32[1,1,5,10,128]{4,3,2,1,0:T(8,128)S(1)} %get-tuple-element.1120), channel_id=1, source_target_pairs={{0,1},{1,2},{2,3},{3,4},{4,5},{5,6},{6,7},{7,8},{8,9},{9,10},{10,1... | collective-permute-start | bytes 76808 | tf_op jit(solution)/shard_map/ppermute | solution.py:22
  24.4 0.7 copy-start.6
  25.1 0.7 copy-start.1
  25.1 0.7 copy-start.2
  31.7 2.5 %collective-permute-start.2 = (f32[1,3,5,10,128]{4,3,2,1,0:T(8,128)S(1)}, f32[1,3,5,10,128]{4,3,2,1,0:T(8,128)S(1)}, u32[]{:S(2)}, u32[]{:S(2)}) collective-permute-start(f32[1,3,5,10,128]{4,3,2,1,0:T(8,128)S(1)} %pad_maximum_fusion.4), channel_id=1, source_target_pairs={{0,960},{64,0},{128,64},{192,128},{256,192},{320,256},{384,320},{4... | collective-permute-start | bytes 230408 | tf_op jit(solution)/shard_map/ppermute | solution.py:34
  34.2 0.7 copy-start.3
  61.0 4.0 %collective-permute-start.3 = (f32[1,3,5,6,128]{4,3,2,1,0:T(8,128)S(1)}, f32[1,3,5,6,128]{4,3,2,1,0:T(8,128)S(1)}, u32[]{:S(2)}, u32[]{:S(2)}) collective-permute-start(f32[1,3,5,6,128]{4,3,2,1,0:T(8,128)S(1)} %slice_bitcast_fusion.47), channel_id=1, source_target_pairs={{0,64},{64,128},{128,192},{192,256},{256,320},{320,384},{384,448},... | collective-permute-start | bytes 138248 | tf_op jit(solution)/shard_map/ppermute | solution.py:34
  65.1 9.5 %collective-permute-start.4 = (f32[1,1,5,6,128]{4,3,2,1,0:T(8,128)S(1)}, f32[1,1,5,6,128]{4,3,2,1,0:T(8,128)S(1)}, u32[]{:S(2)}, u32[]{:S(2)}) collective-permute-start(f32[1,1,5,6,128]{4,3,2,1,0:T(8,128)S(1)} %get-tuple-element.1115), channel_id=1, source_target_pairs={{0,1},{1,2},{2,3},{3,4},{4,5},{5,6},{6,7},{7,8},{8,9},{9,10},{10,1... | collective-permute-start | bytes 46088 | tf_op jit(solution)/shard_map/ppermute | solution.py:22
  67.0 8.7 %collective-permute-start.5 = (f32[1,1,5,6,128]{4,3,2,1,0:T(8,128)S(1)}, f32[1,1,5,6,128]{4,3,2,1,0:T(8,128)S(1)}, u32[]{:S(2)}, u32[]{:S(2)}) collective-permute-start(f32[1,1,5,6,128]{4,3,2,1,0:T(8,128)S(1)} %get-tuple-element.1114), channel_id=1, source_target_pairs={{1,0},{2,1},{3,2},{4,3},{5,4},{6,5},{7,6},{8,7},{9,8},{10,9},{11,1... | collective-permute-start | bytes 46088 | tf_op jit(solution)/shard_map/ppermute | solution.py:24
  75.8 13.4 %collective-permute-start.6 = (f32[1,1,5,6,128]{4,3,2,1,0:T(8,128)S(1)}, f32[1,1,5,6,128]{4,3,2,1,0:T(8,128)S(1)}, u32[]{:S(2)}, u32[]{:S(2)}) collective-permute-start(f32[1,1,5,6,128]{4,3,2,1,0:T(8,128)S(1)} %get-tuple-element.1123), channel_id=1, source_target_pairs={{1,0},{2,1},{3,2},{4,3},{5,4},{6,5},{7,6},{8,7},{9,8},{10,9},{11,1... | collective-permute-start | bytes 46088 | tf_op jit(solution)/shard_map/ppermute | solution.py:24
  83.4 9.0 %collective-permute-start.7 = (f32[1,1,5,6,128]{4,3,2,1,0:T(8,128)S(1)}, f32[1,1,5,6,128]{4,3,2,1,0:T(8,128)S(1)}, u32[]{:S(2)}, u32[]{:S(2)}) collective-permute-start(f32[1,1,5,6,128]{4,3,2,1,0:T(8,128)S(1)} %get-tuple-element.1123), channel_id=1, source_target_pairs={{0,1},{1,2},{2,3},{3,4},{4,5},{5,6},{6,7},{7,8},{8,9},{9,10},{10,1... | collective-permute-start | bytes 46088 | tf_op jit(solution)/shard_map/ppermute | solution.py:22
  92.4 1.9 collective-permute-start.8
  123.8 6.7 %collective-permute-start.9 = (f32[10]{0:T(128)S(1)}, f32[10]{0:T(128)S(1)}, u32[]{:S(2)}, u32[]{:S(2)}) collective-permute-start(f32[10]{0:T(128)S(1)} %concatenate.296), channel_id=1, source_target_pairs={{0,64},{64,0},{128,192},{192,128},{256,320},{320,256},{384,448},{4... | collective-permute-start | bytes 128 | tf_op jit(solution)/shard_map/ppermute | solution.py:215
  130.5 5.4 %collective-permute-start.10 = (f32[10]{0:T(128)S(1)}, f32[10]{0:T(128)S(1)}, u32[]{:S(2)}, u32[]{:S(2)}) collective-permute-start(f32[10]{0:T(128)S(1)} %add.1185), channel_id=1, source_target_pairs={{0,128},{64,192},{128,0},{192,64},{256,384},{320,448},{384,256},{4... | collective-permute-start | bytes 128 | tf_op jit(solution)/shard_map/ppermute | solution.py:215
  135.9 6.3 %collective-permute-start.11 = (f32[10]{0:T(128)S(1)}, f32[10]{0:T(128)S(1)}, u32[]{:S(2)}, u32[]{:S(2)}) collective-permute-start(f32[10]{0:T(128)S(1)} %add.1186), channel_id=1, source_target_pairs={{0,256},{64,320},{128,384},{192,448},{256,0},{320,64},{384,128},{4... | collective-permute-start | bytes 128 | tf_op jit(solution)/shard_map/ppermute | solution.py:215
  142.2 9.3 %collective-permute-start.12 = (f32[10]{0:T(128)S(1)}, f32[10]{0:T(128)S(1)}, u32[]{:S(2)}, u32[]{:S(2)}) collective-permute-start(f32[10]{0:T(128)S(1)} %add.1187), channel_id=1, source_target_pairs={{0,512},{64,576},{128,640},{192,704},{256,768},{320,832},{384,896}... | collective-permute-start | bytes 128 | tf_op jit(solution)/shard_map/ppermute | solution.py:215
  151.6 11.8 %collective-permute-start.15 = (f32[1,3,5,6,128]{4,3,2,1,0:T(8,128)S(1)}, f32[1,3,5,6,128]{4,3,2,1,0:T(8,128)S(1)}, u32[]{:S(2)}, u32[]{:S(2)}) collective-permute-start(f32[1,3,5,6,128]{4,3,2,1,0:T(8,128)S(1)} %slice_bitcast_fusion.46), channel_id=1, source_target_pairs={{0,64},{64,128},{128,192},{192,256},{256,320},{320,384},{384,448},... | collective-permute-start | bytes 138248 | tf_op jit(solution)/shard_map/ppermute | solution.py:34
  151.6 5.4 %collective-permute-start.13 = (f32[10]{0:T(128)S(1)}, f32[10]{0:T(128)S(1)}, u32[]{:S(2)}, u32[]{:S(2)}) collective-permute-start(f32[10]{0:T(128)S(1)} %add.1188), channel_id=1, source_target_pairs={{0,1},{1,0},{2,3},{3,2},{4,5},{5,4},{6,7},{7,6},{8,9},{9,8},{10,11... | collective-permute-start | bytes 128 | tf_op jit(solution)/shard_map/ppermute | solution.py:215
  157.1 6.3 %collective-permute-start.14 = (f32[10]{0:T(128)S(1)}, f32[10]{0:T(128)S(1)}, u32[]{:S(2)}, u32[]{:S(2)}) collective-permute-start(f32[10]{0:T(128)S(1)} %add.1189), channel_id=1, source_target_pairs={{0,2},{1,3},{2,0},{3,1},{4,6},{5,7},{6,4},{7,5},{8,10},{9,11},{10,... | collective-permute-start | bytes 128 | tf_op jit(solution)/shard_map/ppermute | solution.py:215
  163.4 40.2 %collective-permute-start.20 = (f32[1,1,5,6,128]{4,3,2,1,0:T(8,128)S(1)}, f32[1,1,5,6,128]{4,3,2,1,0:T(8,128)S(1)}, u32[]{:S(2)}, u32[]{:S(2)}) collective-permute-start(f32[1,1,5,6,128]{4,3,2,1,0:T(8,128)S(1)} %get-tuple-element.1113), channel_id=1, source_target_pairs={{0,1},{1,2},{2,3},{3,4},{4,5},{5,6},{6,7},{7,8},{8,9},{9,10},{10,1... | collective-permute-start | bytes 46088 | tf_op jit(solution)/shard_map/ppermute | solution.py:22
  165.4 38.3 %collective-permute-start.21 = (f32[1,1,5,6,128]{4,3,2,1,0:T(8,128)S(1)}, f32[1,1,5,6,128]{4,3,2,1,0:T(8,128)S(1)}, u32[]{:S(2)}, u32[]{:S(2)}) collective-permute-start(f32[1,1,5,6,128]{4,3,2,1,0:T(8,128)S(1)} %get-tuple-element.1112), channel_id=1, source_target_pairs={{1,0},{2,1},{3,2},{4,3},{5,4},{6,5},{7,6},{8,7},{9,8},{10,9},{11,1... | collective-permute-start | bytes 46088 | tf_op jit(solution)/shard_map/ppermute | solution.py:24
  172.6 9.3 %collective-permute-start.16 = (f32[10]{0:T(128)S(1)}, f32[10]{0:T(128)S(1)}, u32[]{:S(2)}, u32[]{:S(2)}) collective-permute-start(f32[10]{0:T(128)S(1)} %add.1190), channel_id=1, source_target_pairs={{0,4},{1,5},{2,6},{3,7},{4,0},{5,1},{6,2},{7,3},{8,12},{9,13},{10,... | collective-permute-start | bytes 128 | tf_op jit(solution)/shard_map/ppermute | solution.py:215
  182.0 5.4 %collective-permute-start.17 = (f32[10]{0:T(128)S(1)}, f32[10]{0:T(128)S(1)}, u32[]{:S(2)}, u32[]{:S(2)}) collective-permute-start(f32[10]{0:T(128)S(1)} %add.1191), channel_id=1, source_target_pairs={{0,8},{1,9},{2,10},{3,11},{4,12},{5,13},{6,14},{7,15},{8,0},{9,1},... | collective-permute-start | bytes 128 | tf_op jit(solution)/shard_map/ppermute | solution.py:215
  187.4 6.3 %collective-permute-start.18 = (f32[10]{0:T(128)S(1)}, f32[10]{0:T(128)S(1)}, u32[]{:S(2)}, u32[]{:S(2)}) collective-permute-start(f32[10]{0:T(128)S(1)} %add.1192), channel_id=1, source_target_pairs={{0,16},{1,17},{2,18},{3,19},{4,20},{5,21},{6,22},{7,23},{8,24},{9,... | collective-permute-start | bytes 128 | tf_op jit(solution)/shard_map/ppermute | solution.py:215
  193.7 9.3 %collective-permute-start.19 = (f32[10]{0:T(128)S(1)}, f32[10]{0:T(128)S(1)}, u32[]{:S(2)}, u32[]{:S(2)}) collective-permute-start(f32[10]{0:T(128)S(1)} %add.1193), channel_id=1, source_target_pairs={{0,32},{1,33},{2,34},{3,35},{4,36},{5,37},{6,38},{7,39},{8,40},{9,... | collective-permute-start | bytes 128 | tf_op jit(solution)/shard_map/ppermute | solution.py:215

commit v9 on v8

--- a/solution.py
+++ b/solution.py
@@ -182,7 +182,8 @@
         return own_acc, other_acc
 
     other_acc = jnp.zeros((4,) + own_total.shape, jnp.float32)
-    return lax.fori_loop(1, 5, one_slot, (own_total, other_acc))
+    carry = one_slot(1, (own_total, other_acc))
+    return lax.fori_loop(2, 5, one_slot, carry)
 
 
 def neighbours(block_data):

time: 206 us -> 194 us (0.942)
  the two profiles are of different devices: /device:TPU:48 before, /device:TPU:14 now
where the time goes in v9:
time: 194 us
  starting transfers between devices  76.1 us (39%)
  other arithmetic  59.9 us (31%)
  waiting for transfers between devices  44.7 us (23%)
  local copies, waits for them, and re-layouts  8.44 us (4%)
  between operations  2.72 us (1%)
    reduce_sum x22, other arithmetic, tensor_apply(): jnp.sum(scaled * deltas[member] - coef_three * moments[member], axis=axis...  52.2 us
    ppermute x10, starting transfers between devices, butterfly_sum(): lax.ppermute(values, axis, [(i, i ^ stride) for i in range(count)])  41.6 us
    ppermute x10, waiting for transfers between devices, butterfly_sum(): lax.ppermute(values, axis, [(i, i ^ stride) for i in range(count)])  33.5 us
    ppermute x4, starting transfers between devices, padded_2(): lax.ppermute(tail, axis, [(i, (i + 1) % count) for i in range(count)])  21.3 us
    ppermute x4, starting transfers between devices, padded_2(): lax.ppermute(head, axis, [((i + 1) % count, i) for i in range(count)])  9.76 us
    ppermute x4, waiting for transfers between devices, from_behind(): return lax.ppermute(value, axis, pairs)  8.36 us
  transfers between devices with their start and end apart: 22, of which 14 were waited for; matrix products, arithmetic and copies ran while one was open for 12% of the time, Pallas kernels for 0%

profile of v9, /device:TPU:14, one launch (start us, length us, event | category | flops | bytes accessed | tf_op | source)
XLA Modules:
  0.0 193.5 jit_solution(13219554344342968126)
XLA Ops:
  0.7 0.6 copy-done.7
  1.4 0.6 copy-done
  2.0 5.0 %collective-permute-start.1 = (f32[1,1,5,10,128]{4,3,2,1,0:T(8,128)S(1)}, f32[1,1,5,10,128]{4,3,2,1,0:T(8,128)S(1)}, u32[]{:S(2)}, u32[]{:S(2)}) collective-permute-start(f32[1,1,5,10,128]{4,3,2,1,0:T(8,128)S(1)} %get-tuple-element.1191), channel_id=1, source_target_pairs={{0,1},{1,2},{2,3},{3,4},{4,5},{5,6},{6,7},{7,8},{8,9},{9,10},{10,1... | collective-permute-start | bytes 76808 | tf_op jit(solution)/shard_map/ppermute | solution.py:22
  7.0 1.9 collective-permute-start
  9.0 0.6 copy-done.1
  9.9 0.5 copy-done.6
  12.6 1.3 fusion.286
  13.9 0.8 fusion.284
  14.8 1.4 fusion.214
  17.0 2.1 %fusion.164 = (f32[13,128]{1,0:T(8,128)S(1)}, f32[13,128]{1,0:T(8,128)S(1)}, f32[13,128]{1,0:T(8,128)S(1)}) fusion(f32[13,128]{1,0:T(8,128)S(1)} %get-tuple-element.1294, f32[13,128]{1,0:T(8,128)S(1)} %get-tuple-element.1286, f32[13,128]{1,0:T(8,128)S(1)} %bitcast.726, f32[13,128]{1,0:T(8,128)S(1)} %get-tuple-element.1295, ...), kind=kLoop, calls=%fused_computation.467 | loop fusion | flops 8727680 | bytes 93184 | tf_op jit(solution)/shard_map/reduce_sum | solution.py:46
  19.2 3.4 %fusion.170 = (f32[13,128]{1,0:T(8,128)S(1)}, f32[13,128]{1,0:T(8,128)S(1)}, f32[13,128]{1,0:T(8,128)S(1)}, f32[13,128]{1,0:T(8,128)S(1)}, f32[13,128]{1,0:T(8,1...) fusion(f32[13,128]{1,0:T(8,128)S(1)} %get-tuple-element.1275, ...), kind=kLoop, calls=%fused_computation.473 | loop fusion | flops 16385408 | bytes 173056 | tf_op jit(solution)/shard_map/reduce_sum | solution.py:46
  22.8 3.4 %collective-permute-start.2 = (f32[1,3,5,10,128]{4,3,2,1,0:T(8,128)S(1)}, f32[1,3,5,10,128]{4,3,2,1,0:T(8,128)S(1)}, u32[]{:S(2)}, u32[]{:S(2)}) collective-permute-start(f32[1,3,5,10,128]{4,3,2,1,0:T(8,128)S(1)} %pad_maximum_fusion.4), channel_id=1, source_target_pairs={{0,960},{64,0},{128,64},{192,128},{256,192},{320,256},{384,320},{4... | collective-permute-start | bytes 230408 | tf_op jit(solution)/shard_map/ppermute | solution.py:34
  26.4 0.6 copy-done.3
  27.0 1.7 collective-permute-done.2
  28.8 19.7 %while.44 = (s32[]{:T(128)}, f32[5,6,128]{2,0,1:T(8,128)S(1)}, f32[4,5,6,128]{3,1,2,0:T(8,128)S(1)}, f32[5,3,5]{2,1,0:T(4,128)S(1)}, f32[5,5,4,128]{3,1,2,0:T(8,...) while((s32[]{:T(128)}, f32[5,6,128]{2,0,1:T(8,128)S(1)}, ...), condition=%wide.region_54.55_spmd.clone, body=%wide.region_39.54_spmd.sunk.clone.sunk | while | flops 25193016 | bytes 1414809 | solution.py:186
  29.5 2.1 %fusion.372 = (f32[13,128]{1,0:T(8,128)S(1)}, f32[13,128]{1,0:T(8,128)S(1)}, f32[13,128]{1,0:T(8,128)S(1)}) fusion(f32[13,128]{1,0:T(8,128)S(1)} %get-tuple-element.1528, f32[13,128]{1,0:T(8,128)S(1)} %get-tuple-element.1496, f32[13,128]{1,0:T(8,128)S(1)} %get-tuple-element.1503, f32[13,128]{1,0:T(8,128)S(1)} %get-tuple-element.1529, ...), kind=kLoop, calls=%fused_computation.65.clone.1 | loop fusion | flops 8727680 | bytes 93184 | tf_op jit(solution)/shard_map/while/body/eval_jaxpr/reduce_sum | solution.py:46
  31.6 3.5 %fusion.370 = (f32[13,128]{1,0:T(8,128)S(1)}, f32[13,128]{1,0:T(8,128)S(1)}, f32[13,128]{1,0:T(8,128)S(1)}, f32[13,128]{1,0:T(8,128)S(1)}, f32[13,128]{1,0:T(8,1...) fusion(f32[13,128]{1,0:T(8,128)S(1)} %get-tuple-element.1495, ...), kind=kLoop, calls=%fused_computation.71.clone.1 | loop fusion | flops 16385408 | bytes 173056 | tf_op jit(solution)/shard_map/while/body/eval_jaxpr/reduce_sum | solution.py:46
  36.0 2.1 %fusion.372 = (f32[13,128]{1,0:T(8,128)S(1)}, f32[13,128]{1,0:T(8,128)S(1)}, f32[13,128]{1,0:T(8,128)S(1)}) fusion(f32[13,128]{1,0:T(8,128)S(1)} %get-tuple-element.1528, f32[13,128]{1,0:T(8,128)S(1)} %get-tuple-element.1496, f32[13,128]{1,0:T(8,128)S(1)} %get-tuple-element.1503, f32[13,128]{1,0:T(8,128)S(1)} %get-tuple-element.1529, ...), kind=kLoop, calls=%fused_computation.65.clone.1 | loop fusion | flops 8727680 | bytes 93184 | tf_op jit(solution)/shard_map/while/body/eval_jaxpr/reduce_sum | solution.py:46
  38.1 3.5 %fusion.370 = (f32[13,128]{1,0:T(8,128)S(1)}, f32[13,128]{1,0:T(8,128)S(1)}, f32[13,128]{1,0:T(8,128)S(1)}, f32[13,128]{1,0:T(8,128)S(1)}, f32[13,128]{1,0:T(8,1...) fusion(f32[13,128]{1,0:T(8,128)S(1)} %get-tuple-element.1495, ...), kind=kLoop, calls=%fused_computation.71.clone.1 | loop fusion | flops 16385408 | bytes 173056 | tf_op jit(solution)/shard_map/while/body/eval_jaxpr/reduce_sum | solution.py:46
  42.5 2.1 %fusion.372 = (f32[13,128]{1,0:T(8,128)S(1)}, f32[13,128]{1,0:T(8,128)S(1)}, f32[13,128]{1,0:T(8,128)S(1)}) fusion(f32[13,128]{1,0:T(8,128)S(1)} %get-tuple-element.1528, f32[13,128]{1,0:T(8,128)S(1)} %get-tuple-element.1496, f32[13,128]{1,0:T(8,128)S(1)} %get-tuple-element.1503, f32[13,128]{1,0:T(8,128)S(1)} %get-tuple-element.1529, ...), kind=kLoop, calls=%fused_computation.65.clone.1 | loop fusion | flops 8727680 | bytes 93184 | tf_op jit(solution)/shard_map/while/body/eval_jaxpr/reduce_sum | solution.py:46
  44.6 3.5 %fusion.370 = (f32[13,128]{1,0:T(8,128)S(1)}, f32[13,128]{1,0:T(8,128)S(1)}, f32[13,128]{1,0:T(8,128)S(1)}, f32[13,128]{1,0:T(8,128)S(1)}, f32[13,128]{1,0:T(8,1...) fusion(f32[13,128]{1,0:T(8,128)S(1)} %get-tuple-element.1495, ...), kind=kLoop, calls=%fused_computation.71.clone.1 | loop fusion | flops 16385408 | bytes 173056 | tf_op jit(solution)/shard_map/while/body/eval_jaxpr/reduce_sum | solution.py:46
  48.5 5.0 %collective-permute-done.3 = f32[1,3,5,6,128]{4,3,2,1,0:T(8,128)S(1)} collective-permute-done((f32[1,3,5,6,128]{4,3,2,1,0:T(8,128)S(1)}, f32[1,3,5,6,128]{4,3,2,1,0:T(8,128)S(1)}, u32[]{:S(2)}, u32[]{:S(2)}) %collective-permute-start.3) | collective-permute-done | bytes 46112 | tf_op jit(solution)/shard_map/ppermute | solution.py:34
  53.5 2.0 %collective-permute-start.5 = (f32[1,1,5,6,128]{4,3,2,1,0:T(8,128)S(1)}, f32[1,1,5,6,128]{4,3,2,1,0:T(8,128)S(1)}, u32[]{:S(2)}, u32[]{:S(2)}) collective-permute-start(f32[1,1,5,6,128]{4,3,2,1,0:T(8,128)S(1)} %get-tuple-element.1180), channel_id=1, source_target_pairs={{1,0},{2,1},{3,2},{4,3},{5,4},{6,5},{7,6},{8,7},{9,8},{10,9},{11,1... | collective-permute-start | bytes 46088 | tf_op jit(solution)/shard_map/ppermute | solution.py:24
  55.5 6.0 %collective-permute-start.4 = (f32[1,1,5,6,128]{4,3,2,1,0:T(8,128)S(1)}, f32[1,1,5,6,128]{4,3,2,1,0:T(8,128)S(1)}, u32[]{:S(2)}, u32[]{:S(2)}) collective-permute-start(f32[1,1,5,6,128]{4,3,2,1,0:T(8,128)S(1)} %get-tuple-element.1181), channel_id=1, source_target_pairs={{0,1},{1,2},{2,3},{3,4},{4,5},{5,6},{6,7},{7,8},{8,9},{9,10},{10,1... | collective-permute-start | bytes 46088 | tf_op jit(solution)/shard_map/ppermute | solution.py:22
  61.8 1.1 collective-permute-done.4
  63.0 6.3 %collective-permute-start.7 = (f32[1,1,5,6,128]{4,3,2,1,0:T(8,128)S(1)}, f32[1,1,5,6,128]{4,3,2,1,0:T(8,128)S(1)}, u32[]{:S(2)}, u32[]{:S(2)}) collective-permute-start(f32[1,1,5,6,128]{4,3,2,1,0:T(8,128)S(1)} %get-tuple-element.1202), channel_id=1, source_target_pairs={{0,1},{1,2},{2,3},{3,4},{4,5},{5,6},{6,7},{7,8},{8,9},{9,10},{10,1... | collective-permute-start | bytes 46088 | tf_op jit(solution)/shard_map/ppermute | solution.py:22
  69.3 1.9 collective-permute-start.6
  71.4 1.4 fusion.218
  72.8 1.6 fusion.294
  74.5 0.6 fusion.298
  75.4 1.8 collective-permute-done.6
  77.2 3.5 %fusion.178 = (f32[13,128]{1,0:T(8,128)S(1)}, f32[13,128]{1,0:T(8,128)S(1)}, f32[13,128]{1,0:T(8,128)S(1)}, f32[13,128]{1,0:T(8,128)S(1)}, f32[13,128]{1,0:T(8,1...) fusion(f32[13,128]{1,0:T(8,128)S(1)} %bitcast.735, ...), kind=kLoop, calls=%fused_computation.481 | loop fusion | flops 16385408 | bytes 173056 | tf_op jit(solution)/shard_map/reduce_sum | solution.py:46
  80.7 2.1 %fusion.172 = (f32[13,128]{1,0:T(8,128)S(1)}, f32[13,128]{1,0:T(8,128)S(1)}, f32[13,128]{1,0:T(8,128)S(1)}) fusion(f32[13,128]{1,0:T(8,128)S(1)} %bitcast.740, f32[13,128]{1,0:T(8,128)S(1)} %get-tuple-element.1286, f32[13,128]{1,0:T(8,128)S(1)} %bitcast.729, f32[13,128]{1,0:T(8,128)S(1)} %bitcast.741, f32[13,128]{1,0:T(8,128)S(1)} %bitcast.742, ...), kind=kLoop, calls=%fused_computation.475 | loop fusion | flops 8727680 | bytes 93184 | tf_op jit(solution)/shard_map/reduce_sum | solution.py:46
  83.3 1.7 collective-permute-done.8
  85.0 19.8 %while.45 = (s32[]{:T(128)}, f32[5,6,128]{2,0,1:T(8,128)S(1)}, f32[4,5,6,128]{3,1,2,0:T(8,128)S(1)}, f32[5,3,5]{2,1,0:T(4,128)S(1)}, f32[5,5,4,128]{3,1,2,0:T(8,...) while((s32[]{:T(128)}, f32[5,6,128]{2,0,1:T(8,128)S(1)}, ...), condition=%wide.region_112.113_spmd.clone, body=%wide.region_97.112_spmd.sunk.clone.sunk | while | flops 25193016 | bytes 1414809 | solution.py:186
  85.8 2.1 %fusion.379 = (f32[13,128]{1,0:T(8,128)S(1)}, f32[13,128]{1,0:T(8,128)S(1)}, f32[13,128]{1,0:T(8,128)S(1)}) fusion(f32[13,128]{1,0:T(8,128)S(1)} %get-tuple-element.1582, f32[13,128]{1,0:T(8,128)S(1)} %get-tuple-element.1550, f32[13,128]{1,0:T(8,128)S(1)} %get-tuple-element.1557, f32[13,128]{1,0:T(8,128)S(1)} %get-tuple-element.1583, ...), kind=kLoop, calls=%fused_computation.201.clone.1 | loop fusion | flops 8727680 | bytes 93184 | tf_op jit(solution)/shard_map/while/body/eval_jaxpr/reduce_sum | solution.py:46
  87.9 3.5 %fusion.377 = (f32[13,128]{1,0:T(8,128)S(1)}, f32[13,128]{1,0:T(8,128)S(1)}, f32[13,128]{1,0:T(8,128)S(1)}, f32[13,128]{1,0:T(8,128)S(1)}, f32[13,128]{1,0:T(8,1...) fusion(f32[13,128]{1,0:T(8,128)S(1)} %get-tuple-element.1549, ...), kind=kLoop, calls=%fused_computation.207.clone.1 | loop fusion | flops 16385408 | bytes 173056 | tf_op jit(solution)/shard_map/while/body/eval_jaxpr/reduce_sum | solution.py:46
  92.3 2.1 %fusion.379 = (f32[13,128]{1,0:T(8,128)S(1)}, f32[13,128]{1,0:T(8,128)S(1)}, f32[13,128]{1,0:T(8,128)S(1)}) fusion(f32[13,128]{1,0:T(8,128)S(1)} %get-tuple-element.1582, f32[13,128]{1,0:T(8,128)S(1)} %get-tuple-element.1550, f32[13,128]{1,0:T(8,128)S(1)} %get-tuple-element.1557, f32[13,128]{1,0:T(8,128)S(1)} %get-tuple-element.1583, ...), kind=kLoop, calls=%fused_computation.201.clone.1 | loop fusion | flops 8727680 | bytes 93184 | tf_op jit(solution)/shard_map/while/body/eval_jaxpr/reduce_sum | solution.py:46
  94.4 3.5 %fusion.377 = (f32[13,128]{1,0:T(8,128)S(1)}, f32[13,128]{1,0:T(8,128)S(1)}, f32[13,128]{1,0:T(8,128)S(1)}, f32[13,128]{1,0:T(8,128)S(1)}, f32[13,128]{1,0:T(8,1...) fusion(f32[13,128]{1,0:T(8,128)S(1)} %get-tuple-element.1549, ...), kind=kLoop, calls=%fused_computation.207.clone.1 | loop fusion | flops 16385408 | bytes 173056 | tf_op jit(solution)/shard_map/while/body/eval_jaxpr/reduce_sum | solution.py:46
  98.8 2.1 %fusion.379 = (f32[13,128]{1,0:T(8,128)S(1)}, f32[13,128]{1,0:T(8,128)S(1)}, f32[13,128]{1,0:T(8,128)S(1)}) fusion(f32[13,128]{1,0:T(8,128)S(1)} %get-tuple-element.1582, f32[13,128]{1,0:T(8,128)S(1)} %get-tuple-element.1550, f32[13,128]{1,0:T(8,128)S(1)} %get-tuple-element.1557, f32[13,128]{1,0:T(8,128)S(1)} %get-tuple-element.1583, ...), kind=kLoop, calls=%fused_computation.201.clone.1 | loop fusion | flops 8727680 | bytes 93184 | tf_op jit(solution)/shard_map/while/body/eval_jaxpr/reduce_sum | solution.py:46
  100.9 3.5 %fusion.377 = (f32[13,128]{1,0:T(8,128)S(1)}, f32[13,128]{1,0:T(8,128)S(1)}, f32[13,128]{1,0:T(8,128)S(1)}, f32[13,128]{1,0:T(8,128)S(1)}, f32[13,128]{1,0:T(8,1...) fusion(f32[13,128]{1,0:T(8,128)S(1)} %get-tuple-element.1549, ...), kind=kLoop, calls=%fused_computation.207.clone.1 | loop fusion | flops 16385408 | bytes 173056 | tf_op jit(solution)/shard_map/while/body/eval_jaxpr/reduce_sum | solution.py:46
  108.3 1.9 collective-permute-start.9
  110.2 1.1 collective-permute-done.9
  111.3 1.9 collective-permute-start.10
  113.2 3.5 %collective-permute-done.10 = f32[10]{0:T(128)S(1)} collective-permute-done((f32[10]{0:T(128)S(1)}, f32[10]{0:T(128)S(1)}, u32[]{:S(2)}, u32[]{:S(2)}) %collective-permute-start.10) | collective-permute-done | bytes 72 | tf_op jit(solution)/shard_map/ppermute | solution.py:216
  116.7 3.7 %collective-permute-start.11 = (f32[10]{0:T(128)S(1)}, f32[10]{0:T(128)S(1)}, u32[]{:S(2)}, u32[]{:S(2)}) collective-permute-start(f32[10]{0:T(128)S(1)} %add.1397), channel_id=1, source_target_pairs={{0,256},{64,320},{128,384},{192,448},{256,0},{320,64},{384,128},{4... | collective-permute-start | bytes 128 | tf_op jit(solution)/shard_map/ppermute | solution.py:216
  120.4 2.6 %collective-permute-done.11 = f32[10]{0:T(128)S(1)} collective-permute-done((f32[10]{0:T(128)S(1)}, f32[10]{0:T(128)S(1)}, u32[]{:S(2)}, u32[]{:S(2)}) %collective-permute-start.11) | collective-permute-done | bytes 72 | tf_op jit(solution)/shard_map/ppermute | solution.py:216
  123.0 4.8 %collective-permute-start.12 = (f32[10]{0:T(128)S(1)}, f32[10]{0:T(128)S(1)}, u32[]{:S(2)}, u32[]{:S(2)}) collective-permute-start(f32[10]{0:T(128)S(1)} %add.1398), channel_id=1, source_target_pairs={{0,512},{64,576},{128,640},{192,704},{256,768},{320,832},{384,896}... | collective-permute-start | bytes 128 | tf_op jit(solution)/shard_map/ppermute | solution.py:216
  127.8 4.6 %collective-permute-done.12 = f32[10]{0:T(128)S(1)} collective-permute-done((f32[10]{0:T(128)S(1)}, f32[10]{0:T(128)S(1)}, u32[]{:S(2)}, u32[]{:S(2)}) %collective-permute-start.12) | collective-permute-done | bytes 72 | tf_op jit(solution)/shard_map/ppermute | solution.py:216
  132.4 1.9 collective-permute-start.13
  134.4 3.5 %collective-permute-done.13 = f32[10]{0:T(128)S(1)} collective-permute-done((f32[10]{0:T(128)S(1)}, f32[10]{0:T(128)S(1)}, u32[]{:S(2)}, u32[]{:S(2)}) %collective-permute-start.13) | collective-permute-done | bytes 72 | tf_op jit(solution)/shard_map/ppermute | solution.py:216
  137.9 1.9 collective-permute-start.14
  139.8 4.4 %collective-permute-done.14 = f32[10]{0:T(128)S(1)} collective-permute-done((f32[10]{0:T(128)S(1)}, f32[10]{0:T(128)S(1)}, u32[]{:S(2)}, u32[]{:S(2)}) %collective-permute-start.14) | collective-permute-done | bytes 72 | tf_op jit(solution)/shard_map/ppermute | solution.py:216
  144.2 18.2 %collective-permute-start.16 = (f32[10]{0:T(128)S(1)}, f32[10]{0:T(128)S(1)}, u32[]{:S(2)}, u32[]{:S(2)}) collective-permute-start(f32[10]{0:T(128)S(1)} %add.1401), channel_id=1, source_target_pairs={{0,4},{1,5},{2,6},{3,7},{4,0},{5,1},{6,2},{7,3},{8,12},{9,13},{10,... | collective-permute-start | bytes 128 | tf_op jit(solution)/shard_map/ppermute | solution.py:216
  162.5 3.9 %collective-permute-start.21 = (f32[1,1,5,6,128]{4,3,2,1,0:T(8,128)S(1)}, f32[1,1,5,6,128]{4,3,2,1,0:T(8,128)S(1)}, u32[]{:S(2)}, u32[]{:S(2)}) collective-permute-start(f32[1,1,5,6,128]{4,3,2,1,0:T(8,128)S(1)} %get-tuple-element.1178), channel_id=1, source_target_pairs={{1,0},{2,1},{3,2},{4,3},{5,4},{6,5},{7,6},{8,7},{9,8},{10,9},{11,1... | collective-permute-start | bytes 46088 | tf_op jit(solution)/shard_map/ppermute | solution.py:24
  166.4 4.0 %collective-permute-start.20 = (f32[1,1,5,6,128]{4,3,2,1,0:T(8,128)S(1)}, f32[1,1,5,6,128]{4,3,2,1,0:T(8,128)S(1)}, u32[]{:S(2)}, u32[]{:S(2)}) collective-permute-start(f32[1,1,5,6,128]{4,3,2,1,0:T(8,128)S(1)} %get-tuple-element.1179), channel_id=1, source_target_pairs={{0,1},{1,2},{2,3},{3,4},{4,5},{5,6},{6,7},{7,8},{8,9},{9,10},{10,1... | collective-permute-start | bytes 46088 | tf_op jit(solution)/shard_map/ppermute | solution.py:22
  170.5 1.9 collective-permute-start.17
  172.4 3.5 %collective-permute-done.17 = f32[10]{0:T(128)S(1)} collective-permute-done((f32[10]{0:T(128)S(1)}, f32[10]{0:T(128)S(1)}, u32[]{:S(2)}, u32[]{:S(2)}) %collective-permute-start.17) | collective-permute-done | bytes 72 | tf_op jit(solution)/shard_map/ppermute | solution.py:216
  175.9 1.9 collective-permute-start.18
  177.8 4.4 %collective-permute-done.18 = f32[10]{0:T(128)S(1)} collective-permute-done((f32[10]{0:T(128)S(1)}, f32[10]{0:T(128)S(1)}, u32[]{:S(2)}, u32[]{:S(2)}) %collective-permute-start.18) | collective-permute-done | bytes 72 | tf_op jit(solution)/shard_map/ppermute | solution.py:216
  182.2 3.4 %collective-permute-start.19 = (f32[10]{0:T(128)S(1)}, f32[10]{0:T(128)S(1)}, u32[]{:S(2)}, u32[]{:S(2)}) collective-permute-start(f32[10]{0:T(128)S(1)} %add.1404), channel_id=1, source_target_pairs={{0,32},{1,33},{2,34},{3,35},{4,36},{5,37},{6,38},{7,39},{8,40},{9,... | collective-permute-start | bytes 128 | tf_op jit(solution)/shard_map/ppermute | solution.py:216
  185.6 5.9 %collective-permute-done.19 = f32[10]{0:T(128)S(1)} collective-permute-done((f32[10]{0:T(128)S(1)}, f32[10]{0:T(128)S(1)}, u32[]{:S(2)}, u32[]{:S(2)}) %collective-permute-start.19) | collective-permute-done | bytes 72 | tf_op jit(solution)/shard_map/ppermute | solution.py:216
  192.3 0.6 broadcast_in_dim.400
  192.9 0.6 broadcast_in_dim.398
  (482 shorter events, 12.1 us)
Async XLA Ops:
  0.6 0.7 copy-start.7
  0.6 0.7 copy-start.4
  0.7 0.7 copy-start.5
  1.3 0.7 copy-start
  2.0 20.8 %collective-permute-start.1 = (f32[1,1,5,10,128]{4,3,2,1,0:T(8,128)S(1)}, f32[1,1,5,10,128]{4,3,2,1,0:T(8,128)S(1)}, u32[]{:S(2)}, u32[]{:S(2)}) collective-permute-start(f32[1,1,5,10,128]{4,3,2,1,0:T(8,128)S(1)} %get-tuple-element.1191), channel_id=1, source_target_pairs={{0,1},{1,2},{2,3},{3,4},{4,5},{5,6},{6,7},{7,8},{8,9},{9,10},{10,1... | collective-permute-start | bytes 76808 | tf_op jit(solution)/shard_map/ppermute | solution.py:22
  7.0 9.7 %collective-permute-start = (f32[1,1,5,10,128]{4,3,2,1,0:T(8,128)S(1)}, f32[1,1,5,10,128]{4,3,2,1,0:T(8,128)S(1)}, u32[]{:S(2)}, u32[]{:S(2)}) collective-permute-start(f32[1,1,5,10,128]{4,3,2,1,0:T(8,128)S(1)} %get-tuple-element.1191), channel_id=1, source_target_pairs={{1,0},{2,1},{3,2},{4,3},{5,4},{6,5},{7,6},{8,7},{9,8},{10,9},{11,1... | collective-permute-start | bytes 76808 | tf_op jit(solution)/shard_map/ppermute | solution.py:24
  9.0 0.7 copy-start.1
  9.0 0.7 copy-start.2
  9.8 0.7 copy-start.6
  22.8 5.9 %collective-permute-start.2 = (f32[1,3,5,10,128]{4,3,2,1,0:T(8,128)S(1)}, f32[1,3,5,10,128]{4,3,2,1,0:T(8,128)S(1)}, u32[]{:S(2)}, u32[]{:S(2)}) collective-permute-start(f32[1,3,5,10,128]{4,3,2,1,0:T(8,128)S(1)} %pad_maximum_fusion.4), channel_id=1, source_target_pairs={{0,960},{64,0},{128,64},{192,128},{256,192},{320,256},{384,320},{4... | collective-permute-start | bytes 230408 | tf_op jit(solution)/shard_map/ppermute | solution.py:34
  26.3 0.7 copy-start.3
  48.5 5.0 %collective-permute-start.3 = (f32[1,3,5,6,128]{4,3,2,1,0:T(8,128)S(1)}, f32[1,3,5,6,128]{4,3,2,1,0:T(8,128)S(1)}, u32[]{:S(2)}, u32[]{:S(2)}) collective-permute-start(f32[1,3,5,6,128]{4,3,2,1,0:T(8,128)S(1)} %slice_bitcast_fusion.47), channel_id=1, source_target_pairs={{0,64},{64,128},{128,192},{192,256},{256,320},{320,384},{384,448},... | collective-permute-start | bytes 138248 | tf_op jit(solution)/shard_map/ppermute | solution.py:34
  53.5 8.3 %collective-permute-start.5 = (f32[1,1,5,6,128]{4,3,2,1,0:T(8,128)S(1)}, f32[1,1,5,6,128]{4,3,2,1,0:T(8,128)S(1)}, u32[]{:S(2)}, u32[]{:S(2)}) collective-permute-start(f32[1,1,5,6,128]{4,3,2,1,0:T(8,128)S(1)} %get-tuple-element.1180), channel_id=1, source_target_pairs={{1,0},{2,1},{3,2},{4,3},{5,4},{6,5},{7,6},{8,7},{9,8},{10,9},{11,1... | collective-permute-start | bytes 46088 | tf_op jit(solution)/shard_map/ppermute | solution.py:24
  55.5 7.4 %collective-permute-start.4 = (f32[1,1,5,6,128]{4,3,2,1,0:T(8,128)S(1)}, f32[1,1,5,6,128]{4,3,2,1,0:T(8,128)S(1)}, u32[]{:S(2)}, u32[]{:S(2)}) collective-permute-start(f32[1,1,5,6,128]{4,3,2,1,0:T(8,128)S(1)} %get-tuple-element.1181), channel_id=1, source_target_pairs={{0,1},{1,2},{2,3},{3,4},{4,5},{5,6},{6,7},{7,8},{8,9},{9,10},{10,1... | collective-permute-start | bytes 46088 | tf_op jit(solution)/shard_map/ppermute | solution.py:22
  63.0 20.1 %collective-permute-start.7 = (f32[1,1,5,6,128]{4,3,2,1,0:T(8,128)S(1)}, f32[1,1,5,6,128]{4,3,2,1,0:T(8,128)S(1)}, u32[]{:S(2)}, u32[]{:S(2)}) collective-permute-start(f32[1,1,5,6,128]{4,3,2,1,0:T(8,128)S(1)} %get-tuple-element.1202), channel_id=1, source_target_pairs={{0,1},{1,2},{2,3},{3,4},{4,5},{5,6},{6,7},{7,8},{8,9},{9,10},{10,1... | collective-permute-start | bytes 46088 | tf_op jit(solution)/shard_map/ppermute | solution.py:22
  69.3 7.8 %collective-permute-start.6 = (f32[1,1,5,6,128]{4,3,2,1,0:T(8,128)S(1)}, f32[1,1,5,6,128]{4,3,2,1,0:T(8,128)S(1)}, u32[]{:S(2)}, u32[]{:S(2)}) collective-permute-start(f32[1,1,5,6,128]{4,3,2,1,0:T(8,128)S(1)} %get-tuple-element.1202), channel_id=1, source_target_pairs={{1,0},{2,1},{3,2},{4,3},{5,4},{6,5},{7,6},{8,7},{9,8},{10,9},{11,1... | collective-permute-start | bytes 46088 | tf_op jit(solution)/shard_map/ppermute | solution.py:24
  83.1 1.9 collective-permute-start.8
  108.3 3.0 %collective-permute-start.9 = (f32[10]{0:T(128)S(1)}, f32[10]{0:T(128)S(1)}, u32[]{:S(2)}, u32[]{:S(2)}) collective-permute-start(f32[10]{0:T(128)S(1)} %concatenate.375), channel_id=1, source_target_pairs={{0,64},{64,0},{128,192},{192,128},{256,320},{320,256},{384,448},{4... | collective-permute-start | bytes 128 | tf_op jit(solution)/shard_map/ppermute | solution.py:216
  111.3 5.4 %collective-permute-start.10 = (f32[10]{0:T(128)S(1)}, f32[10]{0:T(128)S(1)}, u32[]{:S(2)}, u32[]{:S(2)}) collective-permute-start(f32[10]{0:T(128)S(1)} %add.1396), channel_id=1, source_target_pairs={{0,128},{64,192},{128,0},{192,64},{256,384},{320,448},{384,256},{4... | collective-permute-start | bytes 128 | tf_op jit(solution)/shard_map/ppermute | solution.py:216
  116.7 6.3 %collective-permute-start.11 = (f32[10]{0:T(128)S(1)}, f32[10]{0:T(128)S(1)}, u32[]{:S(2)}, u32[]{:S(2)}) collective-permute-start(f32[10]{0:T(128)S(1)} %add.1397), channel_id=1, source_target_pairs={{0,256},{64,320},{128,384},{192,448},{256,0},{320,64},{384,128},{4... | collective-permute-start | bytes 128 | tf_op jit(solution)/shard_map/ppermute | solution.py:216
  123.0 9.3 %collective-permute-start.12 = (f32[10]{0:T(128)S(1)}, f32[10]{0:T(128)S(1)}, u32[]{:S(2)}, u32[]{:S(2)}) collective-permute-start(f32[10]{0:T(128)S(1)} %add.1398), channel_id=1, source_target_pairs={{0,512},{64,576},{128,640},{192,704},{256,768},{320,832},{384,896}... | collective-permute-start | bytes 128 | tf_op jit(solution)/shard_map/ppermute | solution.py:216
  132.4 11.8 %collective-permute-start.15 = (f32[1,3,5,6,128]{4,3,2,1,0:T(8,128)S(1)}, f32[1,3,5,6,128]{4,3,2,1,0:T(8,128)S(1)}, u32[]{:S(2)}, u32[]{:S(2)}) collective-permute-start(f32[1,3,5,6,128]{4,3,2,1,0:T(8,128)S(1)} %slice_bitcast_fusion.46), channel_id=1, source_target_pairs={{0,64},{64,128},{128,192},{192,256},{256,320},{320,384},{384,448},... | collective-permute-start | bytes 138248 | tf_op jit(solution)/shard_map/ppermute | solution.py:34
  132.4 5.4 %collective-permute-start.13 = (f32[10]{0:T(128)S(1)}, f32[10]{0:T(128)S(1)}, u32[]{:S(2)}, u32[]{:S(2)}) collective-permute-start(f32[10]{0:T(128)S(1)} %add.1399), channel_id=1, source_target_pairs={{0,1},{1,0},{2,3},{3,2},{4,5},{5,4},{6,7},{7,6},{8,9},{9,8},{10,11... | collective-permute-start | bytes 128 | tf_op jit(solution)/shard_map/ppermute | solution.py:216
  137.9 6.3 %collective-permute-start.14 = (f32[10]{0:T(128)S(1)}, f32[10]{0:T(128)S(1)}, u32[]{:S(2)}, u32[]{:S(2)}) collective-permute-start(f32[10]{0:T(128)S(1)} %add.1400), channel_id=1, source_target_pairs={{0,2},{1,3},{2,0},{3,1},{4,6},{5,7},{6,4},{7,5},{8,10},{9,11},{10,... | collective-permute-start | bytes 128 | tf_op jit(solution)/shard_map/ppermute | solution.py:216
  144.2 26.2 %collective-permute-start.16 = (f32[10]{0:T(128)S(1)}, f32[10]{0:T(128)S(1)}, u32[]{:S(2)}, u32[]{:S(2)}) collective-permute-start(f32[10]{0:T(128)S(1)} %add.1401), channel_id=1, source_target_pairs={{0,4},{1,5},{2,6},{3,7},{4,0},{5,1},{6,2},{7,3},{8,12},{9,13},{10,... | collective-permute-start | bytes 128 | tf_op jit(solution)/shard_map/ppermute | solution.py:216
  162.5 29.7 %collective-permute-start.21 = (f32[1,1,5,6,128]{4,3,2,1,0:T(8,128)S(1)}, f32[1,1,5,6,128]{4,3,2,1,0:T(8,128)S(1)}, u32[]{:S(2)}, u32[]{:S(2)}) collective-permute-start(f32[1,1,5,6,128]{4,3,2,1,0:T(8,128)S(1)} %get-tuple-element.1178), channel_id=1, source_target_pairs={{1,0},{2,1},{3,2},{4,3},{5,4},{6,5},{7,6},{8,7},{9,8},{10,9},{11,1... | collective-permute-start | bytes 46088 | tf_op jit(solution)/shard_map/ppermute | solution.py:24
  166.4 25.8 %collective-permute-start.20 = (f32[1,1,5,6,128]{4,3,2,1,0:T(8,128)S(1)}, f32[1,1,5,6,128]{4,3,2,1,0:T(8,128)S(1)}, u32[]{:S(2)}, u32[]{:S(2)}) collective-permute-start(f32[1,1,5,6,128]{4,3,2,1,0:T(8,128)S(1)} %get-tuple-element.1179), channel_id=1, source_target_pairs={{0,1},{1,2},{2,3},{3,4},{4,5},{5,6},{6,7},{7,8},{8,9},{9,10},{10,1... | collective-permute-start | bytes 46088 | tf_op jit(solution)/shard_map/ppermute | solution.py:22
  170.5 5.4 %collective-permute-start.17 = (f32[10]{0:T(128)S(1)}, f32[10]{0:T(128)S(1)}, u32[]{:S(2)}, u32[]{:S(2)}) collective-permute-start(f32[10]{0:T(128)S(1)} %add.1402), channel_id=1, source_target_pairs={{0,8},{1,9},{2,10},{3,11},{4,12},{5,13},{6,14},{7,15},{8,0},{9,1},... | collective-permute-start | bytes 128 | tf_op jit(solution)/shard_map/ppermute | solution.py:216
  175.9 6.3 %collective-permute-start.18 = (f32[10]{0:T(128)S(1)}, f32[10]{0:T(128)S(1)}, u32[]{:S(2)}, u32[]{:S(2)}) collective-permute-start(f32[10]{0:T(128)S(1)} %add.1403), channel_id=1, source_target_pairs={{0,16},{1,17},{2,18},{3,19},{4,20},{5,21},{6,22},{7,23},{8,24},{9,... | collective-permute-start | bytes 128 | tf_op jit(solution)/shard_map/ppermute | solution.py:216
  182.2 9.3 %collective-permute-start.19 = (f32[10]{0:T(128)S(1)}, f32[10]{0:T(128)S(1)}, u32[]{:S(2)}, u32[]{:S(2)}) collective-permute-start(f32[10]{0:T(128)S(1)} %add.1404), channel_id=1, source_target_pairs={{0,32},{1,33},{2,34},{3,35},{4,36},{5,37},{6,38},{7,39},{8,40},{9,... | collective-permute-start | bytes 128 | tf_op jit(solution)/shard_map/ppermute | solution.py:216

commit v10 on v8

--- a/solution.py
+++ b/solution.py
@@ -182,7 +182,8 @@
         return own_acc, other_acc
 
     other_acc = jnp.zeros((4,) + own_total.shape, jnp.float32)
-    return lax.fori_loop(1, 5, one_slot, (own_total, other_acc))
+    carry = lax.fori_loop(2, 5, one_slot, (own_total, other_acc))
+    return one_slot(1, carry)
 
 
 def neighbours(block_data):

time: 206 us -> 201 us (0.976)
  waiting for transfers between devices: 53.1 us -> 49.6 us
  starting transfers between devices: 78.9 us -> 76.3 us
    ppermute x4, waiting for transfers between devices: 3.1 us -> 0.07 us  [padded_2(): lax.ppermute(tail, axis, [(i, (i + 1) % count) for i in range(count)])]
    ppermute x4, starting transfers between devices: 3.2 us -> 0.56 us  [from_behind(): return lax.ppermute(value, axis, pairs)]
    unnamed x66 -> x75, local copies, waits for them, and re-layouts: 3.71 us -> 6.31 us
  transfers between devices with their start and end apart: 22 -> 22, of which waited for: 15 -> 14; matrix products, arithmetic and copies ran while one was open for 5% -> 11% of each run, Pallas kernels for 0% -> 0%
where the time goes in v10:
time: 201 us; the launch traced here: 200 us
  starting transfers between devices  76.3 us (38%)
  other arithmetic  59.6 us (30%)
  waiting for transfers between devices  49.6 us (25%)
  local copies, waits for them, and re-layouts  10.5 us (5%)
  between operations  2.34 us (1%)
    reduce_sum x22, other arithmetic, tensor_apply(): jnp.sum(scaled * deltas[member] - coef_three * moments[member], axis=axis...  51.8 us
    ppermute x10, waiting for transfers between devices, butterfly_sum(): lax.ppermute(values, axis, [(i, i ^ stride) for i in range(count)])  43.7 us
    ppermute x4, starting transfers between devices, padded_2(): lax.ppermute(head, axis, [((i + 1) % count, i) for i in range(count)])  41.6 us
    ppermute x10, starting transfers between devices, butterfly_sum(): lax.ppermute(values, axis, [(i, i ^ stride) for i in range(count)])  26.4 us
    ppermute x4, starting transfers between devices, padded_2(): lax.ppermute(tail, axis, [(i, (i + 1) % count) for i in range(count)])  7.68 us
    unnamed x75, local copies, waits for them, and re-layouts  6.31 us
    ppermute x4, waiting for transfers between devices, from_behind(): return lax.ppermute(value, axis, pairs)  4.37 us
  transfers between devices with their start and end apart: 22, of which 14 were waited for; matrix products, arithmetic and copies ran while one was open for 11% of the time, Pallas kernels for 0%

profile of v10, /device:TPU:48, one launch (start us, length us, event | category | flops | bytes accessed | tf_op | source)
XLA Modules:
  0.0 199.9 jit_solution(12194969357947371009)
XLA Ops:
  0.6 0.7 copy.61
  1.3 0.7 copy-done.9
  2.0 0.6 copy-done.6
  2.8 19.6 %collective-permute-start = (f32[1,1,5,10,128]{4,2,3,1,0:T(8,128)S(1)}, f32[1,1,5,10,128]{4,2,3,1,0:T(8,128)S(1)}, u32[]{:S(2)}, u32[]{:S(2)}) collective-permute-start(f32[1,1,5,10,128]{4,2,3,1,0:T(8,128)S(1)} %get-tuple-element.1189), channel_id=1, source_target_pairs={{1,0},{2,1},{3,2},{4,3},{5,4},{6,5},{7,6},{8,7},{9,8},{10,9},{11,1... | collective-permute-start | bytes 76808 | tf_op jit(solution)/shard_map/ppermute | solution.py:24
  22.4 1.9 collective-permute-start.1
  24.4 0.7 copy-done.8
  25.1 0.6 copy-done.3
  27.9 0.8 fusion.284
  28.7 1.3 fusion.286
  30.1 1.4 fusion.214
  31.7 0.7 slice-done
  34.0 2.1 %fusion.164 = (f32[13,128]{1,0:T(8,128)S(1)}, f32[13,128]{1,0:T(8,128)S(1)}, f32[13,128]{1,0:T(8,128)S(1)}) fusion(f32[13,128]{1,0:T(8,128)S(1)} %get-tuple-element.1175, f32[13,128]{1,0:T(8,128)S(1)} %get-tuple-element.1290, f32[13,128]{1,0:T(8,128)S(1)} %get-tuple-element.1197, f32[13,128]{1,0:T(8,128)S(1)} %get-tuple-element.1176, ...), kind=kLoop, calls=%fused_computation.465 | loop fusion | flops 8727680 | bytes 93184 | tf_op jit(solution)/shard_map/reduce_sum | solution.py:46
  36.2 3.4 %fusion.170 = (f32[13,128]{1,0:T(8,128)S(1)}, f32[13,128]{1,0:T(8,128)S(1)}, f32[13,128]{1,0:T(8,128)S(1)}, f32[13,128]{1,0:T(8,128)S(1)}, f32[13,128]{1,0:T(8,1...) fusion(f32[13,128]{1,0:T(8,128)S(1)} %get-tuple-element.1180, ...), kind=kLoop, calls=%fused_computation.471 | loop fusion | flops 16385408 | bytes 173056 | tf_op jit(solution)/shard_map/reduce_sum | solution.py:46
  39.8 0.6 copy-done.5
  40.4 19.4 %while.44 = (s32[]{:T(128)}, f32[5,6,128]{2,0,1:T(8,128)S(1)}, f32[4,5,6,128]{3,1,2,0:T(8,128)S(1)}, f32[5,3,5]{2,1,0:T(4,128)S(1)}, f32[5,5,4,128]{3,1,2,0:T(8,...) while((s32[]{:T(128)}, f32[5,6,128]{2,0,1:T(8,128)S(1)}, ...), condition=%wide.region_40.41_spmd.clone, body=%wide.region_25.40_spmd.sunk.clone.sunk | while | flops 25193016 | bytes 1384097 | solution.py:185
  40.8 3.5 %fusion.367 = (f32[13,128]{1,0:T(8,128)S(1)}, f32[13,128]{1,0:T(8,128)S(1)}, f32[13,128]{1,0:T(8,128)S(1)}, f32[13,128]{1,0:T(8,128)S(1)}, f32[13,128]{1,0:T(8,1...) fusion(f32[13,128]{1,0:T(8,128)S(1)} %get-tuple-element.1475, ...), kind=kLoop, calls=%fused_computation.71.clone.1 | loop fusion | flops 16385408 | bytes 173056 | tf_op jit(solution)/shard_map/while/body/eval_jaxpr/reduce_sum | solution.py:46
  44.5 2.1 %fusion.369 = (f32[13,128]{1,0:T(8,128)S(1)}, f32[13,128]{1,0:T(8,128)S(1)}, f32[13,128]{1,0:T(8,128)S(1)}) fusion(f32[13,128]{1,0:T(8,128)S(1)} %get-tuple-element.1508, f32[13,128]{1,0:T(8,128)S(1)} %get-tuple-element.1476, f32[13,128]{1,0:T(8,128)S(1)} %get-tuple-element.1483, f32[13,128]{1,0:T(8,128)S(1)} %get-tuple-element.1509, ...), kind=kLoop, calls=%fused_computation.65.clone.1 | loop fusion | flops 8727680 | bytes 93184 | tf_op jit(solution)/shard_map/while/body/eval_jaxpr/reduce_sum | solution.py:46
  47.2 3.5 %fusion.367 = (f32[13,128]{1,0:T(8,128)S(1)}, f32[13,128]{1,0:T(8,128)S(1)}, f32[13,128]{1,0:T(8,128)S(1)}, f32[13,128]{1,0:T(8,128)S(1)}, f32[13,128]{1,0:T(8,1...) fusion(f32[13,128]{1,0:T(8,128)S(1)} %get-tuple-element.1475, ...), kind=kLoop, calls=%fused_computation.71.clone.1 | loop fusion | flops 16385408 | bytes 173056 | tf_op jit(solution)/shard_map/while/body/eval_jaxpr/reduce_sum | solution.py:46
  50.9 2.1 %fusion.369 = (f32[13,128]{1,0:T(8,128)S(1)}, f32[13,128]{1,0:T(8,128)S(1)}, f32[13,128]{1,0:T(8,128)S(1)}) fusion(f32[13,128]{1,0:T(8,128)S(1)} %get-tuple-element.1508, f32[13,128]{1,0:T(8,128)S(1)} %get-tuple-element.1476, f32[13,128]{1,0:T(8,128)S(1)} %get-tuple-element.1483, f32[13,128]{1,0:T(8,128)S(1)} %get-tuple-element.1509, ...), kind=kLoop, calls=%fused_computation.65.clone.1 | loop fusion | flops 8727680 | bytes 93184 | tf_op jit(solution)/shard_map/while/body/eval_jaxpr/reduce_sum | solution.py:46
  53.7 3.5 %fusion.367 = (f32[13,128]{1,0:T(8,128)S(1)}, f32[13,128]{1,0:T(8,128)S(1)}, f32[13,128]{1,0:T(8,128)S(1)}, f32[13,128]{1,0:T(8,128)S(1)}, f32[13,128]{1,0:T(8,1...) fusion(f32[13,128]{1,0:T(8,128)S(1)} %get-tuple-element.1475, ...), kind=kLoop, calls=%fused_computation.71.clone.1 | loop fusion | flops 16385408 | bytes 173056 | tf_op jit(solution)/shard_map/while/body/eval_jaxpr/reduce_sum | solution.py:46
  57.4 2.1 %fusion.369 = (f32[13,128]{1,0:T(8,128)S(1)}, f32[13,128]{1,0:T(8,128)S(1)}, f32[13,128]{1,0:T(8,128)S(1)}) fusion(f32[13,128]{1,0:T(8,128)S(1)} %get-tuple-element.1508, f32[13,128]{1,0:T(8,128)S(1)} %get-tuple-element.1476, f32[13,128]{1,0:T(8,128)S(1)} %get-tuple-element.1483, f32[13,128]{1,0:T(8,128)S(1)} %get-tuple-element.1509, ...), kind=kLoop, calls=%fused_computation.65.clone.1 | loop fusion | flops 8727680 | bytes 93184 | tf_op jit(solution)/shard_map/while/body/eval_jaxpr/reduce_sum | solution.py:46
  60.4 3.2 %collective-permute-done.3 = f32[1,3,5,6,128]{4,2,3,1,0:T(8,128)S(1)} collective-permute-done((f32[1,3,5,6,128]{4,2,3,1,0:T(8,128)S(1)}, f32[1,3,5,6,128]{4,2,3,1,0:T(8,128)S(1)}, u32[]{:S(2)}, u32[]{:S(2)}) %collective-permute-start.3) | collective-permute-done | bytes 46112 | tf_op jit(solution)/shard_map/ppermute | solution.py:34
  63.7 1.9 collective-permute-start.4
  65.7 7.2 %collective-permute-start.5 = (f32[1,1,5,6,128]{4,2,3,1,0:T(8,128)S(1)}, f32[1,1,5,6,128]{4,2,3,1,0:T(8,128)S(1)}, u32[]{:S(2)}, u32[]{:S(2)}) collective-permute-start(f32[1,1,5,6,128]{4,2,3,1,0:T(8,128)S(1)} %get-tuple-element.1177), channel_id=1, source_target_pairs={{1,0},{2,1},{3,2},{4,3},{5,4},{6,5},{7,6},{8,7},{9,8},{10,9},{11,1... | collective-permute-start | bytes 46088 | tf_op jit(solution)/shard_map/ppermute | solution.py:24
  73.0 1.4 collective-permute-done.5
  74.5 7.5 %collective-permute-start.6 = (f32[1,1,5,6,128]{4,2,3,1,0:T(8,128)S(1)}, f32[1,1,5,6,128]{4,2,3,1,0:T(8,128)S(1)}, u32[]{:S(2)}, u32[]{:S(2)}) collective-permute-start(f32[1,1,5,6,128]{4,2,3,1,0:T(8,128)S(1)} %get-tuple-element.1204), channel_id=1, source_target_pairs={{1,0},{2,1},{3,2},{4,3},{5,4},{6,5},{7,6},{8,7},{9,8},{10,9},{11,1... | collective-permute-start | bytes 46088 | tf_op jit(solution)/shard_map/ppermute | solution.py:24
  82.0 1.9 collective-permute-start.7
  84.0 1.6 fusion.294
  85.6 1.4 fusion.218
  87.1 0.6 fusion.298
  87.9 1.9 fusion.178
  89.9 3.5 %fusion.174 = (f32[13,128]{1,0:T(8,128)S(1)}, f32[13,128]{1,0:T(8,128)S(1)}, f32[13,128]{1,0:T(8,128)S(1)}, f32[13,128]{1,0:T(8,128)S(1)}, f32[13,128]{1,0:T(8,1...) fusion(f32[13,128]{1,0:T(8,128)S(1)} %get-tuple-element.1164, ...), kind=kLoop, calls=%fused_computation.475 | loop fusion | flops 16385408 | bytes 173056 | tf_op jit(solution)/shard_map/reduce_sum | solution.py:46
  94.4 1.2 collective-permute-done.8
  95.6 19.7 %while.45 = (s32[]{:T(128)}, f32[5,6,128]{2,0,1:T(8,128)S(1)}, f32[4,5,6,128]{3,1,2,0:T(8,128)S(1)}, f32[5,3,5]{2,1,0:T(4,128)S(1)}, f32[5,5,4,128]{3,1,2,0:T(8,...) while((s32[]{:T(128)}, f32[5,6,128]{2,0,1:T(8,128)S(1)}, ...), condition=%wide.region_98.99_spmd.clone, body=%wide.region_83.98_spmd.sunk.clone.sunk | while | flops 25193016 | bytes 1384097 | solution.py:185
  96.2 3.5 %fusion.374 = (f32[13,128]{1,0:T(8,128)S(1)}, f32[13,128]{1,0:T(8,128)S(1)}, f32[13,128]{1,0:T(8,128)S(1)}, f32[13,128]{1,0:T(8,128)S(1)}, f32[13,128]{1,0:T(8,1...) fusion(f32[13,128]{1,0:T(8,128)S(1)} %get-tuple-element.1529, ...), kind=kLoop, calls=%fused_computation.206.clone.1 | loop fusion | flops 16385408 | bytes 173056 | tf_op jit(solution)/shard_map/while/body/eval_jaxpr/reduce_sum | solution.py:46
  99.9 2.1 %fusion.376 = (f32[13,128]{1,0:T(8,128)S(1)}, f32[13,128]{1,0:T(8,128)S(1)}, f32[13,128]{1,0:T(8,128)S(1)}) fusion(f32[13,128]{1,0:T(8,128)S(1)} %get-tuple-element.1562, f32[13,128]{1,0:T(8,128)S(1)} %get-tuple-element.1530, f32[13,128]{1,0:T(8,128)S(1)} %get-tuple-element.1537, f32[13,128]{1,0:T(8,128)S(1)} %get-tuple-element.1563, ...), kind=kLoop, calls=%fused_computation.200.clone.1 | loop fusion | flops 8727680 | bytes 93184 | tf_op jit(solution)/shard_map/while/body/eval_jaxpr/reduce_sum | solution.py:46
  102.7 3.5 %fusion.374 = (f32[13,128]{1,0:T(8,128)S(1)}, f32[13,128]{1,0:T(8,128)S(1)}, f32[13,128]{1,0:T(8,128)S(1)}, f32[13,128]{1,0:T(8,128)S(1)}, f32[13,128]{1,0:T(8,1...) fusion(f32[13,128]{1,0:T(8,128)S(1)} %get-tuple-element.1529, ...), kind=kLoop, calls=%fused_computation.206.clone.1 | loop fusion | flops 16385408 | bytes 173056 | tf_op jit(solution)/shard_map/while/body/eval_jaxpr/reduce_sum | solution.py:46
  106.4 2.1 %fusion.376 = (f32[13,128]{1,0:T(8,128)S(1)}, f32[13,128]{1,0:T(8,128)S(1)}, f32[13,128]{1,0:T(8,128)S(1)}) fusion(f32[13,128]{1,0:T(8,128)S(1)} %get-tuple-element.1562, f32[13,128]{1,0:T(8,128)S(1)} %get-tuple-element.1530, f32[13,128]{1,0:T(8,128)S(1)} %get-tuple-element.1537, f32[13,128]{1,0:T(8,128)S(1)} %get-tuple-element.1563, ...), kind=kLoop, calls=%fused_computation.200.clone.1 | loop fusion | flops 8727680 | bytes 93184 | tf_op jit(solution)/shard_map/while/body/eval_jaxpr/reduce_sum | solution.py:46
  109.2 3.5 %fusion.374 = (f32[13,128]{1,0:T(8,128)S(1)}, f32[13,128]{1,0:T(8,128)S(1)}, f32[13,128]{1,0:T(8,128)S(1)}, f32[13,128]{1,0:T(8,128)S(1)}, f32[13,128]{1,0:T(8,1...) fusion(f32[13,128]{1,0:T(8,128)S(1)} %get-tuple-element.1529, ...), kind=kLoop, calls=%fused_computation.206.clone.1 | loop fusion | flops 16385408 | bytes 173056 | tf_op jit(solution)/shard_map/while/body/eval_jaxpr/reduce_sum | solution.py:46
  112.9 2.1 %fusion.376 = (f32[13,128]{1,0:T(8,128)S(1)}, f32[13,128]{1,0:T(8,128)S(1)}, f32[13,128]{1,0:T(8,128)S(1)}) fusion(f32[13,128]{1,0:T(8,128)S(1)} %get-tuple-element.1562, f32[13,128]{1,0:T(8,128)S(1)} %get-tuple-element.1530, f32[13,128]{1,0:T(8,128)S(1)} %get-tuple-element.1537, f32[13,128]{1,0:T(8,128)S(1)} %get-tuple-element.1563, ...), kind=kLoop, calls=%fused_computation.200.clone.1 | loop fusion | flops 8727680 | bytes 93184 | tf_op jit(solution)/shard_map/while/body/eval_jaxpr/reduce_sum | solution.py:46
  118.4 6.2 %collective-permute-start.9 = (f32[10]{0:T(128)S(1)}, f32[10]{0:T(128)S(1)}, u32[]{:S(2)}, u32[]{:S(2)}) collective-permute-start(f32[10]{0:T(128)S(1)} %concatenate.375), channel_id=1, source_target_pairs={{0,64},{64,0},{128,192},{192,128},{256,320},{320,256},{384,448},{4... | collective-permute-start | bytes 128 | tf_op jit(solution)/shard_map/ppermute | solution.py:216
  124.5 0.8 collective-permute-done.9
  125.3 1.9 collective-permute-start.10
  127.3 3.5 %collective-permute-done.10 = f32[10]{0:T(128)S(1)} collective-permute-done((f32[10]{0:T(128)S(1)}, f32[10]{0:T(128)S(1)}, u32[]{:S(2)}, u32[]{:S(2)}) %collective-permute-start.10) | collective-permute-done | bytes 72 | tf_op jit(solution)/shard_map/ppermute | solution.py:216
  130.8 1.9 collective-permute-start.11
  132.7 4.4 %collective-permute-done.11 = f32[10]{0:T(128)S(1)} collective-permute-done((f32[10]{0:T(128)S(1)}, f32[10]{0:T(128)S(1)}, u32[]{:S(2)}, u32[]{:S(2)}) %collective-permute-start.11) | collective-permute-done | bytes 72 | tf_op jit(solution)/shard_map/ppermute | solution.py:216
  137.1 5.0 %collective-permute-start.12 = (f32[10]{0:T(128)S(1)}, f32[10]{0:T(128)S(1)}, u32[]{:S(2)}, u32[]{:S(2)}) collective-permute-start(f32[10]{0:T(128)S(1)} %add.1398), channel_id=1, source_target_pairs={{0,512},{64,576},{128,640},{192,704},{256,768},{320,832},{384,896}... | collective-permute-start | bytes 128 | tf_op jit(solution)/shard_map/ppermute | solution.py:216
  142.1 4.4 %collective-permute-done.12 = f32[10]{0:T(128)S(1)} collective-permute-done((f32[10]{0:T(128)S(1)}, f32[10]{0:T(128)S(1)}, u32[]{:S(2)}, u32[]{:S(2)}) %collective-permute-start.12) | collective-permute-done | bytes 72 | tf_op jit(solution)/shard_map/ppermute | solution.py:216
  146.5 1.9 collective-permute-start.13
  148.4 3.5 %collective-permute-done.13 = f32[10]{0:T(128)S(1)} collective-permute-done((f32[10]{0:T(128)S(1)}, f32[10]{0:T(128)S(1)}, u32[]{:S(2)}, u32[]{:S(2)}) %collective-permute-start.13) | collective-permute-done | bytes 72 | tf_op jit(solution)/shard_map/ppermute | solution.py:216
  151.9 1.9 collective-permute-start.14
  153.8 4.4 %collective-permute-done.14 = f32[10]{0:T(128)S(1)} collective-permute-done((f32[10]{0:T(128)S(1)}, f32[10]{0:T(128)S(1)}, u32[]{:S(2)}, u32[]{:S(2)}) %collective-permute-start.14) | collective-permute-done | bytes 72 | tf_op jit(solution)/shard_map/ppermute | solution.py:216
  158.3 1.9 collective-permute-start.20
  160.2 7.2 %collective-permute-start.21 = (f32[1,1,5,6,128]{4,2,3,1,0:T(8,128)S(1)}, f32[1,1,5,6,128]{4,2,3,1,0:T(8,128)S(1)}, u32[]{:S(2)}, u32[]{:S(2)}) collective-permute-start(f32[1,1,5,6,128]{4,2,3,1,0:T(8,128)S(1)} %get-tuple-element.1153), channel_id=1, source_target_pairs={{1,0},{2,1},{3,2},{4,3},{5,4},{6,5},{7,6},{8,7},{9,8},{10,9},{11,1... | collective-permute-start | bytes 46088 | tf_op jit(solution)/shard_map/ppermute | solution.py:24
  167.5 1.9 collective-permute-start.16
  169.4 7.4 %collective-permute-done.16 = f32[10]{0:T(128)S(1)} collective-permute-done((f32[10]{0:T(128)S(1)}, f32[10]{0:T(128)S(1)}, u32[]{:S(2)}, u32[]{:S(2)}) %collective-permute-start.16) | collective-permute-done | bytes 72 | tf_op jit(solution)/shard_map/ppermute | solution.py:216
  176.8 1.9 collective-permute-start.17
  178.7 3.5 %collective-permute-done.17 = f32[10]{0:T(128)S(1)} collective-permute-done((f32[10]{0:T(128)S(1)}, f32[10]{0:T(128)S(1)}, u32[]{:S(2)}, u32[]{:S(2)}) %collective-permute-start.17) | collective-permute-done | bytes 72 | tf_op jit(solution)/shard_map/ppermute | solution.py:216
  182.2 1.9 collective-permute-start.18
  184.1 4.4 %collective-permute-done.18 = f32[10]{0:T(128)S(1)} collective-permute-done((f32[10]{0:T(128)S(1)}, f32[10]{0:T(128)S(1)}, u32[]{:S(2)}, u32[]{:S(2)}) %collective-permute-start.18) | collective-permute-done | bytes 72 | tf_op jit(solution)/shard_map/ppermute | solution.py:216
  188.6 1.9 collective-permute-start.19
  190.5 7.4 %collective-permute-done.19 = f32[10]{0:T(128)S(1)} collective-permute-done((f32[10]{0:T(128)S(1)}, f32[10]{0:T(128)S(1)}, u32[]{:S(2)}, u32[]{:S(2)}) %collective-permute-start.19) | collective-permute-done | bytes 72 | tf_op jit(solution)/shard_map/ppermute | solution.py:216
  198.6 0.6 copy.37
  199.2 0.6 copy.38
  (438 shorter events, 13.2 us)
Async XLA Ops:
  1.3 0.7 copy-start.9
  2.0 0.7 copy-start.6
  2.0 0.7 copy-start.7
  2.0 0.7 copy-start
  2.8 31.0 %collective-permute-start = (f32[1,1,5,10,128]{4,2,3,1,0:T(8,128)S(1)}, f32[1,1,5,10,128]{4,2,3,1,0:T(8,128)S(1)}, u32[]{:S(2)}, u32[]{:S(2)}) collective-permute-start(f32[1,1,5,10,128]{4,2,3,1,0:T(8,128)S(1)} %get-tuple-element.1189), channel_id=1, source_target_pairs={{1,0},{2,1},{3,2},{4,3},{5,4},{6,5},{7,6},{8,7},{9,8},{10,9},{11,1... | collective-permute-start | bytes 76808 | tf_op jit(solution)/shard_map/ppermute | solution.py:24
  22.4 11.4 %collective-permute-start.1 = (f32[1,1,5,10,128]{4,2,3,1,0:T(8,128)S(1)}, f32[1,1,5,10,128]{4,2,3,1,0:T(8,128)S(1)}, u32[]{:S(2)}, u32[]{:S(2)}) collective-permute-start(f32[1,1,5,10,128]{4,2,3,1,0:T(8,128)S(1)} %get-tuple-element.1189), channel_id=1, source_target_pairs={{0,1},{1,2},{2,3},{3,4},{4,5},{5,6},{6,7},{7,8},{8,9},{9,10},{10,1... | collective-permute-start | bytes 76808 | tf_op jit(solution)/shard_map/ppermute | solution.py:22
  24.4 0.7 copy-start.8
  25.1 0.7 copy-start.3
  25.1 0.7 copy-start.4
  26.9 0.6 copy-start.1
  31.6 0.7 slice-start
  32.7 0.7 copy-start.2
  33.9 5.9 %collective-permute-start.2 = (f32[1,3,5,10,128]{4,2,3,1,0:T(8,128)S(1)}, f32[1,3,5,10,128]{4,2,3,1,0:T(8,128)S(1)}, u32[]{:S(2)}, u32[]{:S(2)}) collective-permute-start(f32[1,3,5,10,128]{4,2,3,1,0:T(8,128)S(1)} %pad_maximum_fusion.6), channel_id=1, source_target_pairs={{0,960},{64,0},{128,64},{192,128},{256,192},{320,256},{384,320},{4... | collective-permute-start | bytes 230408 | tf_op jit(solution)/shard_map/ppermute | solution.py:34
  39.8 0.7 copy-start.5
  59.8 3.8 %collective-permute-start.3 = (f32[1,3,5,6,128]{4,2,3,1,0:T(8,128)S(1)}, f32[1,3,5,6,128]{4,2,3,1,0:T(8,128)S(1)}, u32[]{:S(2)}, u32[]{:S(2)}) collective-permute-start(f32[1,3,5,6,128]{4,2,3,1,0:T(8,128)S(1)} %slice_bitcast_fusion.43), channel_id=1, source_target_pairs={{0,64},{64,128},{128,192},{192,256},{256,320},{320,384},{384,448},... | collective-permute-start | bytes 138248 | tf_op jit(solution)/shard_map/ppermute | solution.py:34
  63.7 9.3 %collective-permute-start.4 = (f32[1,1,5,6,128]{4,2,3,1,0:T(8,128)S(1)}, f32[1,1,5,6,128]{4,2,3,1,0:T(8,128)S(1)}, u32[]{:S(2)}, u32[]{:S(2)}) collective-permute-start(f32[1,1,5,6,128]{4,2,3,1,0:T(8,128)S(1)} %get-tuple-element.1178), channel_id=1, source_target_pairs={{0,1},{1,2},{2,3},{3,4},{4,5},{5,6},{6,7},{7,8},{8,9},{9,10},{10,1... | collective-permute-start | bytes 46088 | tf_op jit(solution)/shard_map/ppermute | solution.py:22
  65.7 8.7 %collective-permute-start.5 = (f32[1,1,5,6,128]{4,2,3,1,0:T(8,128)S(1)}, f32[1,1,5,6,128]{4,2,3,1,0:T(8,128)S(1)}, u32[]{:S(2)}, u32[]{:S(2)}) collective-permute-start(f32[1,1,5,6,128]{4,2,3,1,0:T(8,128)S(1)} %get-tuple-element.1177), channel_id=1, source_target_pairs={{1,0},{2,1},{3,2},{4,3},{5,4},{6,5},{7,6},{8,7},{9,8},{10,9},{11,1... | collective-permute-start | bytes 46088 | tf_op jit(solution)/shard_map/ppermute | solution.py:24
  74.5 15.4 %collective-permute-start.6 = (f32[1,1,5,6,128]{4,2,3,1,0:T(8,128)S(1)}, f32[1,1,5,6,128]{4,2,3,1,0:T(8,128)S(1)}, u32[]{:S(2)}, u32[]{:S(2)}) collective-permute-start(f32[1,1,5,6,128]{4,2,3,1,0:T(8,128)S(1)} %get-tuple-element.1204), channel_id=1, source_target_pairs={{1,0},{2,1},{3,2},{4,3},{5,4},{6,5},{7,6},{8,7},{9,8},{10,9},{11,1... | collective-permute-start | bytes 46088 | tf_op jit(solution)/shard_map/ppermute | solution.py:24
  82.0 11.5 %collective-permute-start.7 = (f32[1,1,5,6,128]{4,2,3,1,0:T(8,128)S(1)}, f32[1,1,5,6,128]{4,2,3,1,0:T(8,128)S(1)}, u32[]{:S(2)}, u32[]{:S(2)}) collective-permute-start(f32[1,1,5,6,128]{4,2,3,1,0:T(8,128)S(1)} %get-tuple-element.1204), channel_id=1, source_target_pairs={{0,1},{1,2},{2,3},{3,4},{4,5},{5,6},{6,7},{7,8},{8,9},{9,10},{10,1... | collective-permute-start | bytes 46088 | tf_op jit(solution)/shard_map/ppermute | solution.py:22
  93.5 2.0 %collective-permute-start.8 = (f32[1,3,5,6,128]{4,2,3,1,0:T(8,128)S(1)}, f32[1,3,5,6,128]{4,2,3,1,0:T(8,128)S(1)}, u32[]{:S(2)}, u32[]{:S(2)}) collective-permute-start(f32[1,3,5,6,128]{4,2,3,1,0:T(8,128)S(1)} %pad_maximum_fusion.9), channel_id=1, source_target_pairs={{0,960},{64,0},{128,64},{192,128},{256,192},{320,256},{384,320},{4... | collective-permute-start | bytes 138248 | tf_op jit(solution)/shard_map/ppermute | solution.py:34
  118.4 7.0 %collective-permute-start.9 = (f32[10]{0:T(128)S(1)}, f32[10]{0:T(128)S(1)}, u32[]{:S(2)}, u32[]{:S(2)}) collective-permute-start(f32[10]{0:T(128)S(1)} %concatenate.375), channel_id=1, source_target_pairs={{0,64},{64,0},{128,192},{192,128},{256,320},{320,256},{384,448},{4... | collective-permute-start | bytes 128 | tf_op jit(solution)/shard_map/ppermute | solution.py:216
  125.3 5.4 %collective-permute-start.10 = (f32[10]{0:T(128)S(1)}, f32[10]{0:T(128)S(1)}, u32[]{:S(2)}, u32[]{:S(2)}) collective-permute-start(f32[10]{0:T(128)S(1)} %add.1396), channel_id=1, source_target_pairs={{0,128},{64,192},{128,0},{192,64},{256,384},{320,448},{384,256},{4... | collective-permute-start | bytes 128 | tf_op jit(solution)/shard_map/ppermute | solution.py:216
  130.8 6.3 %collective-permute-start.11 = (f32[10]{0:T(128)S(1)}, f32[10]{0:T(128)S(1)}, u32[]{:S(2)}, u32[]{:S(2)}) collective-permute-start(f32[10]{0:T(128)S(1)} %add.1397), channel_id=1, source_target_pairs={{0,256},{64,320},{128,384},{192,448},{256,0},{320,64},{384,128},{4... | collective-permute-start | bytes 128 | tf_op jit(solution)/shard_map/ppermute | solution.py:216
  137.1 9.3 %collective-permute-start.12 = (f32[10]{0:T(128)S(1)}, f32[10]{0:T(128)S(1)}, u32[]{:S(2)}, u32[]{:S(2)}) collective-permute-start(f32[10]{0:T(128)S(1)} %add.1398), channel_id=1, source_target_pairs={{0,512},{64,576},{128,640},{192,704},{256,768},{320,832},{384,896}... | collective-permute-start | bytes 128 | tf_op jit(solution)/shard_map/ppermute | solution.py:216
  146.4 11.8 %collective-permute-start.15 = (f32[1,3,5,6,128]{4,2,3,1,0:T(8,128)S(1)}, f32[1,3,5,6,128]{4,2,3,1,0:T(8,128)S(1)}, u32[]{:S(2)}, u32[]{:S(2)}) collective-permute-start(f32[1,3,5,6,128]{4,2,3,1,0:T(8,128)S(1)} %slice_bitcast_fusion.42), channel_id=1, source_target_pairs={{0,64},{64,128},{128,192},{192,256},{256,320},{320,384},{384,448},... | collective-permute-start | bytes 138248 | tf_op jit(solution)/shard_map/ppermute | solution.py:34
  146.5 5.4 %collective-permute-start.13 = (f32[10]{0:T(128)S(1)}, f32[10]{0:T(128)S(1)}, u32[]{:S(2)}, u32[]{:S(2)}) collective-permute-start(f32[10]{0:T(128)S(1)} %add.1399), channel_id=1, source_target_pairs={{0,1},{1,0},{2,3},{3,2},{4,5},{5,4},{6,7},{7,6},{8,9},{9,8},{10,11... | collective-permute-start | bytes 128 | tf_op jit(solution)/shard_map/ppermute | solution.py:216
  151.9 6.3 %collective-permute-start.14 = (f32[10]{0:T(128)S(1)}, f32[10]{0:T(128)S(1)}, u32[]{:S(2)}, u32[]{:S(2)}) collective-permute-start(f32[10]{0:T(128)S(1)} %add.1400), channel_id=1, source_target_pairs={{0,2},{1,3},{2,0},{3,1},{4,6},{5,7},{6,4},{7,5},{8,10},{9,11},{10,... | collective-permute-start | bytes 128 | tf_op jit(solution)/shard_map/ppermute | solution.py:216
  158.3 40.2 %collective-permute-start.20 = (f32[1,1,5,6,128]{4,2,3,1,0:T(8,128)S(1)}, f32[1,1,5,6,128]{4,2,3,1,0:T(8,128)S(1)}, u32[]{:S(2)}, u32[]{:S(2)}) collective-permute-start(f32[1,1,5,6,128]{4,2,3,1,0:T(8,128)S(1)} %get-tuple-element.1154), channel_id=1, source_target_pairs={{0,1},{1,2},{2,3},{3,4},{4,5},{5,6},{6,7},{7,8},{8,9},{9,10},{10,1... | collective-permute-start | bytes 46088 | tf_op jit(solution)/shard_map/ppermute | solution.py:22
  160.2 38.3 %collective-permute-start.21 = (f32[1,1,5,6,128]{4,2,3,1,0:T(8,128)S(1)}, f32[1,1,5,6,128]{4,2,3,1,0:T(8,128)S(1)}, u32[]{:S(2)}, u32[]{:S(2)}) collective-permute-start(f32[1,1,5,6,128]{4,2,3,1,0:T(8,128)S(1)} %get-tuple-element.1153), channel_id=1, source_target_pairs={{1,0},{2,1},{3,2},{4,3},{5,4},{6,5},{7,6},{8,7},{9,8},{10,9},{11,1... | collective-permute-start | bytes 46088 | tf_op jit(solution)/shard_map/ppermute | solution.py:24
  167.5 9.3 %collective-permute-start.16 = (f32[10]{0:T(128)S(1)}, f32[10]{0:T(128)S(1)}, u32[]{:S(2)}, u32[]{:S(2)}) collective-permute-start(f32[10]{0:T(128)S(1)} %add.1401), channel_id=1, source_target_pairs={{0,4},{1,5},{2,6},{3,7},{4,0},{5,1},{6,2},{7,3},{8,12},{9,13},{10,... | collective-permute-start | bytes 128 | tf_op jit(solution)/shard_map/ppermute | solution.py:216
  176.8 5.4 %collective-permute-start.17 = (f32[10]{0:T(128)S(1)}, f32[10]{0:T(128)S(1)}, u32[]{:S(2)}, u32[]{:S(2)}) collective-permute-start(f32[10]{0:T(128)S(1)} %add.1402), channel_id=1, source_target_pairs={{0,8},{1,9},{2,10},{3,11},{4,12},{5,13},{6,14},{7,15},{8,0},{9,1},... | collective-permute-start | bytes 128 | tf_op jit(solution)/shard_map/ppermute | solution.py:216
  182.2 6.3 %collective-permute-start.18 = (f32[10]{0:T(128)S(1)}, f32[10]{0:T(128)S(1)}, u32[]{:S(2)}, u32[]{:S(2)}) collective-permute-start(f32[10]{0:T(128)S(1)} %add.1403), channel_id=1, source_target_pairs={{0,16},{1,17},{2,18},{3,19},{4,20},{5,21},{6,22},{7,23},{8,24},{9,... | collective-permute-start | bytes 128 | tf_op jit(solution)/shard_map/ppermute | solution.py:216
  188.6 9.3 %collective-permute-start.19 = (f32[10]{0:T(128)S(1)}, f32[10]{0:T(128)S(1)}, u32[]{:S(2)}, u32[]{:S(2)}) collective-permute-start(f32[10]{0:T(128)S(1)} %add.1404), channel_id=1, source_target_pairs={{0,32},{1,33},{2,34},{3,35},{4,36},{5,37},{6,38},{7,39},{8,40},{9,... | collective-permute-start | bytes 128 | tf_op jit(solution)/shard_map/ppermute | solution.py:216
